TPU v7x, 32 devices: a whole 2x2x4 slice. The times are simulated.
32 devices in a mesh: dp: 4 (over x, core), expert: 8 (over z, y).
Axes of the slice: x: 2, y: 2, z: 4, core: 2. Of those that a mesh axis runs over, the one named last changes fastest.
Arguments:
- inputs: bfloat16 [512, 4096], P(('dp', 'expert')), may hold values from -6 to 6
- grad_out: bfloat16 [512, 4096], P(('dp', 'expert')), may hold values from -0.796875 to 0.796875
- labels: int32 [512, 1], P(('dp', 'expert')), may hold values from 0 to 7; in each aligned block of 16 rows (0 to 15, 16 to 31, ...) at most 3 rows name the same one
- w_gate: bfloat16 [4096, 57344], P('dp', 'expert'), may hold values from -0.09375 to 0.09375
- w_up: bfloat16 [4096, 57344], P('dp', 'expert'), may hold values from -0.09375 to 0.09375
- w_down: bfloat16 [57344, 4096], P('expert', 'dp'), may hold values from -0.0625 to 0.0625
Outputs:
- grad_in: bfloat16 [512, 4096], P(('dp', 'expert'))
- grad_gate: bfloat16 [4096, 57344], P('dp', 'expert')
- grad_up: bfloat16 [4096, 57344], P('dp', 'expert')
- grad_down: bfloat16 [57344, 4096], P('expert', 'dp')
Inputs may be any that keep to these rules, and one draw needn't show every extreme that they name: `labels`: among the 16 rows of one device no expert is named by more than 3 rows, a bound that some block reaches.
All inputs are finite; a program needn't handle non-finite values.
Results may differ from a plain program's by a relative error of at most 0.011.
Values may be sent and summed in bfloat16 or wider, within the bound.
No kernel may reach another device: no remote copies, remote signals or barrier semaphores. Data moves between devices by JAX's collectives and lax.ppermute only.
A program may use at most 192 MiB of HBM per device.

v0:
```python
import jax
import jax.numpy as jnp
from jax import lax
from jax.sharding import PartitionSpec as P

EXPERTS = 8


def nonlinear(gate, up, dhid):
    sig = jax.nn.sigmoid(gate)
    act = gate * sig
    hidden = (act * up).astype(jnp.bfloat16)
    d_up = (dhid * act).astype(jnp.bfloat16)
    d_gate = (dhid * up * sig * (1.0 + gate * (1.0 - sig))).astype(jnp.bfloat16)
    return (hidden, d_up, d_gate)


def contract_rows(left, right):
    return lax.dot_general(
        left, right, (((0,), (0,)), ((), ())), preferred_element_type=jnp.float32
    )


def on_device(inputs, grad_out, labels, w_gate, w_up, w_down):
    members = lax.axis_size("expert")
    replicas = lax.axis_size("dp")
    group = members // EXPERTS
    tok_count = inputs.shape[0]
    width = inputs.shape[1]
    capacity = 3 * tok_count // (2 * EXPERTS)
    label_col = labels[:, 0]
    onehot = (label_col[:, None] == jnp.arange(EXPERTS, dtype=jnp.int32)[None, :]).astype(jnp.int32)
    before = jnp.cumsum(onehot, axis=0) - onehot
    rank_in = jnp.sum(before * onehot, axis=1)
    slot_ids = label_col * capacity + rank_in

    def spread(values):
        buffer = jnp.zeros((EXPERTS * capacity, width), jnp.bfloat16).at[slot_ids].set(values)
        return jnp.repeat(buffer.reshape(EXPERTS, 1, capacity, width), group, axis=0)

    recv_in, recv_grad = (
        lax.all_to_all(
            lax.all_to_all(spread(inputs), "dp", split_axis=3, concat_axis=1, tiled=True),
            "expert",
            split_axis=0,
            concat_axis=0,
            tiled=True,
        ),
        lax.all_to_all(
            lax.all_to_all(spread(grad_out), "dp", split_axis=3, concat_axis=1, tiled=True),
            "expert",
            split_axis=0,
            concat_axis=0,
            tiled=True,
        ),
    )
    columns = width // replicas
    rows_in = recv_in.reshape(-1, columns)
    rows_grad = recv_grad.reshape(-1, columns)
    gate_part = jnp.dot(rows_in, w_gate, preferred_element_type=jnp.float32)
    up_part = jnp.dot(rows_in, w_up, preferred_element_type=jnp.float32)
    dhid_part = lax.dot_general(
        rows_grad, w_down, (((1,), (1,)), ((), ())), preferred_element_type=jnp.float32
    )
    gate, up, dhid = lax.psum((gate_part, up_part, dhid_part), "dp")
    hidden, d_up, d_gate = nonlinear(gate, up, dhid)
    d_rows = lax.dot_general(
        d_gate, w_gate, (((1,), (1,)), ((), ())), preferred_element_type=jnp.float32
    )
    d_rows = d_rows + lax.dot_general(
        d_up, w_up, (((1,), (1,)), ((), ())), preferred_element_type=jnp.float32
    )
    back_rows = lax.all_to_all(
        lax.all_to_all(
            d_rows.reshape(members, replicas, capacity, columns).astype(jnp.bfloat16),
            "dp",
            split_axis=1,
            concat_axis=3,
            tiled=True,
        ),
        "expert",
        split_axis=0,
        concat_axis=0,
        tiled=True,
    ).astype(jnp.float32)
    summed = jnp.sum(back_rows.reshape(EXPERTS, group, capacity, width), axis=1)
    grad_in = summed.reshape(EXPERTS * capacity, width)[slot_ids].astype(jnp.bfloat16)
    grad_gate = contract_rows(rows_in, d_gate).astype(jnp.bfloat16)
    grad_up = contract_rows(rows_in, d_up).astype(jnp.bfloat16)
    grad_down = contract_rows(hidden, rows_grad).astype(jnp.bfloat16)
    return (grad_in, grad_gate, grad_up, grad_down)


def solution(mesh):
    return jax.shard_map(
        on_device,
        mesh=mesh,
        in_specs=(
            P(("dp", "expert"), None),
            P(("dp", "expert"), None),
            P(("dp", "expert"), None),
            P("dp", "expert"),
            P("dp", "expert"),
            P("expert", "dp"),
        ),
        out_specs=(
            P(("dp", "expert"), None),
            P("dp", "expert"),
            P("dp", "expert"),
            P("expert", "dp"),
        ),
        check_vma=False,
    )
```

profile of v0, /device:TPU:0, one launch (start us, length us, event | category | flops | bytes accessed | tf_op | source)
XLA Modules:
  0.0 330.5 jit_solution(10850027350697886702)
XLA Ops:
  7.2 0.7 fusion.7
  7.9 0.8 select_reduce_fusion
  8.8 0.7 fusion.8
  9.4 1.2 scatter_custom_fusion.1
  10.7 0.1 reshape_broadcast_in_dim_reshape.7
  10.8 4.6 %copy.38 = bf16[8,1,3,4096]{0,2,1,3:T(4,128)(2,1)} copy(bf16[8,1,3,4096]{3,2,0,1:T(4,128)(2,1)S(1)} %reshape_broadcast_in_dim_reshape.7) | data formatting | bytes 393216 | tf_op jit(solution)/shard_map/reshape;broadcast_in_dim;reshape | solution.py:39
  15.4 5.8 %reshape.60 = bf16[4,2,12288]{2,1,0:T(2,128)(2,1)} reshape(bf16[4096,1,3,8]{3,2,1,0:T(4,128)(2,1)} %bitcast.43) | data formatting | bytes 393216
  21.2 4.2 %all-to-all-start.2 = ((bf16[4,2,12288]{2,1,0:T(2,128)(2,1)}), bf16[4,2,12288]{2,1,0:T(2,128)(2,1)S(1)}, u32[]{:S(2)}, u32[]{:S(2)}) async-start(bf16[4,2,12288]{2,1,0:T(2,128)(2,1)} %reshape.60), calls=%async_computation.2 | async-start | bytes 393216 | tf_op jit(solution)/shard_map/all_to_all | solution.py:43
  25.4 1.2 scatter_custom_fusion
  26.6 0.1 reshape_broadcast_in_dim_reshape.6
  26.8 4.6 %copy.34 = bf16[8,1,3,4096]{0,2,1,3:T(4,128)(2,1)} copy(bf16[8,1,3,4096]{3,2,0,1:T(4,128)(2,1)S(1)} %reshape_broadcast_in_dim_reshape.6) | data formatting | bytes 393216 | tf_op jit(solution)/shard_map/reshape;broadcast_in_dim;reshape | solution.py:39
  31.4 5.8 %reshape.62 = bf16[4,2,12288]{2,1,0:T(2,128)(2,1)} reshape(bf16[4096,1,3,8]{3,2,1,0:T(4,128)(2,1)} %bitcast.44) | data formatting | bytes 393216
  37.2 0.0 all-to-all-done.2
  37.2 3.4 %all-to-all-start = ((bf16[4,2,12288]{2,1,0:T(2,128)(2,1)}), bf16[4,2,12288]{2,1,0:T(2,128)(2,1)S(1)}, u32[]{:S(2)}, u32[]{:S(2)}) async-start(bf16[4,2,12288]{2,1,0:T(2,128)(2,1)} %reshape.62), calls=%async_computation | async-start | bytes 393216 | tf_op jit(solution)/shard_map/all_to_all | solution.py:50
  40.6 4.8 %reshape.61 = bf16[4096,1,3,8]{3,2,1,0:T(4,128)(2,1)} reshape(bf16[4,2,12288]{2,1,0:T(2,128)(2,1)S(1)} %all-to-all-done.2) | data formatting | bytes 393216
  45.4 6.6 %copy.40 = bf16[8,4,3,1024]{3,1,2,0:T(4,128)(2,1)} copy(bf16[8,4,3,1024]{0,2,3,1:T(4,128)(2,1)} %bitcast.45) | data formatting | bytes 393216 | tf_op jit(solution)/shard_map/all_to_all | solution.py:43
  52.0 0.0 all-to-all-done
  52.0 6.5 %all-to-all-start.3 = ((bf16[8,4,3,1024]{3,1,2,0:T(4,128)(2,1)}), bf16[8,4,3,1024]{3,1,2,0:T(4,128)(2,1)S(1)}, u32[]{:S(2)}, u32[]{:S(2)}) async-start(bf16[8,4,3,1024]{3,1,2,0:T(4,128)(2,1)} %copy.40), calls=%async_computation.3 | async-start | bytes 393216 | tf_op jit(solution)/shard_map/all_to_all | solution.py:42
  58.5 4.8 %reshape.63 = bf16[4096,1,3,8]{3,2,1,0:T(4,128)(2,1)} reshape(bf16[4,2,12288]{2,1,0:T(2,128)(2,1)S(1)} %all-to-all-done) | data formatting | bytes 393216
  63.2 6.7 %copy.36 = bf16[8,4,3,1024]{3,1,2,0:T(4,128)(2,1)} copy(bf16[8,4,3,1024]{0,2,3,1:T(4,128)(2,1)} %bitcast.46) | data formatting | bytes 393216 | tf_op jit(solution)/shard_map/all_to_all | solution.py:50
  69.9 0.0 all-to-all-done.3
  69.9 6.0 %all-to-all-start.1 = ((bf16[8,4,3,1024]{3,1,2,0:T(4,128)(2,1)}), bf16[8,4,3,1024]{3,1,2,0:T(4,128)(2,1)S(1)}, u32[]{:S(2)}, u32[]{:S(2)}) async-start(bf16[8,4,3,1024]{3,1,2,0:T(4,128)(2,1)} %copy.36), calls=%async_computation.1 | async-start | bytes 393216 | tf_op jit(solution)/shard_map/all_to_all | solution.py:49
  75.9 0.2 all-reduce.3.cloned.1.call-start
  76.1 0.1 copy.41
  76.2 0.2 reshape.26
  76.4 9.2 %fusion.12 = f32[96,7168]{1,0:T(8,128)} fusion(bf16[96,1024]{1,0:T(8,128)(2,1)S(1)} %reshape.26, bf16[1024,7168]{1,0:T(8,128)(2,1)} %param.9), kind=kOutput, calls=%fused_computation.27 | convolution fusion | flops 1409286144 | bytes 17629184 | tf_op jit(solution)/shard_map/dot_general | solution.py:60
  85.6 9.2 %fusion.11 = f32[96,7168]{1,0:T(8,128)} fusion(bf16[96,1024]{1,0:T(8,128)(2,1)S(1)} %reshape.26, bf16[1024,7168]{1,0:T(8,128)(2,1)} %param.10), kind=kOutput, calls=%fused_computation.26 | convolution fusion | flops 1409286144 | bytes 17629184 | tf_op jit(solution)/shard_map/dot_general | solution.py:61
  94.7 0.1 copy.37
  94.9 0.2 reshape.25
  95.0 11.3 %fusion.10 = f32[96,7168]{1,0:T(8,128)} fusion(bf16[96,1024]{1,0:T(8,128)(2,1)S(1)} %reshape.25, bf16[7168,1024]{1,0:T(8,128)(2,1)} %param.11), kind=kOutput, calls=%fused_computation.25 | convolution fusion | flops 1409286144 | bytes 17629184 | tf_op jit(solution)/shard_map/dot_general | solution.py:62
  106.3 0.0 all-reduce.3.cloned.1.call-update
  106.4 153.3 %all-reduce.3.cloned.1.call-done = (f32[96,7168]{1,0:T(8,128)}, f32[96,7168]{1,0:T(8,128)}, f32[96,7168]{1,0:T(8,128)}) async-done(((f32[96,7168]{1,0:T(8,128)}, f32[96,7168]{1,0:T(8,128)}, f32[96,7168]{1,0:T(8,128)}), (f32[96,7168]{1,0:T(8,128)}, f32[96,7168]{1,0:T(8,128)}, f32[96,7168]{1,0:T(8,128)})) %all-reduce.3.cloned.1.call-update) | async-done | bytes 8257552 | tf_op jit(solution)/shard_map/psum | solution.py:65
  259.6 10.3 %convolution_convert_fusion = bf16[7168,1024]{1,0:T(8,128)(2,1)} fusion(bf16[96,1024]{1,0:T(8,128)(2,1)S(1)} %reshape.25, f32[96,7168]{1,0:T(8,128)} %get-tuple-element.6, f32[96,7168]{1,0:T(8,128)} %get-tuple-element.4), kind=kOutput, calls=%fused_computation.3 | convolution fusion | flops 1420754944 | bytes 20381696 | tf_op jit(solution)/shard_map/dot_general | solution.py:19
  270.0 4.0 %multiply_convert_fusion.1 = (bf16[96,7168]{1,0:T(8,128)(2,1)S(1)}, bf16[96,7168]{1,0:T(8,128)(2,1)S(1)}) fusion(f32[96,7168]{1,0:T(8,128)} %get-tuple-element.5, f32[96,7168]{1,0:T(8,128)S(1)} %copy-done, f32[96,7168]{1,0:T(8,128)} %get-tuple-element.6), kind=kLoop, calls=%fused_computation.7 | loop fusion | flops 8945664 | bytes 11010048 | tf_op jit(solution)/shard_map/convert_element_type | solution.py:13
  274.0 10.3 %fusion.13 = f32[96,1024]{1,0:T(8,128)S(1)} fusion(bf16[96,7168]{1,0:T(8,128)(2,1)S(1)} %get-tuple-element.8, bf16[1024,7168]{1,0:T(8,128)(2,1)} %param.9), kind=kOutput, calls=%fused_computation.28 | convolution fusion | flops 1409286144 | bytes 16449536 | tf_op jit(solution)/shard_map/dot_general | solution.py:67
  284.3 9.9 %fusion.1 = bf16[96,1024]{1,0:T(8,128)(2,1)S(1)} fusion(f32[96,1024]{1,0:T(8,128)S(1)} %fusion.13, bf16[96,7168]{1,0:T(8,128)(2,1)S(1)} %get-tuple-element.7, bf16[1024,7168]{1,0:T(8,128)(2,1)} %param.10), kind=kOutput, calls=%fused_computation.12 | convolution fusion | flops 1409482752 | bytes 16646144 | tf_op jit(solution)/shard_map/dot_general | solution.py:70
  294.2 0.1 convert_element_type.35
  294.3 0.8 copy.42
  295.1 3.6 %all-to-all-start.4 = ((bf16[8,4,3,1024]{3,0,2,1:T(8,128)(2,1)}), bf16[8,4,3,1024]{3,0,2,1:T(8,128)(2,1)S(1)}, u32[]{:S(2)}, u32[]{:S(2)}) async-start(bf16[8,4,3,1024]{3,0,2,1:T(8,128)(2,1)} %copy.42), calls=%async_computation.4 | async-start | bytes 393216 | tf_op jit(solution)/shard_map/all_to_all | solution.py:74
  298.8 7.6 %convolution_convert_fusion.1 = bf16[1024,7168]{1,0:T(8,128)(2,1)} fusion(bf16[96,1024]{1,0:T(8,128)(2,1)S(1)} %reshape.26, bf16[96,7168]{1,0:T(8,128)(2,1)S(1)} %get-tuple-element.7), kind=kOutput, calls=%fused_computation.4 | convolution fusion | flops 1416626176 | bytes 16252928 | tf_op jit(solution)/shard_map/dot_general | solution.py:19
  306.4 0.0 all-to-all-done.4
  306.4 0.2 copy.49
  306.5 0.9 reshape.55
  307.4 5.5 %all-to-all-start.5 = ((bf16[8,1,3,4096]{3,2,1,0:T(4,128)(2,1)}), bf16[8,1,3,4096]{3,2,1,0:T(4,128)(2,1)S(1)}, u32[]{:S(2)}, u32[]{:S(2)}) async-start(bf16[8,1,3,4096]{3,2,1,0:T(4,128)(2,1)} %reshape.55), calls=%async_computation.5 | async-start | bytes 524288 | tf_op jit(solution)/shard_map/all_to_all | solution.py:73
  312.9 8.9 %convolution_convert_fusion.2 = bf16[1024,7168]{1,0:T(8,128)(2,1)} fusion(bf16[96,1024]{1,0:T(8,128)(2,1)S(1)} %reshape.26, bf16[96,7168]{1,0:T(8,128)(2,1)} %copy-done.1), kind=kOutput, calls=%fused_computation.5 | convolution fusion | flops 1416626176 | bytes 16252928 | tf_op jit(solution)/shard_map/dot_general | solution.py:19
  321.8 0.3 all-to-all-done.5
  322.2 0.2 reshape.30
  322.3 1.3 gather_fusion
  (7 shorter events, 0.1 us)
Async XLA Ops:
  21.2 16.0 %all-to-all-start.2 = ((bf16[4,2,12288]{2,1,0:T(2,128)(2,1)}), bf16[4,2,12288]{2,1,0:T(2,128)(2,1)S(1)}, u32[]{:S(2)}, u32[]{:S(2)}) async-start(bf16[4,2,12288]{2,1,0:T(2,128)(2,1)} %reshape.60), calls=%async_computation.2 | async-start | bytes 393216 | tf_op jit(solution)/shard_map/all_to_all | solution.py:43
  37.2 14.8 %all-to-all-start = ((bf16[4,2,12288]{2,1,0:T(2,128)(2,1)}), bf16[4,2,12288]{2,1,0:T(2,128)(2,1)S(1)}, u32[]{:S(2)}, u32[]{:S(2)}) async-start(bf16[4,2,12288]{2,1,0:T(2,128)(2,1)} %reshape.62), calls=%async_computation | async-start | bytes 393216 | tf_op jit(solution)/shard_map/all_to_all | solution.py:50
  52.0 17.9 %all-to-all-start.3 = ((bf16[8,4,3,1024]{3,1,2,0:T(4,128)(2,1)}), bf16[8,4,3,1024]{3,1,2,0:T(4,128)(2,1)S(1)}, u32[]{:S(2)}, u32[]{:S(2)}) async-start(bf16[8,4,3,1024]{3,1,2,0:T(4,128)(2,1)} %copy.40), calls=%async_computation.3 | async-start | bytes 393216 | tf_op jit(solution)/shard_map/all_to_all | solution.py:42
  69.9 24.8 %all-to-all-start.1 = ((bf16[8,4,3,1024]{3,1,2,0:T(4,128)(2,1)}), bf16[8,4,3,1024]{3,1,2,0:T(4,128)(2,1)S(1)}, u32[]{:S(2)}, u32[]{:S(2)}) async-start(bf16[8,4,3,1024]{3,1,2,0:T(4,128)(2,1)} %copy.36), calls=%async_computation.1 | async-start | bytes 393216 | tf_op jit(solution)/shard_map/all_to_all | solution.py:49
  75.9 183.8 %all-reduce.3.cloned.1.call-start = ((), (), s32[]{:S(2)}) async-start(), calls=%async_computation.6 | async-start | bytes 16515072 | tf_op jit(solution)/shard_map/psum | solution.py:65
  259.6 10.3 %copy-start = (f32[96,7168]{1,0:T(8,128)S(1)}, f32[96,7168]{1,0:T(8,128)}, u32[]{:S(2)}) copy-start(f32[96,7168]{1,0:T(8,128)} %get-tuple-element.4) | copy-start | bytes 8257540
  274.0 10.3 %copy-start.1 = (bf16[96,7168]{1,0:T(8,128)(2,1)}, bf16[96,7168]{1,0:T(8,128)(2,1)S(1)}, u32[]{:S(2)}) copy-start(bf16[96,7168]{1,0:T(8,128)(2,1)S(1)} %get-tuple-element.8) | copy-start | bytes 4128772
  295.1 11.2 %all-to-all-start.4 = ((bf16[8,4,3,1024]{3,0,2,1:T(8,128)(2,1)}), bf16[8,4,3,1024]{3,0,2,1:T(8,128)(2,1)S(1)}, u32[]{:S(2)}, u32[]{:S(2)}) async-start(bf16[8,4,3,1024]{3,0,2,1:T(8,128)(2,1)} %copy.42), calls=%async_computation.4 | async-start | bytes 393216 | tf_op jit(solution)/shard_map/all_to_all | solution.py:74
  307.4 14.8 %all-to-all-start.5 = ((bf16[8,1,3,4096]{3,2,1,0:T(4,128)(2,1)}), bf16[8,1,3,4096]{3,2,1,0:T(4,128)(2,1)S(1)}, u32[]{:S(2)}, u32[]{:S(2)}) async-start(bf16[8,1,3,4096]{3,2,1,0:T(4,128)(2,1)} %reshape.55), calls=%async_computation.5 | async-start | bytes 524288 | tf_op jit(solution)/shard_map/all_to_all | solution.py:73
Sparse Core Ops, SparseCore 0:
  106.5 153.1 all-reduce.2
where the time goes:
time: 332 us; the launch traced here: 330 us
  waiting for transfers between devices  154 us (46%)
  matrix products  76.6 us (23%)
  local copies, waits for them, and re-layouts  50.4 us (15%)
  starting transfers between devices  29.4 us (9%)
  between operations  14.2 us (4%)
  other arithmetic  6.24 us (2%)
    psum x1, waiting for transfers between devices, on_device(): gate, up, dhid = lax.psum((gate_part, up_part, dhid_part), 'dp')  153 us
    dot_general x3, matrix products, contract_rows(): lax.dot_general(left, right, (((0,), (0,)), ((), ())), preferred_element_...  26.9 us
    unnamed x8, local copies, waits for them, and re-layouts  21.2 us
    dot_general x1, matrix products, on_device(): lax.dot_general(rows_grad, w_down, (((1,), (1,)), ((), ())), preferred_el...  11.3 us
    dot_general x1, matrix products, on_device(): lax.dot_general(d_gate, w_gate, (((1,), (1,)), ((), ())), preferred_eleme...  10.3 us
    dot_general x1, matrix products, on_device(): lax.dot_general(d_up, w_up, (((1,), (1,)), ((), ())), preferred_element_t...  9.9 us
    another operation x4, local copies, waits for them, and re-layouts, spread(): jnp.repeat(buffer.reshape(EXPERTS, 1, capacity, width), group, axis=0)  9.43 us
    dot_general x1, matrix products, on_device(): gate_part = jnp.dot(rows_in, w_gate, preferred_element_type=jnp.float32)  9.16 us
  transfers between devices with their start and end apart: 7, of which 2 were waited for; matrix products, arithmetic and copies ran while one was open for 21% of the time, Pallas kernels for 0%

commit v1 on v0

v1 whole, which is shorter than its diff:
```python
import jax
import jax.numpy as jnp
from jax import lax
from jax.sharding import PartitionSpec as P

EXPERTS = 8
ALL = ("dp", "expert")


def nonlinear(gate, up, dhid):
    sig = jax.nn.sigmoid(gate)
    act = gate * sig
    hidden = (act * up).astype(jnp.bfloat16)
    d_up = (dhid * act).astype(jnp.bfloat16)
    d_gate = (dhid * up * sig * (1.0 + gate * (1.0 - sig))).astype(jnp.bfloat16)
    return (hidden, d_up, d_gate)


def contract_rows(left, right):
    return lax.dot_general(
        left, right, (((0,), (0,)), ((), ())), preferred_element_type=jnp.float32
    )


def on_device(inputs, grad_out, labels, w_gate, w_up, w_down):
    members = lax.axis_size("expert")
    replicas = lax.axis_size("dp")
    group = members // EXPERTS
    tok_count = inputs.shape[0]
    width = inputs.shape[1]
    columns = width // replicas
    capacity = 3 * tok_count // (2 * EXPERTS)
    label_col = labels[:, 0]
    onehot = (label_col[:, None] == jnp.arange(EXPERTS, dtype=jnp.int32)[None, :]).astype(jnp.int32)
    before = jnp.cumsum(onehot, axis=0) - onehot
    rank_in = jnp.sum(before * onehot, axis=1)
    slot_ids = label_col * capacity + rank_in

    both = jnp.stack([inputs, grad_out])
    slots = jnp.zeros((2, EXPERTS * capacity, width), jnp.bfloat16).at[:, slot_ids].set(both)
    send = slots.reshape(2, EXPERTS, capacity, replicas, columns)
    send = jnp.transpose(send, (3, 1, 0, 2, 4))
    send = jnp.broadcast_to(
        send[:, :, None], (replicas, EXPERTS, group, 2, capacity, columns)
    ).reshape(replicas * members, 2 * capacity * columns)
    recv = lax.all_to_all(send, ALL, 0, 0, tiled=True)
    recv = recv.reshape(replicas * members, 2, capacity, columns)
    rows_in = recv[:, 0].reshape(-1, columns)
    rows_grad = recv[:, 1].reshape(-1, columns)

    gate_part = jnp.dot(rows_in, w_gate, preferred_element_type=jnp.float32)
    up_part = jnp.dot(rows_in, w_up, preferred_element_type=jnp.float32)
    dhid_part = lax.dot_general(
        rows_grad, w_down, (((1,), (1,)), ((), ())), preferred_element_type=jnp.float32
    )
    parts = jnp.stack([gate_part, up_part, dhid_part])
    reduced = lax.psum_scatter(parts, "dp", scatter_dimension=2, tiled=True)
    hidden, d_up, d_gate = nonlinear(reduced[0], reduced[1], reduced[2])
    gathered = lax.all_gather(jnp.stack([hidden, d_up, d_gate]), "dp", axis=2, tiled=True)
    hidden, d_up, d_gate = gathered[0], gathered[1], gathered[2]

    d_rows = lax.dot_general(
        d_gate, w_gate, (((1,), (1,)), ((), ())), preferred_element_type=jnp.float32
    )
    d_rows = d_rows + lax.dot_general(
        d_up, w_up, (((1,), (1,)), ((), ())), preferred_element_type=jnp.float32
    )
    back = d_rows.astype(jnp.bfloat16).reshape(replicas * members, capacity * columns)
    back = lax.all_to_all(back, ALL, 0, 0, tiled=True)
    back = back.reshape(replicas, EXPERTS, group, capacity, columns).astype(jnp.float32)
    summed = jnp.sum(back, axis=2)
    summed = jnp.transpose(summed, (1, 2, 0, 3)).reshape(EXPERTS * capacity, width)
    grad_in = summed[slot_ids].astype(jnp.bfloat16)
    grad_gate = contract_rows(rows_in, d_gate).astype(jnp.bfloat16)
    grad_up = contract_rows(rows_in, d_up).astype(jnp.bfloat16)
    grad_down = contract_rows(hidden, rows_grad).astype(jnp.bfloat16)
    return (grad_in, grad_gate, grad_up, grad_down)


def solution(mesh):
    return jax.shard_map(
        on_device,
        mesh=mesh,
        in_specs=(
            P(ALL, None),
            P(ALL, None),
            P(ALL, None),
            P("dp", "expert"),
            P("dp", "expert"),
            P("expert", "dp"),
        ),
        out_specs=(
            P(ALL, None),
            P("dp", "expert"),
            P("dp", "expert"),
            P("expert", "dp"),
        ),
        check_vma=False,
    )
```

time: 332 us -> 239 us (0.72)
  waiting for transfers between devices: 154 us -> 103 us
  local copies, waits for them, and re-layouts: 50.4 us -> 7.87 us
  starting transfers between devices: 29.4 us -> 5.17 us
  blocking collectives: 0 us -> 20.6 us
  other arithmetic: 6.24 us -> 18.1 us
  matrix products: 76.6 us -> 69.7 us
    psum x1 -> x0, waiting for transfers between devices: 153 us -> none  [on_device(): gate, up, dhid = lax.psum((gate_part, up_part, dhid_part), 'dp')]
    reduce_scatter x0 -> x1, waiting for transfers between devices: none -> 68.5 us  [on_device(): reduced = lax.psum_scatter(parts, 'dp', scatter_dimension=2, tiled=True)]
    all_gather x0 -> x1, waiting for transfers between devices: none -> 34.3 us  [on_device(): lax.all_gather(jnp.stack([hidden, d_up, d_gate]), 'dp', axis=2, tiled=True)]
    all_to_all x6 -> x1, starting transfers between devices: 29.1 us -> 4.86 us  [on_device(): back = lax.all_to_all(back, ALL, 0, 0, tiled=True)]
    all_to_all x0 -> x1, blocking collectives: none -> 20.6 us  [on_device(): recv = lax.all_to_all(send, ALL, 0, 0, tiled=True)]
    unnamed x8 -> x7, local copies, waits for them, and re-layouts: 21.2 us -> 1.6 us
    all_to_all x6 -> x3, local copies, waits for them, and re-layouts: 14.6 us -> 1.18 us  [the longest x2 1.03 us: on_device(): recv = lax.all_to_all(send, ALL, 0, 0, tiled=True)]
    another operation x4 -> x3, local copies, waits for them, and re-layouts: 9.43 us -> 0.61 us  [the longest x1 0.27 us: on_device(): both = jnp.stack([inputs, grad_out])]
  transfers between devices with their start and end apart: 7 -> 3, of which waited for: 2 -> 2; matrix products, arithmetic and copies ran while one was open for 21% -> 10% of each run, Pallas kernels for 0% -> 0%
where the time goes in v1:
time: 239 us; the launch traced here: 238 us
  waiting for transfers between devices  103 us (43%)
  matrix products  69.7 us (29%)
  blocking collectives  20.6 us (9%)
  other arithmetic  18.1 us (8%)
  between operations  14.2 us (6%)
  local copies, waits for them, and re-layouts  7.87 us (3%)
  starting transfers between devices  5.17 us (2%)
    reduce_scatter x1, waiting for transfers between devices, on_device(): reduced = lax.psum_scatter(parts, 'dp', scatter_dimension=2, tiled=True)  68.5 us
    all_gather x1, waiting for transfers between devices, on_device(): lax.all_gather(jnp.stack([hidden, d_up, d_gate]), 'dp', axis=2, tiled=True)  34.3 us
    dot_general x3, matrix products, contract_rows(): lax.dot_general(left, right, (((0,), (0,)), ((), ())), preferred_element_...  24.2 us
    all_to_all x1, blocking collectives, on_device(): recv = lax.all_to_all(send, ALL, 0, 0, tiled=True)  20.6 us
    dot_general x1, matrix products, on_device(): lax.dot_general(d_up, w_up, (((1,), (1,)), ((), ())), preferred_element_t...  10.3 us
    dot_general x1, matrix products, on_device(): lax.dot_general(d_gate, w_gate, (((1,), (1,)), ((), ())), preferred_eleme...  10.2 us
    dot_general x1, matrix products, on_device(): lax.dot_general(rows_grad, w_down, (((1,), (1,)), ((), ())), preferred_el...  9.74 us
    dot_general x1, matrix products, on_device(): gate_part = jnp.dot(rows_in, w_gate, preferred_element_type=jnp.float32)  7.63 us
  transfers between devices with their start and end apart: 3, of which 2 were waited for; matrix products, arithmetic and copies ran while one was open for 10% of the time, Pallas kernels for 0%

profile of v1, /device:TPU:0, one launch (start us, length us, event | category | flops | bytes accessed | tf_op | source)
XLA Modules:
  0.0 238.4 jit_solution(11816957071394104013)
XLA Ops:
  7.2 0.0 reduce-scatter.2.cloned.1.call-start
  7.2 0.7 fusion.5
  8.0 0.8 select_reduce_fusion
  8.8 0.7 fusion.6
  9.5 1.0 maximum_bitcast_fusion
  10.5 0.3 copy.20
  10.8 0.3 broadcast_in_dim.2
  11.1 1.1 scatter_fusion
  12.2 0.2 reshape.38
  12.4 0.3 copy.27
  12.8 0.5 all_to_all.16
  13.3 0.5 broadcast.47
  13.8 2.9 %reduce.3 = bf16[32,6144]{1,0:T(8,128)(2,1)S(1)} reduce(bf16[32,1,6144]{2,1,0:T(2,128)(2,1)S(1)} %all_to_all.16, bf16[]{:T(256)} %broadcast.47), dimensions={1}, to_apply=%all_to_all.16.reduce_sub_computation | reduce | bytes 786434 | tf_op jit(solution)/shard_map/all_to_all | solution.py:46
  16.8 0.3 reshape.66
  17.0 20.6 %all_to_all.20 = bf16[32,2,3072]{2,1,0:T(2,128)(2,1)S(1)} all-to-all(bf16[32,2,3072]{2,1,0:T(2,128)(2,1)S(1)} %reshape.66), channel_id=1, replica_groups=mesh['dp'=4,'expert'=8] {'dp','expert'}, dimensions={0} | all-to-all | bytes 786432 | tf_op jit(solution)/shard_map/all_to_all | solution.py:46
  37.7 0.3 reshape.67
  38.0 2.3 reduce
  40.3 0.6 reshape.39
  40.9 0.2 fusion.7
  41.1 0.2 reshape_squeeze.6
  41.3 0.2 reshape_squeeze.7
  41.4 7.6 %convolution_bitcast_fusion.1 = f32[1,96,7168]{2,1,0:T(8,128)S(1)} fusion(bf16[96,1024]{1,0:T(8,128)(2,1)S(1)} %reshape_squeeze.6, bf16[1024,7168]{1,0:T(8,128)(2,1)} %param.10), kind=kOutput, calls=%fused_computation.6 | convolution fusion | flops 1409286144 | bytes 17629184 | tf_op jit(solution)/shard_map/dot_general | solution.py:52
  49.1 7.6 %convolution_bitcast_fusion.2 = f32[1,96,7168]{2,1,0:T(8,128)S(1)} fusion(bf16[96,1024]{1,0:T(8,128)(2,1)S(1)} %reshape_squeeze.6, bf16[1024,7168]{1,0:T(8,128)(2,1)} %param.9), kind=kOutput, calls=%fused_computation.7 | convolution fusion | flops 1409286144 | bytes 17629184 | tf_op jit(solution)/shard_map/dot_general | solution.py:51
  56.7 9.7 %convolution_bitcast_fusion = f32[1,96,7168]{2,1,0:T(8,128)S(1)} fusion(bf16[96,1024]{1,0:T(8,128)(2,1)S(1)} %reshape_squeeze.7, bf16[7168,1024]{1,0:T(8,128)(2,1)} %param.11), kind=kOutput, calls=%fused_computation.5 | convolution fusion | flops 1409286144 | bytes 17629184 | tf_op jit(solution)/shard_map/dot_general | solution.py:53
  66.4 3.7 %pad_maximum_fusion = f32[3,96,7168]{2,1,0:T(8,128)} fusion(f32[1,96,7168]{2,1,0:T(8,128)S(1)} %convolution_bitcast_fusion, f32[1,96,7168]{2,1,0:T(8,128)S(1)} %convolution_bitcast_fusion.1, f32[1,96,7168]{2,1,0:T(8,128)S(1)} %convolution_bitcast_fusion.2), kind=kLoop, calls=%fused_computation.8 | loop fusion | flops 4128768 | bytes 16515072 | tf_op jit(solution)/shard_map/stack | solution.py:56
  70.2 0.0 reduce-scatter.2.cloned.1.call-update
  70.2 0.3 all-gather.2.cloned.1.call-start
  70.5 68.5 %reduce-scatter.2.cloned.1.call-done = f32[3,96,1792]{2,1,0:T(8,128)} async-done(((f32[3,96,7168]{2,1,0:T(8,128)}), f32[3,96,1792]{2,1,0:T(8,128)}) %reduce-scatter.2.cloned.1.call-update) | async-done | bytes 2064400 | tf_op jit(solution)/shard_map/reduce_scatter | solution.py:57
  138.9 1.9 multiply_convert_fusion.2
  140.8 1.1 pad_maximum_fusion.1
  141.9 0.0 all-gather.2.cloned.1.call-update
  141.9 34.3 %all-gather.2.cloned.1.call-done = bf16[3,96,7168]{2,1,0:T(8,128)(2,1)} async-done(((bf16[3,96,1792]{2,1,0:T(8,128)(2,1)}), bf16[3,96,7168]{2,1,0:T(8,128)(2,1)}) %all-gather.2.cloned.1.call-update) | async-done | bytes 4128784 | tf_op jit(solution)/shard_map/all_gather | solution.py:59
  176.2 10.2 %fusion = f32[96,1024]{1,0:T(8,128)S(1)} fusion(bf16[1024,7168]{1,0:T(8,128)(2,1)} %param.9, bf16[3,96,7168]{2,1,0:T(8,128)(2,1)} %all-gather.2.cloned.1.call-done), kind=kOutput, calls=%fused_computation.12 | convolution fusion | flops 1409286144 | bytes 16449536 | tf_op jit(solution)/shard_map/dot_general | solution.py:62
  186.4 10.3 %fusion.3 = bf16[96,1024]{1,0:T(8,128)(2,1)S(1)} fusion(f32[96,1024]{1,0:T(8,128)S(1)} %fusion, bf16[1024,7168]{1,0:T(8,128)(2,1)} %param.10, bf16[3,96,7168]{2,1,0:T(8,128)(2,1)} %all-gather.2.cloned.1.call-done), kind=kOutput, calls=%fused_computation.15 | convolution fusion | flops 1409482752 | bytes 16646144 | tf_op jit(solution)/shard_map/dot_general | solution.py:65
  196.7 0.1 all_to_all.17
  196.8 1.8 reduce.4
  198.6 0.8 reshape.68
  199.4 4.9 %all-to-all-start.1 = ((bf16[32,2,1536]{2,1,0:T(2,128)(2,1)}), bf16[32,2,1536]{2,1,0:T(2,128)(2,1)S(1)}, u32[]{:S(2)}, u32[]{:S(2)}) async-start(bf16[32,2,1536]{2,1,0:T(2,128)(2,1)} %reshape.68), calls=%async_computation.2 | async-start | bytes 393216 | tf_op jit(solution)/shard_map/all_to_all | solution.py:69
  204.3 9.1 %convolution_convert_fusion = bf16[7168,1024]{1,0:T(8,128)(2,1)} fusion(bf16[96,1024]{1,0:T(8,128)(2,1)S(1)} %reshape_squeeze.7, bf16[3,96,7168]{2,1,0:T(8,128)(2,1)} %all-gather.2.cloned.1.call-done), kind=kOutput, calls=%fused_computation.2 | convolution fusion | flops 1416626176 | bytes 16252928 | tf_op jit(solution)/shard_map/dot_general | solution.py:20
  213.4 7.6 %convolution_convert_fusion.1 = bf16[1024,7168]{1,0:T(8,128)(2,1)} fusion(bf16[96,1024]{1,0:T(8,128)(2,1)S(1)} %reshape_squeeze.6, bf16[3,96,7168]{2,1,0:T(8,128)(2,1)S(1)} %copy-done), kind=kOutput, calls=%fused_computation.3 | convolution fusion | flops 1416626176 | bytes 16252928 | tf_op jit(solution)/shard_map/dot_general | solution.py:20
  220.9 7.6 %convolution_convert_fusion.2 = bf16[1024,7168]{1,0:T(8,128)(2,1)} fusion(bf16[96,1024]{1,0:T(8,128)(2,1)S(1)} %reshape_squeeze.6, bf16[3,96,7168]{2,1,0:T(8,128)(2,1)S(1)} %copy-done), kind=kOutput, calls=%fused_computation.4 | convolution fusion | flops 1416626176 | bytes 16252928 | tf_op jit(solution)/shard_map/dot_general | solution.py:20
  228.5 0.0 all-to-all-done.1
  228.5 0.1 reshape.69
  228.7 1.1 convert_reduce_fusion
  229.8 0.3 reshape.46
  230.1 0.2 copy.24
  230.3 0.1 copy.25
  230.3 1.3 gather_fusion
  (4 shorter events, 0.0 us)
Async XLA Ops:
  7.2 131.8 %reduce-scatter.2.cloned.1.call-start = ((), (), s32[]{:S(2)}) async-start(), calls=%async_computation.3 | async-start | bytes 10321920 | tf_op jit(solution)/shard_map/reduce_scatter | solution.py:57
  70.2 106.0 %all-gather.2.cloned.1.call-start = ((), (), s32[]{:S(2)}) async-start(), calls=%async_computation.4 | async-start | bytes 5160960 | tf_op jit(solution)/shard_map/all_gather | solution.py:59
  199.4 29.1 %all-to-all-start.1 = ((bf16[32,2,1536]{2,1,0:T(2,128)(2,1)}), bf16[32,2,1536]{2,1,0:T(2,128)(2,1)S(1)}, u32[]{:S(2)}, u32[]{:S(2)}) async-start(bf16[32,2,1536]{2,1,0:T(2,128)(2,1)} %reshape.68), calls=%async_computation.2 | async-start | bytes 393216 | tf_op jit(solution)/shard_map/all_to_all | solution.py:69
  204.3 9.1 %copy-start = (bf16[3,96,7168]{2,1,0:T(8,128)(2,1)S(1)}, bf16[3,96,7168]{2,1,0:T(8,128)(2,1)}, u32[]{:S(2)}) copy-start(bf16[3,96,7168]{2,1,0:T(8,128)(2,1)} %all-gather.2.cloned.1.call-done) | copy-start | bytes 12386308
Sparse Core Ops, SparseCore 0:
  70.3 68.5 reduce-scatter.1
  142.0 34.0 all-gather.1

commit v2 on v1

--- a/solution.py
+++ b/solution.py
@@ -53,8 +53,8 @@
     dhid_part = lax.dot_general(
         rows_grad, w_down, (((1,), (1,)), ((), ())), preferred_element_type=jnp.float32
     )
-    parts = jnp.stack([gate_part, up_part, dhid_part])
-    reduced = lax.psum_scatter(parts, "dp", scatter_dimension=2, tiled=True)
+    parts = jnp.stack([gate_part, up_part, dhid_part]).astype(jnp.bfloat16)
+    reduced = lax.psum_scatter(parts, "dp", scatter_dimension=2, tiled=True).astype(jnp.float32)
     hidden, d_up, d_gate = nonlinear(reduced[0], reduced[1], reduced[2])
     gathered = lax.all_gather(jnp.stack([hidden, d_up, d_gate]), "dp", axis=2, tiled=True)
     hidden, d_up, d_gate = gathered[0], gathered[1], gathered[2]

time: 239 us -> 210 us (0.88)
  waiting for transfers between devices: 103 us -> 75.9 us
    reduce_scatter x1, waiting for transfers between devices: 68.5 us -> 41.6 us  [on_device(): lax.psum_scatter(parts, 'dp', scatter_dimension=2, tiled=True)]
  transfers between devices with their start and end apart: 3 -> 3, of which waited for: 2 -> 2; matrix products, arithmetic and copies ran while one was open for 10% -> 12% of each run, Pallas kernels for 0% -> 0%
where the time goes in v2:
time: 210 us
  waiting for transfers between devices  75.9 us (36%)
  matrix products  69.6 us (33%)
  blocking collectives  20.6 us (10%)
  other arithmetic  16.5 us (8%)
  between operations  14.3 us (7%)
  local copies, waits for them, and re-layouts  7.87 us (4%)
  starting transfers between devices  5.17 us (2%)
    reduce_scatter x1, waiting for transfers between devices, on_device(): lax.psum_scatter(parts, 'dp', scatter_dimension=2, tiled=True)  41.6 us
    all_gather x1, waiting for transfers between devices, on_device(): lax.all_gather(jnp.stack([hidden, d_up, d_gate]), 'dp', axis=2, tiled=True)  34.3 us
    dot_general x3, matrix products, contract_rows(): lax.dot_general(left, right, (((0,), (0,)), ((), ())), preferred_element_...  24.2 us
    all_to_all x1, blocking collectives, on_device(): recv = lax.all_to_all(send, ALL, 0, 0, tiled=True)  20.6 us
    dot_general x1, matrix products, on_device(): lax.dot_general(d_up, w_up, (((1,), (1,)), ((), ())), preferred_element_t...  10.2 us
    dot_general x1, matrix products, on_device(): lax.dot_general(d_gate, w_gate, (((1,), (1,)), ((), ())), preferred_eleme...  10.2 us
    dot_general x1, matrix products, on_device(): lax.dot_general(rows_grad, w_down, (((1,), (1,)), ((), ())), preferred_el...  9.74 us
    dot_general x1, matrix products, on_device(): up_part = jnp.dot(rows_in, w_up, preferred_element_type=jnp.float32)  7.61 us
  transfers between devices with their start and end apart: 3, of which 2 were waited for; matrix products, arithmetic and copies ran while one was open for 12% of the time, Pallas kernels for 0%

profile of v2, /device:TPU:0, one launch (start us, length us, event | category | flops | bytes accessed | tf_op | source)
XLA Modules:
  0.0 209.9 jit_solution(955686034386004192)
XLA Ops:
  7.2 0.0 reduce-scatter.2.cloned.1.call-start
  7.2 0.7 fusion.8
  8.0 0.8 select_reduce_fusion
  8.8 0.7 fusion.9
  9.5 1.0 maximum_bitcast_fusion
  10.5 0.3 copy.20
  10.8 0.3 broadcast_in_dim.2
  11.1 1.1 scatter_fusion
  12.2 0.2 reshape.38
  12.4 0.3 copy.27
  12.8 0.5 all_to_all.16
  13.3 0.5 broadcast.47
  13.8 2.9 %reduce.3 = bf16[32,6144]{1,0:T(8,128)(2,1)S(1)} reduce(bf16[32,1,6144]{2,1,0:T(2,128)(2,1)S(1)} %all_to_all.16, bf16[]{:T(256)} %broadcast.47), dimensions={1}, to_apply=%all_to_all.16.reduce_sub_computation | reduce | bytes 786434 | tf_op jit(solution)/shard_map/all_to_all | solution.py:46
  16.8 0.3 reshape.66
  17.0 20.6 %all_to_all.20 = bf16[32,2,3072]{2,1,0:T(2,128)(2,1)S(1)} all-to-all(bf16[32,2,3072]{2,1,0:T(2,128)(2,1)S(1)} %reshape.66), channel_id=1, replica_groups=mesh['dp'=4,'expert'=8] {'dp','expert'}, dimensions={0} | all-to-all | bytes 786432 | tf_op jit(solution)/shard_map/all_to_all | solution.py:46
  37.7 0.3 reshape.67
  38.0 2.3 %reduce = bf16[32,6144]{1,0:T(8,128)(2,1)S(1)} reduce(bf16[32,1,6144]{2,1,0:T(2,128)(2,1)S(1)} %reshape.67, bf16[]{:T(256)} %constant.19), dimensions={1}, to_apply=%all_to_all.13.reduce_sub_computation | reduce | bytes 786434 | tf_op jit(solution)/shard_map/all_to_all | solution.py:46
  40.3 0.6 reshape.39
  40.9 0.2 fusion.10
  41.1 0.2 reshape_squeeze.6
  41.3 0.2 reshape_squeeze.7
  41.4 7.6 %fusion.1 = bf16[1,96,7168]{2,1,0:T(8,128)(2,1)S(1)} fusion(bf16[96,1024]{1,0:T(8,128)(2,1)S(1)} %reshape_squeeze.6, bf16[1024,7168]{1,0:T(8,128)(2,1)} %param.10), kind=kOutput, calls=%fused_computation.9 | convolution fusion | flops 1409974272 | bytes 16252928 | tf_op jit(solution)/shard_map/dot_general | solution.py:52
  49.0 7.6 %fusion = bf16[1,96,7168]{2,1,0:T(8,128)(2,1)S(1)} fusion(bf16[96,1024]{1,0:T(8,128)(2,1)S(1)} %reshape_squeeze.6, bf16[1024,7168]{1,0:T(8,128)(2,1)} %param.9), kind=kOutput, calls=%fused_computation.8 | convolution fusion | flops 1409974272 | bytes 16252928 | tf_op jit(solution)/shard_map/dot_general | solution.py:51
  56.7 9.7 %fusion.2 = bf16[1,96,7168]{2,1,0:T(8,128)(2,1)S(1)} fusion(bf16[96,1024]{1,0:T(8,128)(2,1)S(1)} %reshape_squeeze.7, bf16[7168,1024]{1,0:T(8,128)(2,1)} %param.11), kind=kOutput, calls=%fused_computation.10 | convolution fusion | flops 1409974272 | bytes 16252928 | tf_op jit(solution)/shard_map/dot_general | solution.py:53
  66.4 2.2 %pad_maximum_fusion = bf16[3,96,7168]{2,1,0:T(8,128)(2,1)} fusion(bf16[1,96,7168]{2,1,0:T(8,128)(2,1)S(1)} %fusion.2, bf16[1,96,7168]{2,1,0:T(8,128)(2,1)S(1)} %fusion.1, bf16[1,96,7168]{2,1,0:T(8,128)(2,1)S(1)} %fusion), kind=kLoop, calls=%fused_computation.11 | loop fusion | flops 4128768 | bytes 8257536 | tf_op jit(solution)/shard_map/stack | solution.py:56
  68.6 0.0 reduce-scatter.2.cloned.1.call-update
  68.7 0.3 all-gather.2.cloned.1.call-start
  68.9 41.6 %reduce-scatter.2.cloned.1.call-done = bf16[3,96,1792]{2,1,0:T(8,128)(2,1)} async-done(((bf16[3,96,7168]{2,1,0:T(8,128)(2,1)}), bf16[3,96,1792]{2,1,0:T(8,128)(2,1)}) %reduce-scatter.2.cloned.1.call-update) | async-done | bytes 1032208 | tf_op jit(solution)/shard_map/reduce_scatter | solution.py:57
  110.6 1.4 convert_element_type.42
  111.9 0.4 multiply_convert_fusion.2
  112.3 1.1 pad_maximum_fusion.1
  113.4 0.0 all-gather.2.cloned.1.call-update
  113.4 34.3 %all-gather.2.cloned.1.call-done = bf16[3,96,7168]{2,1,0:T(8,128)(2,1)} async-done(((bf16[3,96,1792]{2,1,0:T(8,128)(2,1)}), bf16[3,96,7168]{2,1,0:T(8,128)(2,1)}) %all-gather.2.cloned.1.call-update) | async-done | bytes 4128784 | tf_op jit(solution)/shard_map/all_gather | solution.py:59
  147.7 10.2 %fusion.3 = f32[96,1024]{1,0:T(8,128)S(1)} fusion(bf16[1024,7168]{1,0:T(8,128)(2,1)} %param.9, bf16[3,96,7168]{2,1,0:T(8,128)(2,1)} %all-gather.2.cloned.1.call-done), kind=kOutput, calls=%fused_computation.15 | convolution fusion | flops 1409286144 | bytes 16449536 | tf_op jit(solution)/shard_map/dot_general | solution.py:62
  157.9 10.2 %fusion.6 = bf16[96,1024]{1,0:T(8,128)(2,1)S(1)} fusion(f32[96,1024]{1,0:T(8,128)S(1)} %fusion.3, bf16[1024,7168]{1,0:T(8,128)(2,1)} %param.10, bf16[3,96,7168]{2,1,0:T(8,128)(2,1)} %all-gather.2.cloned.1.call-done), kind=kOutput, calls=%fused_computation.18 | convolution fusion | flops 1409482752 | bytes 16646144 | tf_op jit(solution)/shard_map/dot_general | solution.py:65
  168.2 0.1 all_to_all.17
  168.3 1.8 reduce.4
  170.1 0.8 reshape.68
  170.9 4.9 %all-to-all-start.1 = ((bf16[32,2,1536]{2,1,0:T(2,128)(2,1)}), bf16[32,2,1536]{2,1,0:T(2,128)(2,1)S(1)}, u32[]{:S(2)}, u32[]{:S(2)}) async-start(bf16[32,2,1536]{2,1,0:T(2,128)(2,1)} %reshape.68), calls=%async_computation.2 | async-start | bytes 393216 | tf_op jit(solution)/shard_map/all_to_all | solution.py:69
  175.8 9.1 %convolution_convert_fusion = bf16[7168,1024]{1,0:T(8,128)(2,1)} fusion(bf16[96,1024]{1,0:T(8,128)(2,1)S(1)} %reshape_squeeze.7, bf16[3,96,7168]{2,1,0:T(8,128)(2,1)} %all-gather.2.cloned.1.call-done), kind=kOutput, calls=%fused_computation.2 | convolution fusion | flops 1416626176 | bytes 16252928 | tf_op jit(solution)/shard_map/dot_general | solution.py:20
  184.9 7.6 %convolution_convert_fusion.1 = bf16[1024,7168]{1,0:T(8,128)(2,1)} fusion(bf16[96,1024]{1,0:T(8,128)(2,1)S(1)} %reshape_squeeze.6, bf16[3,96,7168]{2,1,0:T(8,128)(2,1)S(1)} %copy-done), kind=kOutput, calls=%fused_computation.3 | convolution fusion | flops 1416626176 | bytes 16252928 | tf_op jit(solution)/shard_map/dot_general | solution.py:20
  192.4 7.6 %convolution_convert_fusion.2 = bf16[1024,7168]{1,0:T(8,128)(2,1)} fusion(bf16[96,1024]{1,0:T(8,128)(2,1)S(1)} %reshape_squeeze.6, bf16[3,96,7168]{2,1,0:T(8,128)(2,1)S(1)} %copy-done), kind=kOutput, calls=%fused_computation.4 | convolution fusion | flops 1416626176 | bytes 16252928 | tf_op jit(solution)/shard_map/dot_general | solution.py:20
  200.0 0.1 reshape.69
  200.2 1.1 convert_reduce_fusion
  201.3 0.3 reshape.46
  201.6 0.2 copy.24
  201.8 0.1 copy.25
  201.8 1.3 gather_fusion
  (5 shorter events, 0.0 us)
Async XLA Ops:
  7.2 103.4 %reduce-scatter.2.cloned.1.call-start = ((), (), s32[]{:S(2)}) async-start(), calls=%async_computation.3 | async-start | bytes 5160960 | tf_op jit(solution)/shard_map/reduce_scatter | solution.py:57
  68.7 79.0 %all-gather.2.cloned.1.call-start = ((), (), s32[]{:S(2)}) async-start(), calls=%async_computation.4 | async-start | bytes 5160960 | tf_op jit(solution)/shard_map/all_gather | solution.py:59
  170.9 29.1 %all-to-all-start.1 = ((bf16[32,2,1536]{2,1,0:T(2,128)(2,1)}), bf16[32,2,1536]{2,1,0:T(2,128)(2,1)S(1)}, u32[]{:S(2)}, u32[]{:S(2)}) async-start(bf16[32,2,1536]{2,1,0:T(2,128)(2,1)} %reshape.68), calls=%async_computation.2 | async-start | bytes 393216 | tf_op jit(solution)/shard_map/all_to_all | solution.py:69
  175.8 9.1 %copy-start = (bf16[3,96,7168]{2,1,0:T(8,128)(2,1)S(1)}, bf16[3,96,7168]{2,1,0:T(8,128)(2,1)}, u32[]{:S(2)}) copy-start(bf16[3,96,7168]{2,1,0:T(8,128)(2,1)} %all-gather.2.cloned.1.call-done) | copy-start | bytes 12386308
Sparse Core Ops, SparseCore 0:
  68.8 41.7 reduce-scatter.1
  113.5 34.0 all-gather.1

commit v3 on v2

--- a/solution.py
+++ b/solution.py
@@ -5,6 +5,8 @@
 
 EXPERTS = 8
 ALL = ("dp", "expert")
+CHUNKS = 2
+LINK = jnp.float32
 
 
 def nonlinear(gate, up, dhid):
@@ -48,32 +50,42 @@
     rows_in = recv[:, 0].reshape(-1, columns)
     rows_grad = recv[:, 1].reshape(-1, columns)
 
-    gate_part = jnp.dot(rows_in, w_gate, preferred_element_type=jnp.float32)
-    up_part = jnp.dot(rows_in, w_up, preferred_element_type=jnp.float32)
-    dhid_part = lax.dot_general(
-        rows_grad, w_down, (((1,), (1,)), ((), ())), preferred_element_type=jnp.float32
-    )
-    parts = jnp.stack([gate_part, up_part, dhid_part]).astype(jnp.bfloat16)
-    reduced = lax.psum_scatter(parts, "dp", scatter_dimension=2, tiled=True).astype(jnp.float32)
-    hidden, d_up, d_gate = nonlinear(reduced[0], reduced[1], reduced[2])
-    gathered = lax.all_gather(jnp.stack([hidden, d_up, d_gate]), "dp", axis=2, tiled=True)
-    hidden, d_up, d_gate = gathered[0], gathered[1], gathered[2]
-
-    d_rows = lax.dot_general(
-        d_gate, w_gate, (((1,), (1,)), ((), ())), preferred_element_type=jnp.float32
-    )
-    d_rows = d_rows + lax.dot_general(
-        d_up, w_up, (((1,), (1,)), ((), ())), preferred_element_type=jnp.float32
-    )
+    ff = w_gate.shape[1]
+    step = ff // CHUNKS
+    d_rows = None
+    grads = ([], [], [])
+    for k in range(CHUNKS):
+        cols = slice(k * step, (k + 1) * step)
+        g_mat, u_mat, d_mat = w_gate[:, cols], w_up[:, cols], w_down[cols, :]
+        gate_part = jnp.dot(rows_in, g_mat, preferred_element_type=jnp.float32)
+        up_part = jnp.dot(rows_in, u_mat, preferred_element_type=jnp.float32)
+        dhid_part = lax.dot_general(
+            rows_grad, d_mat, (((1,), (1,)), ((), ())), preferred_element_type=jnp.float32
+        )
+        parts = jnp.stack([gate_part, up_part, dhid_part]).astype(LINK)
+        reduced = lax.psum_scatter(parts, "dp", scatter_dimension=2, tiled=True)
+        reduced = reduced.astype(jnp.float32)
+        hidden, d_up, d_gate = nonlinear(reduced[0], reduced[1], reduced[2])
+        gathered = lax.all_gather(jnp.stack([hidden, d_up, d_gate]), "dp", axis=2, tiled=True)
+        hidden, d_up, d_gate = gathered[0], gathered[1], gathered[2]
+        part_rows = lax.dot_general(
+            d_gate, g_mat, (((1,), (1,)), ((), ())), preferred_element_type=jnp.float32
+        ) + lax.dot_general(
+            d_up, u_mat, (((1,), (1,)), ((), ())), preferred_element_type=jnp.float32
+        )
+        d_rows = part_rows if d_rows is None else d_rows + part_rows
+        grads[0].append(contract_rows(rows_in, d_gate).astype(jnp.bfloat16))
+        grads[1].append(contract_rows(rows_in, d_up).astype(jnp.bfloat16))
+        grads[2].append(contract_rows(hidden, rows_grad).astype(jnp.bfloat16))
     back = d_rows.astype(jnp.bfloat16).reshape(replicas * members, capacity * columns)
     back = lax.all_to_all(back, ALL, 0, 0, tiled=True)
     back = back.reshape(replicas, EXPERTS, group, capacity, columns).astype(jnp.float32)
     summed = jnp.sum(back, axis=2)
     summed = jnp.transpose(summed, (1, 2, 0, 3)).reshape(EXPERTS * capacity, width)
     grad_in = summed[slot_ids].astype(jnp.bfloat16)
-    grad_gate = contract_rows(rows_in, d_gate).astype(jnp.bfloat16)
-    grad_up = contract_rows(rows_in, d_up).astype(jnp.bfloat16)
-    grad_down = contract_rows(hidden, rows_grad).astype(jnp.bfloat16)
+    grad_gate = jnp.concatenate(grads[0], axis=1)
+    grad_up = jnp.concatenate(grads[1], axis=1)
+    grad_down = jnp.concatenate(grads[2], axis=0)
     return (grad_in, grad_gate, grad_up, grad_down)
 
 

time: 210 us -> 299 us (1.42); the launches traced: 210 us -> 294 us
  other arithmetic: 16.5 us -> 60.5 us
  waiting for transfers between devices: 75.9 us -> 110 us
  matrix products: 69.6 us -> 73.7 us
    concatenate x0 -> x2, other arithmetic: none -> 40.1 us  [the longest x1 21.8 us: on_device(): grad_down = jnp.concatenate(grads[2], axis=0)]
    reduce_scatter x1 -> x2, waiting for transfers between devices: 41.6 us -> 69.1 us  [on_device(): reduced = lax.psum_scatter(parts, 'dp', scatter_dimension=2, tiled=True)]
    all_gather x1 -> x2, waiting for transfers between devices: 34.3 us -> 41.1 us  [on_device(): lax.all_gather(jnp.stack([hidden, d_up, d_gate]), 'dp', axis=2, tiled=True)]
    dot_general x5 -> x10, matrix products: 45.4 us -> 52 us  [the longest x2 11.3 us: on_device(): lax.dot_general(d_up, u_mat, (((1,), (1,)), ((), ())), preferred_element_...]
    dot_general x3 -> x6, matrix products: 24.2 us -> 21.6 us  [contract_rows(): lax.dot_general(left, right, (((0,), (0,)), ((), ())), preferred_element_...]
  transfers between devices with their start and end apart: 3 -> 5, of which waited for: 2 -> 4; matrix products, arithmetic and copies ran while one was open for 12% -> 30% of each run, Pallas kernels for 0% -> 0%
where the time goes in v3:
time: 299 us; the launch traced here: 294 us
  waiting for transfers between devices  110 us (37%)
  matrix products  73.7 us (25%)
  other arithmetic  60.5 us (20%)
  blocking collectives  20.8 us (7%)
  between operations  14.5 us (5%)
  local copies, waits for them, and re-layouts  9.31 us (3%)
  starting transfers between devices  5.09 us (2%)
    reduce_scatter x2, waiting for transfers between devices, on_device(): reduced = lax.psum_scatter(parts, 'dp', scatter_dimension=2, tiled=True)  69.1 us
    all_gather x2, waiting for transfers between devices, on_device(): lax.all_gather(jnp.stack([hidden, d_up, d_gate]), 'dp', axis=2, tiled=True)  41.1 us
    concatenate x1, other arithmetic, on_device(): grad_down = jnp.concatenate(grads[2], axis=0)  21.8 us
    dot_general x6, matrix products, contract_rows(): lax.dot_general(left, right, (((0,), (0,)), ((), ())), preferred_element_...  21.6 us
    all_to_all x1, blocking collectives, on_device(): recv = lax.all_to_all(send, ALL, 0, 0, tiled=True)  20.8 us
    concatenate x1, other arithmetic, on_device(): grad_gate = jnp.concatenate(grads[0], axis=1)  18.4 us
    dot_general x2, matrix products, on_device(): lax.dot_general(d_up, u_mat, (((1,), (1,)), ((), ())), preferred_element_...  11.3 us
    dot_general x2, matrix products, on_device(): lax.dot_general(d_gate, g_mat, (((1,), (1,)), ((), ())), preferred_elemen...  11.2 us
  transfers between devices with their start and end apart: 5, of which 4 were waited for; matrix products, arithmetic and copies ran while one was open for 30% of the time, Pallas kernels for 0%

profile of v3, /device:TPU:0, one launch (start us, length us, event | category | flops | bytes accessed | tf_op | source)
XLA Modules:
  0.0 294.2 jit_solution(2347005948940509694)
XLA Ops:
  7.2 0.7 fusion.52
  8.0 0.8 select_reduce_fusion
  8.8 0.7 fusion.53
  9.5 1.0 maximum_bitcast_fusion
  10.8 0.3 broadcast_in_dim.2
  11.1 1.1 scatter_fusion
  12.4 0.3 copy.27
  12.8 0.5 all_to_all.16
  13.3 0.5 broadcast.61
  13.8 2.9 %reduce.3 = bf16[32,6144]{1,0:T(8,128)(2,1)S(1)} reduce(bf16[32,1,6144]{2,1,0:T(2,128)(2,1)S(1)} %all_to_all.16, bf16[]{:T(256)} %broadcast.61), dimensions={1}, to_apply=%all_to_all.16.reduce_sub_computation | reduce | bytes 786434 | tf_op jit(solution)/shard_map/all_to_all | solution.py:48
  17.0 20.8 %all_to_all.20 = bf16[32,2,3072]{2,1,0:T(2,128)(2,1)S(1)} all-to-all(bf16[32,2,3072]{2,1,0:T(2,128)(2,1)S(1)} %reshape.66), channel_id=1, replica_groups=mesh['dp'=4,'expert'=8] {'dp','expert'}, dimensions={0} | all-to-all | bytes 786432 | tf_op jit(solution)/shard_map/all_to_all | solution.py:48
  37.8 0.3 reshape.67
  38.2 2.3 reduce
  40.5 0.6 reshape.39
  41.4 4.4 %fusion.26 = f32[1,96,3584]{2,1,0:T(8,128)S(1)} fusion(bf16[96,1024]{1,0:T(8,128)(2,1)S(1)} %reshape_squeeze.6, bf16[1024,7168]{1,0:T(8,128)(2,1)} %param.9), kind=kOutput, calls=%fused_computation.33 | convolution fusion | flops 704643072 | bytes 8912896 | tf_op jit(solution)/shard_map/dot_general | solution.py:60
  45.8 4.4 %fusion.29 = f32[1,96,3584]{2,1,0:T(8,128)S(1)} fusion(bf16[96,1024]{1,0:T(8,128)(2,1)S(1)} %reshape_squeeze.6, bf16[1024,7168]{1,0:T(8,128)(2,1)} %param.10), kind=kOutput, calls=%fused_computation.34 | convolution fusion | flops 704643072 | bytes 8912896 | tf_op jit(solution)/shard_map/dot_general | solution.py:61
  50.3 5.4 %fusion.35 = f32[1,96,3584]{2,1,0:T(8,128)S(1)} fusion(bf16[96,1024]{1,0:T(8,128)(2,1)S(1)} %reshape_squeeze.7, bf16[7168,1024]{1,0:T(8,128)(2,1)} %param.11), kind=kOutput, calls=%fused_computation.36 | convolution fusion | flops 704643072 | bytes 8912896 | tf_op jit(solution)/shard_map/dot_general | solution.py:62
  55.8 2.3 pad_maximum_fusion.4
  58.1 4.4 %fusion.20 = f32[1,96,3584]{2,1,0:T(8,128)S(1)} fusion(bf16[96,1024]{1,0:T(8,128)(2,1)S(1)} %reshape_squeeze.6, bf16[1024,7168]{1,0:T(8,128)(2,1)} %param.9), kind=kOutput, calls=%fused_computation.31 | convolution fusion | flops 704643072 | bytes 8912896 | tf_op jit(solution)/shard_map/dot_general | solution.py:60
  62.5 5.6 %fusion.23 = f32[1,96,3584]{2,1,0:T(8,128)S(1)} fusion(bf16[96,1024]{1,0:T(8,128)(2,1)S(1)} %reshape_squeeze.6, bf16[1024,7168]{1,0:T(8,128)(2,1)} %param.10), kind=kOutput, calls=%fused_computation.32 | convolution fusion | flops 704643072 | bytes 8912896 | tf_op jit(solution)/shard_map/dot_general | solution.py:61
  68.1 5.4 %fusion.32 = f32[1,96,3584]{2,1,0:T(8,128)S(1)} fusion(bf16[96,1024]{1,0:T(8,128)(2,1)S(1)} %reshape_squeeze.7, bf16[7168,1024]{1,0:T(8,128)(2,1)} %param.11), kind=kOutput, calls=%fused_computation.35 | convolution fusion | flops 704643072 | bytes 8912896 | tf_op jit(solution)/shard_map/dot_general | solution.py:62
  73.5 2.3 pad_maximum_fusion.3
  75.9 24.1 %reduce-scatter.5.cloned.1.call-done = f32[3,96,896]{2,1,0:T(8,128)} async-done(((f32[3,96,3584]{2,1,0:T(8,128)}), f32[3,96,896]{2,1,0:T(8,128)}) %reduce-scatter.5.cloned.1.call-update) | async-done | bytes 1032208 | tf_op jit(solution)/shard_map/reduce_scatter | solution.py:66
  100.0 1.4 multiply_convert_fusion.2
  101.4 0.9 pad_maximum_fusion.6
  102.5 45.0 %reduce-scatter.3.cloned.1.call-done = f32[3,96,896]{2,1,0:T(8,128)} async-done(((f32[3,96,3584]{2,1,0:T(8,128)}), f32[3,96,896]{2,1,0:T(8,128)}) %reduce-scatter.3.cloned.1.call-update) | async-done | bytes 1032208 | tf_op jit(solution)/shard_map/reduce_scatter | solution.py:66
  147.5 1.4 multiply_convert_fusion.5
  148.9 0.9 pad_maximum_fusion.5
  149.8 22.3 %all-gather.5.cloned.1.call-done = bf16[3,96,3584]{2,1,0:T(8,128)(2,1)} async-done(((bf16[3,96,896]{2,1,0:T(8,128)(2,1)}), bf16[3,96,3584]{2,1,0:T(8,128)(2,1)}) %all-gather.5.cloned.1.call-update) | async-done | bytes 2064400 | tf_op jit(solution)/shard_map/all_gather | solution.py:69
  172.1 5.6 %fusion.4 = f32[96,1024]{1,0:T(8,128)S(1)} fusion(bf16[1024,7168]{1,0:T(8,128)(2,1)} %param.10, bf16[3,96,3584]{2,1,0:T(8,128)(2,1)} %all-gather.5.cloned.1.call-done), kind=kOutput, calls=%fused_computation.15 | convolution fusion | flops 704643072 | bytes 8421376 | tf_op jit(solution)/shard_map/dot_general | solution.py:73
  177.7 18.8 %all-gather.3.cloned.1.call-done = bf16[3,96,3584]{2,1,0:T(8,128)(2,1)} async-done(((bf16[3,96,896]{2,1,0:T(8,128)(2,1)}), bf16[3,96,3584]{2,1,0:T(8,128)(2,1)}) %all-gather.3.cloned.1.call-update) | async-done | bytes 2064400 | tf_op jit(solution)/shard_map/all_gather | solution.py:69
  196.5 5.6 %fusion.12 = f32[96,1024]{1,0:T(8,128)S(1)} fusion(bf16[1024,7168]{1,0:T(8,128)(2,1)} %param.10, bf16[3,96,3584]{2,1,0:T(8,128)(2,1)} %all-gather.3.cloned.1.call-done), kind=kOutput, calls=%fused_computation.23 | convolution fusion | flops 704643072 | bytes 8421376 | tf_op jit(solution)/shard_map/dot_general | solution.py:73
  202.2 5.8 %fusion.38 = f32[96,1024]{1,0:T(8,128)S(1)} fusion(f32[96,1024]{1,0:T(8,128)S(1)} %fusion.12, bf16[1024,7168]{1,0:T(8,128)(2,1)} %param.9, bf16[3,96,3584]{2,1,0:T(8,128)(2,1)} %all-gather.3.cloned.1.call-done), kind=kOutput, calls=%fused_computation.39 | convolution fusion | flops 704741376 | bytes 8814592 | tf_op jit(solution)/shard_map/dot_general | solution.py:71
  207.9 5.4 %fusion.47 = bf16[96,1024]{1,0:T(8,128)(2,1)S(1)} fusion(f32[96,1024]{1,0:T(8,128)S(1)} %fusion.38, f32[96,1024]{1,0:T(8,128)S(1)} %fusion.4, bf16[1024,7168]{1,0:T(8,128)(2,1)} %param.9, bf16[3,96,3584]{2,1,0:T(8,128)(2,1)S(1)} %copy-done), kind=kOutput, calls=%fused_computation.42 | convolution fusion | flops 704937984 | bytes 9011200 | tf_op jit(solution)/shard_map/dot_general | solution.py:71
  213.5 1.8 reduce.4
  215.3 0.8 reshape.68
  216.1 4.7 %all-to-all-start.1 = ((bf16[32,2,1536]{2,1,0:T(2,128)(2,1)}), bf16[32,2,1536]{2,1,0:T(2,128)(2,1)}, u32[]{:S(2)}, u32[]{:S(2)}) async-start(bf16[32,2,1536]{2,1,0:T(2,128)(2,1)} %reshape.68), calls=%async_computation.3 | async-start | bytes 393216 | tf_op jit(solution)/shard_map/all_to_all | solution.py:81
  220.8 2.1 convolution_convert_fusion.2
  223.0 5.2 %convolution_convert_fusion.4 = bf16[1024,3584]{1,0:T(8,128)(2,1)} fusion(bf16[96,1024]{1,0:T(8,128)(2,1)S(1)} %reshape_squeeze.6, bf16[3,96,3584]{2,1,0:T(8,128)(2,1)S(1)} %copy-done), kind=kOutput, calls=%fused_computation.9 | convolution fusion | flops 708313088 | bytes 8224768 | tf_op jit(solution)/shard_map/dot_general | solution.py:22
  228.1 5.1 %convolution_convert_fusion.3 = bf16[1024,3584]{1,0:T(8,128)(2,1)} fusion(bf16[96,1024]{1,0:T(8,128)(2,1)S(1)} %reshape_squeeze.6, bf16[3,96,3584]{2,1,0:T(8,128)(2,1)S(1)} %copy-done.1), kind=kOutput, calls=%fused_computation.8 | convolution fusion | flops 708313088 | bytes 8224768 | tf_op jit(solution)/shard_map/dot_general | solution.py:22
  233.3 5.1 %convolution_convert_fusion.5 = bf16[1024,3584]{1,0:T(8,128)(2,1)} fusion(bf16[96,1024]{1,0:T(8,128)(2,1)S(1)} %reshape_squeeze.6, bf16[3,96,3584]{2,1,0:T(8,128)(2,1)S(1)} %copy-done.1), kind=kOutput, calls=%fused_computation.10 | convolution fusion | flops 708313088 | bytes 8224768 | tf_op jit(solution)/shard_map/dot_general | solution.py:22
  238.3 18.4 %pad_maximum_fusion = (bf16[1024,7168]{1,0:T(8,128)(2,1)}, bf16[1024,7168]{1,0:T(8,128)(2,1)}) fusion(bf16[1024,3584]{1,0:T(8,128)(2,1)} %convolution_convert_fusion.4, bf16[1024,3584]{1,0:T(8,128)(2,1)} %convolution_convert_fusion.5, bf16[1024,3584]{1,0:T(8,128)(2,1)S(1)} %convolution_convert_fusion.2, bf16[1024,3584]{1,0:T(8,128)(2,1)} %convolution_convert_fusion.3), kind=kLoop, calls=%fused_computation.2 | loop fusion | flops 58720256 | bytes 58720256 | tf_op jit(solution)/shard_map/concatenate | solution.py:86
  256.7 2.1 convolution_convert_fusion
  258.8 2.1 convolution_convert_fusion.1
  260.9 21.8 %pad_maximum_fusion.2 = bf16[7168,1024]{1,0:T(8,128)(2,1)} fusion(bf16[3584,1024]{1,0:T(8,128)(2,1)S(1)} %convolution_convert_fusion, bf16[3584,1024]{1,0:T(8,128)(2,1)S(1)} %convolution_convert_fusion.1), kind=kLoop, calls=%fused_computation.4 | loop fusion | flops 29360128 | bytes 29360128 | tf_op jit(solution)/shard_map/concatenate | solution.py:88
  282.6 1.6 reshape.69
  284.2 1.1 convert_reduce_fusion
  285.9 1.3 gather_fusion
  (27 shorter events, 2.5 us)
Async XLA Ops:
  7.2 92.8 %reduce-scatter.5.cloned.1.call-start = ((), (), s32[]{:S(2)}) async-start(), calls=%async_computation.6 | async-start | bytes 5160960 | tf_op jit(solution)/shard_map/reduce_scatter | solution.py:66
  58.1 89.4 %reduce-scatter.3.cloned.1.call-start = ((), (), s32[]{:S(2)}) async-start(), calls=%async_computation.4 | async-start | bytes 5160960 | tf_op jit(solution)/shard_map/reduce_scatter | solution.py:66
  75.8 96.3 %all-gather.5.cloned.1.call-start = ((), (), s32[]{:S(2)}) async-start(), calls=%async_computation.7 | async-start | bytes 2580480 | tf_op jit(solution)/shard_map/all_gather | solution.py:69
  102.3 94.2 %all-gather.3.cloned.1.call-start = ((), (), s32[]{:S(2)}) async-start(), calls=%async_computation.5 | async-start | bytes 2580480 | tf_op jit(solution)/shard_map/all_gather | solution.py:69
  202.1 5.8 %copy-start = (bf16[3,96,3584]{2,1,0:T(8,128)(2,1)S(1)}, bf16[3,96,3584]{2,1,0:T(8,128)(2,1)}, u32[]{:S(2)}) copy-start(bf16[3,96,3584]{2,1,0:T(8,128)(2,1)} %all-gather.5.cloned.1.call-done) | copy-start | bytes 6193156
  216.1 66.5 %all-to-all-start.1 = ((bf16[32,2,1536]{2,1,0:T(2,128)(2,1)}), bf16[32,2,1536]{2,1,0:T(2,128)(2,1)}, u32[]{:S(2)}, u32[]{:S(2)}) async-start(bf16[32,2,1536]{2,1,0:T(2,128)(2,1)} %reshape.68), calls=%async_computation.3 | async-start | bytes 393216 | tf_op jit(solution)/shard_map/all_to_all | solution.py:81
  223.0 5.2 %copy-start.1 = (bf16[3,96,3584]{2,1,0:T(8,128)(2,1)S(1)}, bf16[3,96,3584]{2,1,0:T(8,128)(2,1)}, u32[]{:S(2)}) copy-start(bf16[3,96,3584]{2,1,0:T(8,128)(2,1)} %all-gather.3.cloned.1.call-done) | copy-start | bytes 6193156
  256.7 2.1 copy-start.2
Sparse Core Ops, SparseCore 0:
  58.2 41.7 reduce-scatter.4
  103.3 44.1 reduce-scatter.2
  149.7 22.3 all-gather.4
  174.1 22.3 all-gather.2

commit v4 on v2

--- a/solution.py
+++ b/solution.py
@@ -2,6 +2,8 @@
 import jax.numpy as jnp
 from jax import lax
 from jax.sharding import PartitionSpec as P
+from jax.experimental import pallas as pl
+from jax.experimental.pallas import tpu as pltpu
 
 EXPERTS = 8
 ALL = ("dp", "expert")
@@ -20,6 +22,60 @@
     return lax.dot_general(
         left, right, (((0,), (0,)), ((), ())), preferred_element_type=jnp.float32
     )
+
+
+def _bwd_body(dg_ref, du_ref, ht_ref, xt_ref, y_ref, wg_ref, wu_ref,
+              drows_ref, gg_ref, gu_ref, gd_ref):
+    @pl.when(pl.program_id(0) == 0)
+    def _():
+        drows_ref[...] = jnp.zeros_like(drows_ref)
+    dg = dg_ref[...]
+    du = du_ref[...]
+    nt = (((1,), (1,)), ((), ()))
+    drows_ref[...] += lax.dot_general(dg, wg_ref[...], nt, preferred_element_type=jnp.float32) + \
+        lax.dot_general(du, wu_ref[...], nt, preferred_element_type=jnp.float32)
+    xt = xt_ref[...]
+    gg_ref[...] = jnp.dot(xt, dg, preferred_element_type=jnp.float32).astype(gg_ref.dtype)
+    gu_ref[...] = jnp.dot(xt, du, preferred_element_type=jnp.float32).astype(gu_ref.dtype)
+    gd_ref[...] = jnp.dot(ht_ref[...], y_ref[...], preferred_element_type=jnp.float32).astype(gd_ref.dtype)
+
+def fused_backward(d_gate, d_up, hidden, rows_in, rows_grad, w_gate, w_up):
+    rows, ff = d_gate.shape
+    cols = rows_in.shape[1]
+    tile = 512 if ff % 512 == 0 else ff
+    steps = ff // tile
+    hidden_t = hidden.T
+    rows_in_t = rows_in.T
+    bf = jnp.bfloat16
+    return pl.pallas_call(
+        _bwd_body,
+        grid=(steps,),
+        in_specs=[
+            pl.BlockSpec((rows, tile), lambda k: (0, k)),
+            pl.BlockSpec((rows, tile), lambda k: (0, k)),
+            pl.BlockSpec((tile, rows), lambda k: (k, 0)),
+            pl.BlockSpec((cols, rows), lambda k: (0, 0)),
+            pl.BlockSpec((rows, cols), lambda k: (0, 0)),
+            pl.BlockSpec((cols, tile), lambda k: (0, k)),
+            pl.BlockSpec((cols, tile), lambda k: (0, k)),
+        ],
+        out_specs=[
+            pl.BlockSpec((rows, cols), lambda k: (0, 0)),
+            pl.BlockSpec((cols, tile), lambda k: (0, k)),
+            pl.BlockSpec((cols, tile), lambda k: (0, k)),
+            pl.BlockSpec((tile, cols), lambda k: (k, 0)),
+        ],
+        out_shape=[
+            jax.ShapeDtypeStruct((rows, cols), jnp.float32),
+            jax.ShapeDtypeStruct((cols, ff), bf),
+            jax.ShapeDtypeStruct((cols, ff), bf),
+            jax.ShapeDtypeStruct((ff, cols), bf),
+        ],
+        compiler_params=pltpu.CompilerParams(dimension_semantics=("arbitrary",)),
+        cost_estimate=pl.CostEstimate(
+            flops=2 * rows * ff * cols * 5, transcendentals=0,
+            bytes_accessed=2 * (2 * cols * ff + 3 * cols * ff + 3 * rows * ff)),
+    )(d_gate, d_up, hidden_t, rows_in_t, rows_grad, w_gate, w_up)
 
 
 def on_device(inputs, grad_out, labels, w_gate, w_up, w_down):
@@ -59,11 +115,8 @@
     gathered = lax.all_gather(jnp.stack([hidden, d_up, d_gate]), "dp", axis=2, tiled=True)
     hidden, d_up, d_gate = gathered[0], gathered[1], gathered[2]
 
-    d_rows = lax.dot_general(
-        d_gate, w_gate, (((1,), (1,)), ((), ())), preferred_element_type=jnp.float32
-    )
-    d_rows = d_rows + lax.dot_general(
-        d_up, w_up, (((1,), (1,)), ((), ())), preferred_element_type=jnp.float32
+    d_rows, grad_gate, grad_up, grad_down = fused_backward(
+        d_gate, d_up, hidden, rows_in, rows_grad, w_gate, w_up
     )
     back = d_rows.astype(jnp.bfloat16).reshape(replicas * members, capacity * columns)
     back = lax.all_to_all(back, ALL, 0, 0, tiled=True)
@@ -71,9 +124,6 @@
     summed = jnp.sum(back, axis=2)
     summed = jnp.transpose(summed, (1, 2, 0, 3)).reshape(EXPERTS * capacity, width)
     grad_in = summed[slot_ids].astype(jnp.bfloat16)
-    grad_gate = contract_rows(rows_in, d_gate).astype(jnp.bfloat16)
-    grad_up = contract_rows(rows_in, d_up).astype(jnp.bfloat16)
-    grad_down = contract_rows(hidden, rows_grad).astype(jnp.bfloat16)
     return (grad_in, grad_gate, grad_up, grad_down)
 
 

time: 210 us -> 248 us (1.18)
  matrix products: 69.6 us -> 32.8 us
  Pallas kernels: 0 us -> 34.8 us
  waiting for transfers between devices: 75.9 us -> 101 us
  local copies, waits for them, and re-layouts: 7.87 us -> 20.2 us
  other arithmetic: 16.5 us -> 19.2 us
    dot_general x5 -> x0, matrix products: 44.7 us -> none  [the longest x3 24.2 us: contract_rows(): lax.dot_general(left, right, (((0,), (0,)), ((), ())), preferred_element_...]
    pallas_call x0 -> x1, Pallas kernels: none -> 34.8 us  [fused_backward(): pl.pallas_call(_bwd_body, grid=(steps,), in_specs=[pl.BlockSpec((rows, ti...]
    reduce_scatter x1, waiting for transfers between devices: 41.6 us -> 50.9 us  [on_device(): lax.psum_scatter(parts, 'dp', scatter_dimension=2, tiled=True)]
    all_to_all x1, waiting for transfers between devices: 0.01 us -> 8.53 us  [on_device(): back = lax.all_to_all(back, ALL, 0, 0, tiled=True)]
    all_gather x1, waiting for transfers between devices: 34.3 us -> 41.2 us  [on_device(): lax.all_gather(jnp.stack([hidden, d_up, d_gate]), 'dp', axis=2, tiled=True)]
    squeeze x0 -> x2, local copies, waits for them, and re-layouts: none -> 6.56 us  [on_device(): hidden, d_up, d_gate = (gathered[0], gathered[1], gathered[2])]
    dot_general x1, matrix products: 7.61 us -> 12.5 us  [on_device(): up_part = jnp.dot(rows_in, w_up, preferred_element_type=jnp.float32)]
    transpose x0 -> x1, local copies, waits for them, and re-layouts: none -> 4.79 us  [fused_backward(): hidden_t = hidden.T]
  transfers between devices with their start and end apart: 3 -> 3, of which waited for: 2 -> 3; matrix products, arithmetic and copies ran while one was open for 12% -> 0% of each run, Pallas kernels for 0% -> 0%
where the time goes in v4:
time: 248 us; the launch traced here: 247 us
  waiting for transfers between devices  101 us (41%)
  Pallas kernels  34.8 us (14%)
  matrix products  32.8 us (13%)
  blocking collectives  20.6 us (8%)
  local copies, waits for them, and re-layouts  20.2 us (8%)
  other arithmetic  19.2 us (8%)
  between operations  14.3 us (6%)
  starting transfers between devices  4.68 us (2%)
    reduce_scatter x1, waiting for transfers between devices, on_device(): lax.psum_scatter(parts, 'dp', scatter_dimension=2, tiled=True)  50.9 us
    all_gather x1, waiting for transfers between devices, on_device(): lax.all_gather(jnp.stack([hidden, d_up, d_gate]), 'dp', axis=2, tiled=True)  41.2 us
    pallas_call x1, Pallas kernels, fused_backward(): pl.pallas_call(_bwd_body, grid=(steps,), in_specs=[pl.BlockSpec((rows, ti...  34.8 us
    all_to_all x1, blocking collectives, on_device(): recv = lax.all_to_all(send, ALL, 0, 0, tiled=True)  20.6 us
    dot_general x1, matrix products, on_device(): up_part = jnp.dot(rows_in, w_up, preferred_element_type=jnp.float32)  12.5 us
    dot_general x1, matrix products, on_device(): gate_part = jnp.dot(rows_in, w_gate, preferred_element_type=jnp.float32)  11 us
    dot_general x1, matrix products, on_device(): lax.dot_general(rows_grad, w_down, (((1,), (1,)), ((), ())), preferred_el...  9.29 us
    all_to_all x1, waiting for transfers between devices, on_device(): back = lax.all_to_all(back, ALL, 0, 0, tiled=True)  8.53 us
  transfers between devices with their start and end apart: 3, of which 3 were waited for; matrix products, arithmetic and copies ran while one was open for 0% of the time, Pallas kernels for 0%

profile of v4, /device:TPU:0, one launch (start us, length us, event | category | flops | bytes accessed | tf_op | source)
XLA Modules:
  0.0 247.3 jit_solution(2043144694085044262)
XLA Ops:
  7.2 0.0 reduce-scatter.2.cloned.1.call-start
  7.2 0.7 fusion.4
  8.0 0.8 select_reduce_fusion
  8.8 0.7 fusion.5
  9.5 1.0 maximum_bitcast_fusion
  10.5 0.3 copy.38
  10.8 0.3 broadcast_in_dim.2
  11.1 1.1 scatter_fusion
  12.2 0.2 reshape.38
  12.4 0.3 copy.54
  12.8 0.5 all_to_all.16
  13.3 0.5 broadcast.47
  13.8 2.9 %reduce.3 = bf16[32,6144]{1,0:T(8,128)(2,1)S(1)} reduce(bf16[32,1,6144]{2,1,0:T(2,128)(2,1)S(1)} %all_to_all.16, bf16[]{:T(256)} %broadcast.47), dimensions={1}, to_apply=%all_to_all.16.reduce_sub_computation | reduce | bytes 786434 | tf_op jit(solution)/shard_map/all_to_all | solution.py:102
  16.8 0.3 reshape.66
  17.0 20.6 %all_to_all.20 = bf16[32,2,3072]{2,1,0:T(2,128)(2,1)S(1)} all-to-all(bf16[32,2,3072]{2,1,0:T(2,128)(2,1)S(1)} %reshape.66), channel_id=1, replica_groups=mesh['dp'=4,'expert'=8] {'dp','expert'}, dimensions={0} | all-to-all | bytes 786432 | tf_op jit(solution)/shard_map/all_to_all | solution.py:102
  37.7 0.5 reshape.67
  38.2 2.3 reduce
  40.5 0.6 reshape.39
  41.1 0.2 fusion.6
  41.3 0.2 reshape_squeeze.6
  41.4 11.0 %fusion = bf16[1,96,7168]{1,2,0:T(8,128)(2,1)S(1)} fusion(bf16[96,1024]{1,0:T(8,128)(2,1)S(1)} %reshape_squeeze.6, bf16[1024,7168]{1,0:T(8,128)(2,1)} %wg_ref.1), kind=kOutput, calls=%fused_computation.5 | convolution fusion | flops 1409974272 | bytes 16252928 | tf_op jit(solution)/shard_map/dot_general | solution.py:107
  52.4 12.5 %fusion.1 = bf16[1,96,7168]{1,2,0:T(8,128)(2,1)} fusion(bf16[96,1024]{1,0:T(8,128)(2,1)S(1)} %reshape_squeeze.6, bf16[1024,7168]{1,0:T(8,128)(2,1)} %wu_ref.1), kind=kOutput, calls=%fused_computation.6 | convolution fusion | flops 1409974272 | bytes 16252928 | tf_op jit(solution)/shard_map/dot_general | solution.py:108
  64.9 0.2 reshape_squeeze.7.y_ref
  65.1 9.3 %fusion.2 = bf16[1,96,7168]{1,2,0:T(8,128)(2,1)S(1)} fusion(bf16[96,1024]{1,0:T(8,128)(2,1)S(1)} %reshape_squeeze.7.y_ref, bf16[7168,1024]{1,0:T(8,128)(2,1)} %param.11), kind=kOutput, calls=%fused_computation.7 | convolution fusion | flops 1409974272 | bytes 16252928 | tf_op jit(solution)/shard_map/dot_general | solution.py:109
  74.4 3.3 %pad_maximum_fusion = bf16[3,96,7168]{1,2,0:T(8,128)(2,1)} fusion(bf16[1,96,7168]{1,2,0:T(8,128)(2,1)S(1)} %fusion.2, bf16[1,96,7168]{1,2,0:T(8,128)(2,1)S(1)} %copy-done, bf16[1,96,7168]{1,2,0:T(8,128)(2,1)S(1)} %fusion), kind=kLoop, calls=%fused_computation.8 | loop fusion | flops 4128768 | bytes 8257536 | tf_op jit(solution)/shard_map/stack | solution.py:112
  77.7 0.0 all-gather.2.cloned.1.call-start
  77.7 50.9 %reduce-scatter.2.cloned.1.call-done = bf16[3,96,1792]{1,2,0:T(8,128)(2,1)} async-done(((bf16[3,96,7168]{1,2,0:T(8,128)(2,1)}), bf16[3,96,1792]{1,2,0:T(8,128)(2,1)}) %reduce-scatter.2.cloned.1.call-update) | async-done | bytes 1032208 | tf_op jit(solution)/shard_map/reduce_scatter | solution.py:113
  128.7 1.5 convert_element_type.33
  130.2 0.6 multiply_convert_fusion.2
  130.8 1.4 pad_maximum_fusion.1
  132.2 0.8 copy.44
  133.0 41.2 %all-gather.2.cloned.1.call-done = bf16[3,96,7168]{1,2,0:T(8,128)(2,1)} async-done(((bf16[3,96,1792]{1,2,0:T(8,128)(2,1)}), bf16[3,96,7168]{1,2,0:T(8,128)(2,1)}) %all-gather.2.cloned.1.call-update) | async-done | bytes 4128784 | tf_op jit(solution)/shard_map/all_gather | solution.py:115
  174.3 4.8 %slice_bitcast_fusion = (bf16[7168,96]{1,0:T(8,128)(2,1)}, bf16[96,7168]{0,1:T(8,128)(2,1)S(1)}, bf16[96,7168]{0,1:T(8,128)(2,1)}) fusion(bf16[3,96,7168]{1,2,0:T(8,128)(2,1)} %all-gather.2.cloned.1.call-done), kind=kLoop, calls=%fused_computation.9 | loop fusion | bytes 8257536 | tf_op jit(solution)/shard_map/transpose | solution.py:47
  179.1 3.7 %copy.45.dg_ref = bf16[96,7168]{1,0:T(8,128)(2,1)} copy(bf16[96,7168]{0,1:T(8,128)(2,1)} %get-tuple-element.14) | data formatting | bytes 2752512 | tf_op jit(solution)/shard_map/squeeze | solution.py:116
  182.8 2.8 %copy.46.du_ref = bf16[96,7168]{1,0:T(8,128)(2,1)} copy(bf16[96,7168]{0,1:T(8,128)(2,1)S(1)} %get-tuple-element.13) | data formatting | bytes 2752512 | tf_op jit(solution)/shard_map/squeeze | solution.py:116
  185.6 34.8 %shard_map.93 = (f32[96,1024]{1,0:T(8,128)}, bf16[1024,7168]{1,0:T(8,128)(2,1)}, bf16[1024,7168]{1,0:T(8,128)(2,1)}, bf16[7168,1024]{1,0:T(8,128)(2,1)}) custom-call(bf16[96,7168]{1,0:T(8,128)(2,1)} %copy.45.dg_ref, bf16[96,7168]{1,0:T(8,128)(2,1)} %copy.46.du_ref, bf16[7168,96]{1,0:T(8,128)(2,1)} %get-tuple-element.12.ht_ref, bf16[1024,96]{1,0:T(8,128)(2,1)} %bitcast.43, ...), custom_call_target="tpu_custom_call" | custom-call | flops 7046430720 | bytes 77529088 | tf_op jit(solution)/shard_map/pallas_call | solution.py:50
  220.4 1.0 convert_element_type.37
  221.4 0.1 all_to_all.17
  221.6 1.8 reduce.4
  223.4 0.8 reshape.68
  224.2 4.6 %all-to-all-start.1 = ((bf16[32,2,1536]{2,1,0:T(2,128)(2,1)}), bf16[32,2,1536]{2,1,0:T(2,128)(2,1)S(1)}, u32[]{:S(2)}, u32[]{:S(2)}) async-start(bf16[32,2,1536]{2,1,0:T(2,128)(2,1)} %reshape.68), calls=%async_computation.2 | async-start | bytes 393216 | tf_op jit(solution)/shard_map/all_to_all | solution.py:122
  228.8 8.5 %all-to-all-done.1 = bf16[32,2,1536]{2,1,0:T(2,128)(2,1)S(1)} async-done(((bf16[32,2,1536]{2,1,0:T(2,128)(2,1)}), bf16[32,2,1536]{2,1,0:T(2,128)(2,1)S(1)}, u32[]{:S(2)}, u32[]{:S(2)}) %all-to-all-start.1) | async-done | bytes 196640 | tf_op jit(solution)/shard_map/all_to_all | solution.py:122
  237.3 0.1 reshape.69
  237.5 1.1 convert_reduce_fusion
  238.6 0.3 reshape.46
  238.9 0.2 copy.48
  239.1 0.1 copy.52
  239.2 1.3 gather_fusion
  (8 shorter events, 0.1 us)
Async XLA Ops:
  7.2 121.5 %reduce-scatter.2.cloned.1.call-start = ((), (), s32[]{:S(2)}) async-start(), calls=%async_computation.3 | async-start | bytes 6881280 | tf_op jit(solution)/shard_map/reduce_scatter | solution.py:113
  65.1 9.3 %copy-start.1 = (bf16[96,1024]{1,0:T(8,128)(2,1)}, bf16[96,1024]{1,0:T(8,128)(2,1)S(1)}, u32[]{:S(2)}) copy-start(bf16[96,1024]{1,0:T(8,128)(2,1)S(1)} %reshape_squeeze.7.y_ref) | copy-start | bytes 589828
  65.1 9.3 %copy-start = (bf16[1,96,7168]{1,2,0:T(8,128)(2,1)S(1)}, bf16[1,96,7168]{1,2,0:T(8,128)(2,1)}, u32[]{:S(2)}) copy-start(bf16[1,96,7168]{1,2,0:T(8,128)(2,1)} %fusion.1) | copy-start | bytes 4128772
  77.7 96.6 %all-gather.2.cloned.1.call-start = ((), (), s32[]{:S(2)}) async-start(), calls=%async_computation.4 | async-start | bytes 6881280 | tf_op jit(solution)/shard_map/all_gather | solution.py:115
  224.2 13.2 %all-to-all-start.1 = ((bf16[32,2,1536]{2,1,0:T(2,128)(2,1)}), bf16[32,2,1536]{2,1,0:T(2,128)(2,1)S(1)}, u32[]{:S(2)}, u32[]{:S(2)}) async-start(bf16[32,2,1536]{2,1,0:T(2,128)(2,1)} %reshape.68), calls=%async_computation.2 | async-start | bytes 393216 | tf_op jit(solution)/shard_map/all_to_all | solution.py:122
Sparse Core Ops, SparseCore 0:
  77.8 50.8 reduce-scatter.1
  132.3 41.9 all-gather.1

commit v5 on v4

--- a/solution.py
+++ b/solution.py
@@ -24,7 +24,7 @@
     )
 
 
-def _bwd_body(dg_ref, du_ref, ht_ref, xt_ref, y_ref, wg_ref, wu_ref,
+def _bwd_body(dg_ref, du_ref, h_ref, x_ref, y_ref, wg_ref, wu_ref,
               drows_ref, gg_ref, gu_ref, gd_ref):
     @pl.when(pl.program_id(0) == 0)
     def _():
@@ -32,29 +32,33 @@
     dg = dg_ref[...]
     du = du_ref[...]
     nt = (((1,), (1,)), ((), ()))
+    tn = (((0,), (0,)), ((), ()))
     drows_ref[...] += lax.dot_general(dg, wg_ref[...], nt, preferred_element_type=jnp.float32) + \
         lax.dot_general(du, wu_ref[...], nt, preferred_element_type=jnp.float32)
-    xt = xt_ref[...]
-    gg_ref[...] = jnp.dot(xt, dg, preferred_element_type=jnp.float32).astype(gg_ref.dtype)
-    gu_ref[...] = jnp.dot(xt, du, preferred_element_type=jnp.float32).astype(gu_ref.dtype)
-    gd_ref[...] = jnp.dot(ht_ref[...], y_ref[...], preferred_element_type=jnp.float32).astype(gd_ref.dtype)
+    x = x_ref[...]
+    gg_ref[...] = lax.dot_general(x, dg, tn, preferred_element_type=jnp.float32).astype(gg_ref.dtype)
+    gu_ref[...] = lax.dot_general(x, du, tn, preferred_element_type=jnp.float32).astype(gu_ref.dtype)
+    gd_ref[...] = lax.dot_general(h_ref[...], y_ref[...], tn, preferred_element_type=jnp.float32).astype(gd_ref.dtype)
 
-def fused_backward(d_gate, d_up, hidden, rows_in, rows_grad, w_gate, w_up):
-    rows, ff = d_gate.shape
+
+def fused_backward(gathered, rows_in, rows_grad, w_gate, w_up, interpret=False):
+    rows, ff = gathered.shape[1], gathered.shape[2]
     cols = rows_in.shape[1]
     tile = 512 if ff % 512 == 0 else ff
     steps = ff // tile
-    hidden_t = hidden.T
-    rows_in_t = rows_in.T
     bf = jnp.bfloat16
+
+    def plane(p):
+        return pl.BlockSpec((None, rows, tile), lambda k: (p, 0, k))
+
     return pl.pallas_call(
         _bwd_body,
         grid=(steps,),
         in_specs=[
-            pl.BlockSpec((rows, tile), lambda k: (0, k)),
-            pl.BlockSpec((rows, tile), lambda k: (0, k)),
-            pl.BlockSpec((tile, rows), lambda k: (k, 0)),
-            pl.BlockSpec((cols, rows), lambda k: (0, 0)),
+            plane(2),
+            plane(1),
+            plane(0),
+            pl.BlockSpec((rows, cols), lambda k: (0, 0)),
             pl.BlockSpec((rows, cols), lambda k: (0, 0)),
             pl.BlockSpec((cols, tile), lambda k: (0, k)),
             pl.BlockSpec((cols, tile), lambda k: (0, k)),
@@ -75,7 +79,8 @@
         cost_estimate=pl.CostEstimate(
             flops=2 * rows * ff * cols * 5, transcendentals=0,
             bytes_accessed=2 * (2 * cols * ff + 3 * cols * ff + 3 * rows * ff)),
-    )(d_gate, d_up, hidden_t, rows_in_t, rows_grad, w_gate, w_up)
+        interpret=interpret,
+    )(gathered, gathered, gathered, rows_in, rows_grad, w_gate, w_up)
 
 
 def on_device(inputs, grad_out, labels, w_gate, w_up, w_down):
@@ -113,10 +118,9 @@
     reduced = lax.psum_scatter(parts, "dp", scatter_dimension=2, tiled=True).astype(jnp.float32)
     hidden, d_up, d_gate = nonlinear(reduced[0], reduced[1], reduced[2])
     gathered = lax.all_gather(jnp.stack([hidden, d_up, d_gate]), "dp", axis=2, tiled=True)
-    hidden, d_up, d_gate = gathered[0], gathered[1], gathered[2]
 
     d_rows, grad_gate, grad_up, grad_down = fused_backward(
-        d_gate, d_up, hidden, rows_in, rows_grad, w_gate, w_up
+        gathered, rows_in, rows_grad, w_gate, w_up
     )
     back = d_rows.astype(jnp.bfloat16).reshape(replicas * members, capacity * columns)
     back = lax.all_to_all(back, ALL, 0, 0, tiled=True)

time: 248 us -> 210 us (0.85)
  waiting for transfers between devices: 101 us -> 84.5 us
  local copies, waits for them, and re-layouts: 20.2 us -> 7.88 us
  matrix products: 32.8 us -> 25.1 us
    reduce_scatter x1, waiting for transfers between devices: 50.9 us -> 41.7 us  [on_device(): lax.psum_scatter(parts, 'dp', scatter_dimension=2, tiled=True)]
    all_gather x1, waiting for transfers between devices: 41.2 us -> 34.3 us  [on_device(): lax.all_gather(jnp.stack([hidden, d_up, d_gate]), 'dp', axis=2, tiled=True)]
    squeeze x2 -> x0, local copies, waits for them, and re-layouts: 6.56 us -> none  [on_device(): hidden, d_up, d_gate = (gathered[0], gathered[1], gathered[2])]
    dot_general x1, matrix products: 12.5 us -> 7.61 us  [on_device(): up_part = jnp.dot(rows_in, w_up, preferred_element_type=jnp.float32)]
    transpose x1 -> x0, local copies, waits for them, and re-layouts: 4.79 us -> none  [fused_backward(): hidden_t = hidden.T]
    dot_general x1, matrix products: 11 us -> 7.68 us  [on_device(): gate_part = jnp.dot(rows_in, w_gate, preferred_element_type=jnp.float32)]
where the time goes in v5:
time: 210 us; the launch traced here: 209 us
  waiting for transfers between devices  84.5 us (40%)
  Pallas kernels  34.6 us (16%)
  matrix products  25.1 us (12%)
  blocking collectives  20.6 us (10%)
  other arithmetic  17.5 us (8%)
  between operations  14.3 us (7%)
  local copies, waits for them, and re-layouts  7.88 us (4%)
  starting transfers between devices  4.9 us (2%)
    reduce_scatter x1, waiting for transfers between devices, on_device(): lax.psum_scatter(parts, 'dp', scatter_dimension=2, tiled=True)  41.7 us
    pallas_call x1, Pallas kernels, fused_backward(): pl.pallas_call(_bwd_body, grid=(steps,), in_specs=[plane(2), plane(1), pl...  34.6 us
    all_gather x1, waiting for transfers between devices, on_device(): lax.all_gather(jnp.stack([hidden, d_up, d_gate]), 'dp', axis=2, tiled=True)  34.3 us
    all_to_all x1, blocking collectives, on_device(): recv = lax.all_to_all(send, ALL, 0, 0, tiled=True)  20.6 us
    dot_general x1, matrix products, on_device(): lax.dot_general(rows_grad, w_down, (((1,), (1,)), ((), ())), preferred_el...  9.81 us
    all_to_all x1, waiting for transfers between devices, on_device(): back = lax.all_to_all(back, ALL, 0, 0, tiled=True)  8.53 us
    dot_general x1, matrix products, on_device(): gate_part = jnp.dot(rows_in, w_gate, preferred_element_type=jnp.float32)  7.68 us
    dot_general x1, matrix products, on_device(): up_part = jnp.dot(rows_in, w_up, preferred_element_type=jnp.float32)  7.61 us
  transfers between devices with their start and end apart: 3, of which 3 were waited for; matrix products, arithmetic and copies ran while one was open for 0% of the time, Pallas kernels for 0%

profile of v5, /device:TPU:0, one launch (start us, length us, event | category | flops | bytes accessed | tf_op | source)
XLA Modules:
  0.0 209.4 jit_solution(10696274662862702696)
XLA Ops:
  7.2 0.0 reduce-scatter.2.cloned.1.call-start
  7.2 0.7 fusion.4
  8.0 0.8 select_reduce_fusion
  8.8 0.7 fusion.5
  9.5 1.0 maximum_bitcast_fusion
  10.5 0.3 copy.20
  10.8 0.3 broadcast_in_dim.2
  11.1 1.1 scatter_fusion
  12.2 0.2 reshape.38
  12.4 0.3 copy.27
  12.8 0.5 all_to_all.16
  13.3 0.5 broadcast.47
  13.8 2.9 %reduce.3 = bf16[32,6144]{1,0:T(8,128)(2,1)S(1)} reduce(bf16[32,1,6144]{2,1,0:T(2,128)(2,1)S(1)} %all_to_all.16, bf16[]{:T(256)} %broadcast.47), dimensions={1}, to_apply=%all_to_all.16.reduce_sub_computation | reduce | bytes 786434 | tf_op jit(solution)/shard_map/all_to_all | solution.py:107
  16.8 0.3 reshape.66
  17.0 20.6 %all_to_all.20 = bf16[32,2,3072]{2,1,0:T(2,128)(2,1)S(1)} all-to-all(bf16[32,2,3072]{2,1,0:T(2,128)(2,1)S(1)} %reshape.66), channel_id=1, replica_groups=mesh['dp'=4,'expert'=8] {'dp','expert'}, dimensions={0} | all-to-all | bytes 786432 | tf_op jit(solution)/shard_map/all_to_all | solution.py:107
  37.7 0.3 reshape.67
  38.0 2.3 %reduce = bf16[32,6144]{1,0:T(8,128)(2,1)S(1)} reduce(bf16[32,1,6144]{2,1,0:T(2,128)(2,1)S(1)} %reshape.67, bf16[]{:T(256)} %constant.19), dimensions={1}, to_apply=%all_to_all.13.reduce_sub_computation | reduce | bytes 786434 | tf_op jit(solution)/shard_map/all_to_all | solution.py:107
  40.3 0.6 reshape.39
  40.9 0.2 fusion.6
  41.1 0.2 reshape_squeeze.6.x_ref
  41.3 7.7 %fusion = bf16[1,96,7168]{2,1,0:T(8,128)(2,1)S(1)} fusion(bf16[96,1024]{1,0:T(8,128)(2,1)S(1)} %reshape_squeeze.6.x_ref, bf16[1024,7168]{1,0:T(8,128)(2,1)} %wg_ref.1), kind=kOutput, calls=%fused_computation.5 | convolution fusion | flops 1409974272 | bytes 16252928 | tf_op jit(solution)/shard_map/dot_general | solution.py:112
  48.9 0.0 copy-done
  49.0 7.6 %fusion.1 = bf16[1,96,7168]{2,1,0:T(8,128)(2,1)S(1)} fusion(bf16[96,1024]{1,0:T(8,128)(2,1)S(1)} %reshape_squeeze.6.x_ref, bf16[1024,7168]{1,0:T(8,128)(2,1)} %wu_ref.1), kind=kOutput, calls=%fused_computation.6 | convolution fusion | flops 1409974272 | bytes 16252928 | tf_op jit(solution)/shard_map/dot_general | solution.py:113
  56.6 0.2 reshape_squeeze.7.y_ref
  56.7 0.0 copy-start.1
  56.8 9.8 %fusion.2 = bf16[1,96,7168]{2,1,0:T(8,128)(2,1)S(1)} fusion(bf16[96,1024]{1,0:T(8,128)(2,1)S(1)} %reshape_squeeze.7.y_ref, bf16[7168,1024]{1,0:T(8,128)(2,1)} %param.11), kind=kOutput, calls=%fused_computation.7 | convolution fusion | flops 1409974272 | bytes 16252928 | tf_op jit(solution)/shard_map/dot_general | solution.py:114
  66.6 2.2 %pad_maximum_fusion = bf16[3,96,7168]{2,1,0:T(8,128)(2,1)} fusion(bf16[1,96,7168]{2,1,0:T(8,128)(2,1)S(1)} %fusion.2, bf16[1,96,7168]{2,1,0:T(8,128)(2,1)S(1)} %fusion.1, bf16[1,96,7168]{2,1,0:T(8,128)(2,1)S(1)} %fusion), kind=kLoop, calls=%fused_computation.8 | loop fusion | flops 4128768 | bytes 8257536 | tf_op jit(solution)/shard_map/stack | solution.py:117
  68.8 0.0 reduce-scatter.2.cloned.1.call-update
  68.8 0.3 all-gather.2.cloned.1.call-start
  69.1 41.7 %reduce-scatter.2.cloned.1.call-done = bf16[3,96,1792]{2,1,0:T(8,128)(2,1)} async-done(((bf16[3,96,7168]{2,1,0:T(8,128)(2,1)}), bf16[3,96,1792]{2,1,0:T(8,128)(2,1)}) %reduce-scatter.2.cloned.1.call-update) | async-done | bytes 1032208 | tf_op jit(solution)/shard_map/reduce_scatter | solution.py:118
  110.8 1.4 convert_element_type.33
  112.2 0.4 multiply_convert_fusion.2
  112.5 1.1 pad_maximum_fusion.1
  113.6 0.0 all-gather.2.cloned.1.call-update
  113.6 34.3 %all-gather.2.cloned.1.call-done.dg_ref.du_ref.h_ref = bf16[3,96,7168]{2,1,0:T(8,128)(2,1)} async-done(((bf16[3,96,1792]{2,1,0:T(8,128)(2,1)}), bf16[3,96,7168]{2,1,0:T(8,128)(2,1)}) %all-gather.2.cloned.1.call-update) | async-done | bytes 4128784 | tf_op jit(solution)/shard_map/all_gather | solution.py:120
  147.9 34.6 %shard_map.93 = (f32[96,1024]{1,0:T(8,128)}, bf16[1024,7168]{1,0:T(8,128)(2,1)}, bf16[1024,7168]{1,0:T(8,128)(2,1)}, bf16[7168,1024]{1,0:T(8,128)(2,1)}) custom-call(bf16[3,96,7168]{2,1,0:T(8,128)(2,1)} %all-gather.2.cloned.1.call-done.dg_ref.du_ref.h_ref, bf16[3,96,7168]{2,1,0:T(8,128)(2,1)} %all-gather.2.cloned.1.call-done.dg_ref.du_ref.h_ref, ...), custom_call_target="tpu_custom_call" | custom-call | flops 7046430720 | bytes 77529088 | tf_op jit(solution)/shard_map/pallas_call | solution.py:54
  182.5 1.0 convert_element_type.37
  183.6 0.1 all_to_all.17
  183.7 1.8 reduce.4
  185.5 0.8 reshape.68
  186.3 4.6 %all-to-all-start.1 = ((bf16[32,2,1536]{2,1,0:T(2,128)(2,1)}), bf16[32,2,1536]{2,1,0:T(2,128)(2,1)S(1)}, u32[]{:S(2)}, u32[]{:S(2)}) async-start(bf16[32,2,1536]{2,1,0:T(2,128)(2,1)} %reshape.68), calls=%async_computation.2 | async-start | bytes 393216 | tf_op jit(solution)/shard_map/all_to_all | solution.py:126
  190.9 8.5 %all-to-all-done.1 = bf16[32,2,1536]{2,1,0:T(2,128)(2,1)S(1)} async-done(((bf16[32,2,1536]{2,1,0:T(2,128)(2,1)}), bf16[32,2,1536]{2,1,0:T(2,128)(2,1)S(1)}, u32[]{:S(2)}, u32[]{:S(2)}) %all-to-all-start.1) | async-done | bytes 196640 | tf_op jit(solution)/shard_map/all_to_all | solution.py:126
  199.5 0.1 reshape.69
  199.6 1.1 convert_reduce_fusion
  200.7 0.3 reshape.46
  201.0 0.2 copy.24
  201.2 0.1 copy.25
  201.3 1.3 gather_fusion
  (4 shorter events, 0.0 us)
Async XLA Ops:
  7.2 103.6 %reduce-scatter.2.cloned.1.call-start = ((), (), s32[]{:S(2)}) async-start(), calls=%async_computation.3 | async-start | bytes 5160960 | tf_op jit(solution)/shard_map/reduce_scatter | solution.py:118
  41.3 7.7 %copy-start = (bf16[96,1024]{1,0:T(8,128)(2,1)}, bf16[96,1024]{1,0:T(8,128)(2,1)S(1)}, u32[]{:S(2)}) copy-start(bf16[96,1024]{1,0:T(8,128)(2,1)S(1)} %reshape_squeeze.6.x_ref) | copy-start | bytes 589828
  56.7 9.8 %copy-start.1 = (bf16[96,1024]{1,0:T(8,128)(2,1)}, bf16[96,1024]{1,0:T(8,128)(2,1)S(1)}, u32[]{:S(2)}) copy-start(bf16[96,1024]{1,0:T(8,128)(2,1)S(1)} %reshape_squeeze.7.y_ref) | copy-start | bytes 589828
  68.8 79.1 %all-gather.2.cloned.1.call-start = ((), (), s32[]{:S(2)}) async-start(), calls=%async_computation.4 | async-start | bytes 5160960 | tf_op jit(solution)/shard_map/all_gather | solution.py:120
  186.3 13.2 %all-to-all-start.1 = ((bf16[32,2,1536]{2,1,0:T(2,128)(2,1)}), bf16[32,2,1536]{2,1,0:T(2,128)(2,1)S(1)}, u32[]{:S(2)}, u32[]{:S(2)}) async-start(bf16[32,2,1536]{2,1,0:T(2,128)(2,1)} %reshape.68), calls=%async_computation.2 | async-start | bytes 393216 | tf_op jit(solution)/shard_map/all_to_all | solution.py:126
Sparse Core Ops, SparseCore 0:
  69.0 41.7 reduce-scatter.1
  113.7 34.1 all-gather.1

commit v6 on v5

--- a/solution.py
+++ b/solution.py
@@ -24,63 +24,84 @@
     )
 
 
-def _bwd_body(dg_ref, du_ref, h_ref, x_ref, y_ref, wg_ref, wu_ref,
-              drows_ref, gg_ref, gu_ref, gd_ref):
+def _rows_body(dg_ref, du_ref, wg_ref, wu_ref, drows_ref):
     @pl.when(pl.program_id(0) == 0)
     def _():
         drows_ref[...] = jnp.zeros_like(drows_ref)
-    dg = dg_ref[...]
-    du = du_ref[...]
     nt = (((1,), (1,)), ((), ()))
+    drows_ref[...] += lax.dot_general(
+        dg_ref[...], wg_ref[...], nt, preferred_element_type=jnp.float32
+    ) + lax.dot_general(du_ref[...], wu_ref[...], nt, preferred_element_type=jnp.float32)
+
+
+def _grads_body(dg_ref, du_ref, h_ref, x_ref, y_ref, gg_ref, gu_ref, gd_ref):
     tn = (((0,), (0,)), ((), ()))
-    drows_ref[...] += lax.dot_general(dg, wg_ref[...], nt, preferred_element_type=jnp.float32) + \
-        lax.dot_general(du, wu_ref[...], nt, preferred_element_type=jnp.float32)
     x = x_ref[...]
-    gg_ref[...] = lax.dot_general(x, dg, tn, preferred_element_type=jnp.float32).astype(gg_ref.dtype)
-    gu_ref[...] = lax.dot_general(x, du, tn, preferred_element_type=jnp.float32).astype(gu_ref.dtype)
+    gg_ref[...] = lax.dot_general(x, dg_ref[...], tn, preferred_element_type=jnp.float32).astype(gg_ref.dtype)
+    gu_ref[...] = lax.dot_general(x, du_ref[...], tn, preferred_element_type=jnp.float32).astype(gu_ref.dtype)
     gd_ref[...] = lax.dot_general(h_ref[...], y_ref[...], tn, preferred_element_type=jnp.float32).astype(gd_ref.dtype)
 
 
-def fused_backward(gathered, rows_in, rows_grad, w_gate, w_up, interpret=False):
+def backward_rows(gathered, w_gate, w_up):
+    rows, ff = gathered.shape[1], gathered.shape[2]
+    cols = w_gate.shape[0]
+    tile = 512 if ff % 512 == 0 else ff
+
+    def plane(p):
+        return pl.BlockSpec((None, rows, tile), lambda k: (p, 0, k))
+
+    return pl.pallas_call(
+        _rows_body,
+        grid=(ff // tile,),
+        in_specs=[
+            plane(2),
+            plane(1),
+            pl.BlockSpec((cols, tile), lambda k: (0, k)),
+            pl.BlockSpec((cols, tile), lambda k: (0, k)),
+        ],
+        out_specs=pl.BlockSpec((rows, cols), lambda k: (0, 0)),
+        out_shape=jax.ShapeDtypeStruct((rows, cols), jnp.float32),
+        compiler_params=pltpu.CompilerParams(dimension_semantics=("arbitrary",)),
+        cost_estimate=pl.CostEstimate(
+            flops=4 * rows * ff * cols, transcendentals=0,
+            bytes_accessed=2 * (2 * cols * ff + 2 * rows * ff) + 4 * rows * cols),
+    )(gathered, gathered, w_gate, w_up)
+
+
+def backward_grads(gathered, rows_in, rows_grad):
     rows, ff = gathered.shape[1], gathered.shape[2]
     cols = rows_in.shape[1]
     tile = 512 if ff % 512 == 0 else ff
-    steps = ff // tile
     bf = jnp.bfloat16
 
     def plane(p):
         return pl.BlockSpec((None, rows, tile), lambda k: (p, 0, k))
 
     return pl.pallas_call(
-        _bwd_body,
-        grid=(steps,),
+        _grads_body,
+        grid=(ff // tile,),
         in_specs=[
             plane(2),
             plane(1),
             plane(0),
             pl.BlockSpec((rows, cols), lambda k: (0, 0)),
             pl.BlockSpec((rows, cols), lambda k: (0, 0)),
-            pl.BlockSpec((cols, tile), lambda k: (0, k)),
-            pl.BlockSpec((cols, tile), lambda k: (0, k)),
         ],
         out_specs=[
-            pl.BlockSpec((rows, cols), lambda k: (0, 0)),
             pl.BlockSpec((cols, tile), lambda k: (0, k)),
             pl.BlockSpec((cols, tile), lambda k: (0, k)),
             pl.BlockSpec((tile, cols), lambda k: (k, 0)),
         ],
         out_shape=[
-            jax.ShapeDtypeStruct((rows, cols), jnp.float32),
             jax.ShapeDtypeStruct((cols, ff), bf),
             jax.ShapeDtypeStruct((cols, ff), bf),
             jax.ShapeDtypeStruct((ff, cols), bf),
         ],
-        compiler_params=pltpu.CompilerParams(dimension_semantics=("arbitrary",)),
+        compiler_params=pltpu.CompilerParams(dimension_semantics=("parallel",)),
         cost_estimate=pl.CostEstimate(
-            flops=2 * rows * ff * cols * 5, transcendentals=0,
-            bytes_accessed=2 * (2 * cols * ff + 3 * cols * ff + 3 * rows * ff)),
-        interpret=interpret,
-    )(gathered, gathered, gathered, rows_in, rows_grad, w_gate, w_up)
+            flops=6 * rows * ff * cols, transcendentals=0,
+            bytes_accessed=2 * (3 * cols * ff + 3 * rows * ff + 2 * rows * cols)),
+    )(gathered, gathered, gathered, rows_in, rows_grad)
 
 
 def on_device(inputs, grad_out, labels, w_gate, w_up, w_down):
@@ -119,15 +140,14 @@
     hidden, d_up, d_gate = nonlinear(reduced[0], reduced[1], reduced[2])
     gathered = lax.all_gather(jnp.stack([hidden, d_up, d_gate]), "dp", axis=2, tiled=True)
 
-    d_rows, grad_gate, grad_up, grad_down = fused_backward(
-        gathered, rows_in, rows_grad, w_gate, w_up
-    )
+    d_rows = backward_rows(gathered, w_gate, w_up)
     back = d_rows.astype(jnp.bfloat16).reshape(replicas * members, capacity * columns)
     back = lax.all_to_all(back, ALL, 0, 0, tiled=True)
     back = back.reshape(replicas, EXPERTS, group, capacity, columns).astype(jnp.float32)
     summed = jnp.sum(back, axis=2)
     summed = jnp.transpose(summed, (1, 2, 0, 3)).reshape(EXPERTS * capacity, width)
     grad_in = summed[slot_ids].astype(jnp.bfloat16)
+    grad_gate, grad_up, grad_down = backward_grads(gathered, rows_in, rows_grad)
     return (grad_in, grad_gate, grad_up, grad_down)
 
 

time: 210 us -> 205 us (0.976)
  waiting for transfers between devices: 84.5 us -> 76 us
  Pallas kernels: 34.6 us -> 37.8 us
    all_to_all x1, waiting for transfers between devices: 8.53 us -> 0.01 us  [on_device(): back = lax.all_to_all(back, ALL, 0, 0, tiled=True)]
    pallas_call x1 -> x2, Pallas kernels: 34.6 us -> 37.8 us  [the longest x1 19.2 us: backward_rows(): pl.pallas_call(_rows_body, grid=(ff // tile,), in_specs=[plane(2), plane(...]
  transfers between devices with their start and end apart: 3 -> 3, of which waited for: 3 -> 2; matrix products, arithmetic and copies ran while one was open for 0% -> 0% of each run, Pallas kernels for 0% -> 9%
where the time goes in v6:
time: 205 us; the launch traced here: 204 us
  waiting for transfers between devices  76 us (37%)
  Pallas kernels  37.8 us (18%)
  matrix products  25.1 us (12%)
  blocking collectives  20.6 us (10%)
  other arithmetic  17.5 us (9%)
  between operations  14.3 us (7%)
  local copies, waits for them, and re-layouts  7.88 us (4%)
  starting transfers between devices  4.9 us (2%)
    reduce_scatter x1, waiting for transfers between devices, on_device(): lax.psum_scatter(parts, 'dp', scatter_dimension=2, tiled=True)  41.7 us
    all_gather x1, waiting for transfers between devices, on_device(): lax.all_gather(jnp.stack([hidden, d_up, d_gate]), 'dp', axis=2, tiled=True)  34.3 us
    all_to_all x1, blocking collectives, on_device(): recv = lax.all_to_all(send, ALL, 0, 0, tiled=True)  20.6 us
    pallas_call x1, Pallas kernels, backward_rows(): pl.pallas_call(_rows_body, grid=(ff // tile,), in_specs=[plane(2), plane(...  19.2 us
    pallas_call x1, Pallas kernels, backward_grads(): pl.pallas_call(_grads_body, grid=(ff // tile,), in_specs=[plane(2), plane...  18.6 us
    dot_general x1, matrix products, on_device(): lax.dot_general(rows_grad, w_down, (((1,), (1,)), ((), ())), preferred_el...  9.81 us
    dot_general x1, matrix products, on_device(): gate_part = jnp.dot(rows_in, w_gate, preferred_element_type=jnp.float32)  7.68 us
    dot_general x1, matrix products, on_device(): up_part = jnp.dot(rows_in, w_up, preferred_element_type=jnp.float32)  7.61 us
  transfers between devices with their start and end apart: 3, of which 2 were waited for; matrix products, arithmetic and copies ran while one was open for 0% of the time, Pallas kernels for 9%

profile of v6, /device:TPU:0, one launch (start us, length us, event | category | flops | bytes accessed | tf_op | source)
XLA Modules:
  0.0 204.0 jit_solution(14621605446630326458)
XLA Ops:
  7.2 0.0 reduce-scatter.2.cloned.1.call-start
  7.2 0.7 fusion.4
  8.0 0.8 select_reduce_fusion
  8.8 0.7 fusion.5
  9.5 1.0 maximum_bitcast_fusion
  10.5 0.3 copy.20
  10.8 0.3 broadcast_in_dim.2
  11.1 1.1 scatter_fusion
  12.2 0.2 reshape.38
  12.4 0.3 copy.27
  12.8 0.5 all_to_all.16
  13.3 0.5 broadcast.47
  13.8 2.9 %reduce.3 = bf16[32,6144]{1,0:T(8,128)(2,1)S(1)} reduce(bf16[32,1,6144]{2,1,0:T(2,128)(2,1)S(1)} %all_to_all.16, bf16[]{:T(256)} %broadcast.47), dimensions={1}, to_apply=%all_to_all.16.reduce_sub_computation | reduce | bytes 786434 | tf_op jit(solution)/shard_map/all_to_all | solution.py:128
  16.8 0.3 reshape.66
  17.0 20.6 %all_to_all.20 = bf16[32,2,3072]{2,1,0:T(2,128)(2,1)S(1)} all-to-all(bf16[32,2,3072]{2,1,0:T(2,128)(2,1)S(1)} %reshape.66), channel_id=1, replica_groups=mesh['dp'=4,'expert'=8] {'dp','expert'}, dimensions={0} | all-to-all | bytes 786432 | tf_op jit(solution)/shard_map/all_to_all | solution.py:128
  37.7 0.3 reshape.67
  38.0 2.3 %reduce = bf16[32,6144]{1,0:T(8,128)(2,1)S(1)} reduce(bf16[32,1,6144]{2,1,0:T(2,128)(2,1)S(1)} %reshape.67, bf16[]{:T(256)} %constant.19), dimensions={1}, to_apply=%all_to_all.13.reduce_sub_computation | reduce | bytes 786434 | tf_op jit(solution)/shard_map/all_to_all | solution.py:128
  40.3 0.6 reshape.39
  40.9 0.2 fusion.6
  41.1 0.2 reshape_squeeze.6.x_ref
  41.3 7.7 %fusion = bf16[1,96,7168]{2,1,0:T(8,128)(2,1)S(1)} fusion(bf16[96,1024]{1,0:T(8,128)(2,1)S(1)} %reshape_squeeze.6.x_ref, bf16[1024,7168]{1,0:T(8,128)(2,1)} %wg_ref.1), kind=kOutput, calls=%fused_computation.5 | convolution fusion | flops 1409974272 | bytes 16252928 | tf_op jit(solution)/shard_map/dot_general | solution.py:133
  49.0 7.6 %fusion.1 = bf16[1,96,7168]{2,1,0:T(8,128)(2,1)S(1)} fusion(bf16[96,1024]{1,0:T(8,128)(2,1)S(1)} %reshape_squeeze.6.x_ref, bf16[1024,7168]{1,0:T(8,128)(2,1)} %wu_ref.1), kind=kOutput, calls=%fused_computation.6 | convolution fusion | flops 1409974272 | bytes 16252928 | tf_op jit(solution)/shard_map/dot_general | solution.py:134
  56.6 0.2 reshape_squeeze.7.y_ref
  56.7 0.0 copy-start.1
  56.8 9.8 %fusion.2 = bf16[1,96,7168]{2,1,0:T(8,128)(2,1)S(1)} fusion(bf16[96,1024]{1,0:T(8,128)(2,1)S(1)} %reshape_squeeze.7.y_ref, bf16[7168,1024]{1,0:T(8,128)(2,1)} %param.11), kind=kOutput, calls=%fused_computation.7 | convolution fusion | flops 1409974272 | bytes 16252928 | tf_op jit(solution)/shard_map/dot_general | solution.py:135
  66.6 2.2 %pad_maximum_fusion = bf16[3,96,7168]{2,1,0:T(8,128)(2,1)} fusion(bf16[1,96,7168]{2,1,0:T(8,128)(2,1)S(1)} %fusion.2, bf16[1,96,7168]{2,1,0:T(8,128)(2,1)S(1)} %fusion.1, bf16[1,96,7168]{2,1,0:T(8,128)(2,1)S(1)} %fusion), kind=kLoop, calls=%fused_computation.8 | loop fusion | flops 4128768 | bytes 8257536 | tf_op jit(solution)/shard_map/stack | solution.py:138
  68.8 0.0 reduce-scatter.2.cloned.1.call-update
  68.8 0.3 all-gather.2.cloned.1.call-start
  69.1 41.7 %reduce-scatter.2.cloned.1.call-done = bf16[3,96,1792]{2,1,0:T(8,128)(2,1)} async-done(((bf16[3,96,7168]{2,1,0:T(8,128)(2,1)}), bf16[3,96,1792]{2,1,0:T(8,128)(2,1)}) %reduce-scatter.2.cloned.1.call-update) | async-done | bytes 1032208 | tf_op jit(solution)/shard_map/reduce_scatter | solution.py:139
  110.8 1.4 convert_element_type.33
  112.2 0.4 multiply_convert_fusion.2
  112.5 1.1 pad_maximum_fusion.1
  113.6 0.0 all-gather.2.cloned.1.call-update
  113.6 34.3 %all-gather.2.cloned.1.call-done.dg_ref.du_ref.h_ref = bf16[3,96,7168]{2,1,0:T(8,128)(2,1)} async-done(((bf16[3,96,1792]{2,1,0:T(8,128)(2,1)}), bf16[3,96,7168]{2,1,0:T(8,128)(2,1)}) %all-gather.2.cloned.1.call-update) | async-done | bytes 4128784 | tf_op jit(solution)/shard_map/all_gather | solution.py:141
  147.9 19.2 %shard_map.93 = f32[96,1024]{1,0:T(8,128)} custom-call(bf16[3,96,7168]{2,1,0:T(8,128)(2,1)} %all-gather.2.cloned.1.call-done.dg_ref.du_ref.h_ref, bf16[3,96,7168]{2,1,0:T(8,128)(2,1)} %all-gather.2.cloned.1.call-done.dg_ref.du_ref.h_ref, bf16[1024,7168]{1,0:T(8,128)(2,1)} %wg_ref.1, bf16[1024,7168]{1,0:T(8,128)(2,1)} %wu_ref.1), custom_call_target="tpu_custom_call" | custom-call | flops 2818572288 | bytes 32505856 | tf_op jit(solution)/shard_map/pallas_call | solution.py:53
  167.1 1.0 convert_element_type.37
  168.1 0.1 all_to_all.17
  168.2 1.8 reduce.4
  170.0 0.8 reshape.68
  170.8 4.6 %all-to-all-start.1 = ((bf16[32,2,1536]{2,1,0:T(2,128)(2,1)}), bf16[32,2,1536]{2,1,0:T(2,128)(2,1)S(1)}, u32[]{:S(2)}, u32[]{:S(2)}) async-start(bf16[32,2,1536]{2,1,0:T(2,128)(2,1)} %reshape.68), calls=%async_computation.2 | async-start | bytes 393216 | tf_op jit(solution)/shard_map/all_to_all | solution.py:145
  175.4 18.6 %shard_map.94 = (bf16[1024,7168]{1,0:T(8,128)(2,1)}, bf16[1024,7168]{1,0:T(8,128)(2,1)}, bf16[7168,1024]{1,0:T(8,128)(2,1)}) custom-call(bf16[3,96,7168]{2,1,0:T(8,128)(2,1)} %all-gather.2.cloned.1.call-done.dg_ref.du_ref.h_ref, bf16[3,96,7168]{2,1,0:T(8,128)(2,1)} %all-gather.2.cloned.1.call-done.dg_ref.du_ref.h_ref, ...), custom_call_target="tpu_custom_call" | custom-call | flops 4227858432 | bytes 48562176 | tf_op jit(solution)/shard_map/pallas_call | solution.py:80
  194.0 0.0 all-to-all-done.1
  194.0 0.1 reshape.69
  194.2 1.1 convert_reduce_fusion
  195.3 0.3 reshape.46
  195.6 0.2 copy.24
  195.8 0.1 copy.25
  195.9 1.3 gather_fusion
  (5 shorter events, 0.0 us)
Async XLA Ops:
  7.2 103.6 %reduce-scatter.2.cloned.1.call-start = ((), (), s32[]{:S(2)}) async-start(), calls=%async_computation.3 | async-start | bytes 5160960 | tf_op jit(solution)/shard_map/reduce_scatter | solution.py:139
  41.3 7.7 %copy-start = (bf16[96,1024]{1,0:T(8,128)(2,1)}, bf16[96,1024]{1,0:T(8,128)(2,1)S(1)}, u32[]{:S(2)}) copy-start(bf16[96,1024]{1,0:T(8,128)(2,1)S(1)} %reshape_squeeze.6.x_ref) | copy-start | bytes 589828
  56.7 9.8 %copy-start.1 = (bf16[96,1024]{1,0:T(8,128)(2,1)}, bf16[96,1024]{1,0:T(8,128)(2,1)S(1)}, u32[]{:S(2)}) copy-start(bf16[96,1024]{1,0:T(8,128)(2,1)S(1)} %reshape_squeeze.7.y_ref) | copy-start | bytes 589828
  68.8 79.1 %all-gather.2.cloned.1.call-start = ((), (), s32[]{:S(2)}) async-start(), calls=%async_computation.4 | async-start | bytes 5160960 | tf_op jit(solution)/shard_map/all_gather | solution.py:141
  170.8 23.2 %all-to-all-start.1 = ((bf16[32,2,1536]{2,1,0:T(2,128)(2,1)}), bf16[32,2,1536]{2,1,0:T(2,128)(2,1)S(1)}, u32[]{:S(2)}, u32[]{:S(2)}) async-start(bf16[32,2,1536]{2,1,0:T(2,128)(2,1)} %reshape.68), calls=%async_computation.2 | async-start | bytes 393216 | tf_op jit(solution)/shard_map/all_to_all | solution.py:145
Sparse Core Ops, SparseCore 0:
  69.0 41.7 reduce-scatter.1
  113.7 34.1 all-gather.1

commit v7 on v6

--- a/solution.py
+++ b/solution.py
@@ -30,8 +30,8 @@
         drows_ref[...] = jnp.zeros_like(drows_ref)
     nt = (((1,), (1,)), ((), ()))
     drows_ref[...] += lax.dot_general(
-        dg_ref[...], wg_ref[...], nt, preferred_element_type=jnp.float32
-    ) + lax.dot_general(du_ref[...], wu_ref[...], nt, preferred_element_type=jnp.float32)
+        wg_ref[...], dg_ref[...], nt, preferred_element_type=jnp.float32
+    ) + lax.dot_general(wu_ref[...], du_ref[...], nt, preferred_element_type=jnp.float32)
 
 
 def _grads_body(dg_ref, du_ref, h_ref, x_ref, y_ref, gg_ref, gu_ref, gd_ref):
@@ -59,8 +59,8 @@
             pl.BlockSpec((cols, tile), lambda k: (0, k)),
             pl.BlockSpec((cols, tile), lambda k: (0, k)),
         ],
-        out_specs=pl.BlockSpec((rows, cols), lambda k: (0, 0)),
-        out_shape=jax.ShapeDtypeStruct((rows, cols), jnp.float32),
+        out_specs=pl.BlockSpec((cols, rows), lambda k: (0, 0)),
+        out_shape=jax.ShapeDtypeStruct((cols, rows), jnp.float32),
         compiler_params=pltpu.CompilerParams(dimension_semantics=("arbitrary",)),
         cost_estimate=pl.CostEstimate(
             flops=4 * rows * ff * cols, transcendentals=0,
@@ -140,7 +140,7 @@
     hidden, d_up, d_gate = nonlinear(reduced[0], reduced[1], reduced[2])
     gathered = lax.all_gather(jnp.stack([hidden, d_up, d_gate]), "dp", axis=2, tiled=True)
 
-    d_rows = backward_rows(gathered, w_gate, w_up)
+    d_rows = backward_rows(gathered, w_gate, w_up).T
     back = d_rows.astype(jnp.bfloat16).reshape(replicas * members, capacity * columns)
     back = lax.all_to_all(back, ALL, 0, 0, tiled=True)
     back = back.reshape(replicas, EXPERTS, group, capacity, columns).astype(jnp.float32)

time: 205 us -> 205 us (level)
  no operation moved by 1% of the time
where the time goes in v7:
time: 205 us; the launch traced here: 204 us
  waiting for transfers between devices  75.9 us (37%)
  Pallas kernels  37.4 us (18%)
  matrix products  25 us (12%)
  blocking collectives  20.6 us (10%)
  other arithmetic  17.5 us (9%)
  between operations  14.3 us (7%)
  local copies, waits for them, and re-layouts  8.02 us (4%)
  starting transfers between devices  4.9 us (2%)
    reduce_scatter x1, waiting for transfers between devices, on_device(): lax.psum_scatter(parts, 'dp', scatter_dimension=2, tiled=True)  41.7 us
    all_gather x1, waiting for transfers between devices, on_device(): lax.all_gather(jnp.stack([hidden, d_up, d_gate]), 'dp', axis=2, tiled=True)  34.2 us
    all_to_all x1, blocking collectives, on_device(): recv = lax.all_to_all(send, ALL, 0, 0, tiled=True)  20.6 us
    pallas_call x1, Pallas kernels, backward_rows(): pl.pallas_call(_rows_body, grid=(ff // tile,), in_specs=[plane(2), plane(...  18.7 us
    pallas_call x1, Pallas kernels, backward_grads(): pl.pallas_call(_grads_body, grid=(ff // tile,), in_specs=[plane(2), plane...  18.6 us
    dot_general x1, matrix products, on_device(): lax.dot_general(rows_grad, w_down, (((1,), (1,)), ((), ())), preferred_el...  9.74 us
    dot_general x1, matrix products, on_device(): up_part = jnp.dot(rows_in, w_up, preferred_element_type=jnp.float32)  7.68 us
    dot_general x1, matrix products, on_device(): gate_part = jnp.dot(rows_in, w_gate, preferred_element_type=jnp.float32)  7.61 us
  transfers between devices with their start and end apart: 3, of which 2 were waited for; matrix products, arithmetic and copies ran while one was open for 0% of the time, Pallas kernels for 9%

profile of v7, /device:TPU:0, one launch (start us, length us, event | category | flops | bytes accessed | tf_op | source)
XLA Modules:
  0.0 203.7 jit_solution(7182711131641586632)
XLA Ops:
  7.2 0.0 reduce-scatter.2.cloned.1.call-start
  7.2 0.7 fusion.4
  8.0 0.8 select_reduce_fusion
  8.8 0.7 fusion.5
  9.5 1.0 maximum_bitcast_fusion
  10.5 0.3 copy.15
  10.8 0.3 broadcast_in_dim.2
  11.1 1.1 scatter_fusion
  12.2 0.2 reshape.38
  12.4 0.3 copy.23
  12.8 0.5 all_to_all.16
  13.3 0.5 broadcast.47
  13.8 2.9 %reduce.3 = bf16[32,6144]{1,0:T(8,128)(2,1)S(1)} reduce(bf16[32,1,6144]{2,1,0:T(2,128)(2,1)S(1)} %all_to_all.16, bf16[]{:T(256)} %broadcast.47), dimensions={1}, to_apply=%all_to_all.16.reduce_sub_computation | reduce | bytes 786434 | tf_op jit(solution)/shard_map/all_to_all | solution.py:128
  16.8 0.3 reshape.66
  17.0 20.6 %all_to_all.20 = bf16[32,2,3072]{2,1,0:T(2,128)(2,1)S(1)} all-to-all(bf16[32,2,3072]{2,1,0:T(2,128)(2,1)S(1)} %reshape.66), channel_id=1, replica_groups=mesh['dp'=4,'expert'=8] {'dp','expert'}, dimensions={0} | all-to-all | bytes 786432 | tf_op jit(solution)/shard_map/all_to_all | solution.py:128
  37.7 0.3 reshape.67
  38.0 2.3 %reduce = bf16[32,6144]{1,0:T(8,128)(2,1)S(1)} reduce(bf16[32,1,6144]{2,1,0:T(2,128)(2,1)S(1)} %reshape.67, bf16[]{:T(256)} %constant.19), dimensions={1}, to_apply=%all_to_all.13.reduce_sub_computation | reduce | bytes 786434 | tf_op jit(solution)/shard_map/all_to_all | solution.py:128
  40.3 0.6 reshape.39
  40.9 0.2 fusion.6
  41.1 0.2 reshape_squeeze.6.x_ref
  41.3 0.2 reshape_squeeze.7.y_ref
  41.4 7.7 %fusion.1 = bf16[1,96,7168]{2,1,0:T(8,128)(2,1)S(1)} fusion(bf16[96,1024]{1,0:T(8,128)(2,1)S(1)} %reshape_squeeze.6.x_ref, bf16[1024,7168]{1,0:T(8,128)(2,1)} %wu_ref.1), kind=kOutput, calls=%fused_computation.6 | convolution fusion | flops 1409974272 | bytes 16252928 | tf_op jit(solution)/shard_map/dot_general | solution.py:134
  49.1 7.6 %fusion = bf16[1,96,7168]{2,1,0:T(8,128)(2,1)S(1)} fusion(bf16[96,1024]{1,0:T(8,128)(2,1)S(1)} %reshape_squeeze.6.x_ref, bf16[1024,7168]{1,0:T(8,128)(2,1)} %wg_ref.1), kind=kOutput, calls=%fused_computation.5 | convolution fusion | flops 1409974272 | bytes 16252928 | tf_op jit(solution)/shard_map/dot_general | solution.py:133
  56.8 9.7 %fusion.2 = bf16[1,96,7168]{2,1,0:T(8,128)(2,1)S(1)} fusion(bf16[96,1024]{1,0:T(8,128)(2,1)S(1)} %reshape_squeeze.7.y_ref, bf16[7168,1024]{1,0:T(8,128)(2,1)} %param.11), kind=kOutput, calls=%fused_computation.7 | convolution fusion | flops 1409974272 | bytes 16252928 | tf_op jit(solution)/shard_map/dot_general | solution.py:135
  66.5 2.2 %pad_maximum_fusion = bf16[3,96,7168]{2,1,0:T(8,128)(2,1)} fusion(bf16[1,96,7168]{2,1,0:T(8,128)(2,1)S(1)} %fusion.2, bf16[1,96,7168]{2,1,0:T(8,128)(2,1)S(1)} %fusion.1, bf16[1,96,7168]{2,1,0:T(8,128)(2,1)S(1)} %fusion), kind=kLoop, calls=%fused_computation.8 | loop fusion | flops 4128768 | bytes 8257536 | tf_op jit(solution)/shard_map/stack | solution.py:138
  68.7 0.0 reduce-scatter.2.cloned.1.call-update
  68.8 0.3 all-gather.2.cloned.1.call-start
  69.0 41.7 %reduce-scatter.2.cloned.1.call-done = bf16[3,96,1792]{2,1,0:T(8,128)(2,1)} async-done(((bf16[3,96,7168]{2,1,0:T(8,128)(2,1)}), bf16[3,96,1792]{2,1,0:T(8,128)(2,1)}) %reduce-scatter.2.cloned.1.call-update) | async-done | bytes 1032208 | tf_op jit(solution)/shard_map/reduce_scatter | solution.py:139
  110.7 1.4 convert_element_type.36
  112.1 0.4 multiply_convert_fusion.2
  112.5 1.1 pad_maximum_fusion.1
  113.5 0.0 all-gather.2.cloned.1.call-update
  113.6 34.2 %all-gather.2.cloned.1.call-done.dg_ref.du_ref.h_ref = bf16[3,96,7168]{2,1,0:T(8,128)(2,1)} async-done(((bf16[3,96,1792]{2,1,0:T(8,128)(2,1)}), bf16[3,96,7168]{2,1,0:T(8,128)(2,1)}) %all-gather.2.cloned.1.call-update) | async-done | bytes 4128784 | tf_op jit(solution)/shard_map/all_gather | solution.py:141
  147.8 18.7 %shard_map.93 = f32[1024,96]{1,0:T(8,128)} custom-call(bf16[3,96,7168]{2,1,0:T(8,128)(2,1)} %all-gather.2.cloned.1.call-done.dg_ref.du_ref.h_ref, bf16[3,96,7168]{2,1,0:T(8,128)(2,1)} %all-gather.2.cloned.1.call-done.dg_ref.du_ref.h_ref, bf16[1024,7168]{1,0:T(8,128)(2,1)} %wg_ref.1, bf16[1024,7168]{1,0:T(8,128)(2,1)} %wu_ref.1), custom_call_target="tpu_custom_call" | custom-call | flops 2818572288 | bytes 32505856 | tf_op jit(solution)/shard_map/pallas_call | solution.py:53
  166.6 1.1 convert_bitcast_fusion
  167.6 0.1 copy.18
  167.8 0.1 all_to_all.17
  167.9 1.8 reduce.4
  169.7 0.8 reshape.68
  170.5 4.6 %all-to-all-start.1 = ((bf16[32,2,1536]{2,1,0:T(2,128)(2,1)}), bf16[32,2,1536]{2,1,0:T(2,128)(2,1)S(1)}, u32[]{:S(2)}, u32[]{:S(2)}) async-start(bf16[32,2,1536]{2,1,0:T(2,128)(2,1)} %reshape.68), calls=%async_computation.2 | async-start | bytes 393216 | tf_op jit(solution)/shard_map/all_to_all | solution.py:145
  175.1 18.6 %shard_map.94 = (bf16[1024,7168]{1,0:T(8,128)(2,1)}, bf16[1024,7168]{1,0:T(8,128)(2,1)}, bf16[7168,1024]{1,0:T(8,128)(2,1)}) custom-call(bf16[3,96,7168]{2,1,0:T(8,128)(2,1)} %all-gather.2.cloned.1.call-done.dg_ref.du_ref.h_ref, bf16[3,96,7168]{2,1,0:T(8,128)(2,1)} %all-gather.2.cloned.1.call-done.dg_ref.du_ref.h_ref, ...), custom_call_target="tpu_custom_call" | custom-call | flops 4227858432 | bytes 48562176 | tf_op jit(solution)/shard_map/pallas_call | solution.py:80
  193.7 0.0 all-to-all-done.1
  193.8 0.1 reshape.69
  193.9 1.1 convert_reduce_fusion
  195.0 0.3 reshape.46
  195.3 0.2 copy.20
  195.5 0.1 copy.21
  195.6 1.3 gather_fusion
  (6 shorter events, 0.1 us)
Async XLA Ops:
  7.2 103.5 %reduce-scatter.2.cloned.1.call-start = ((), (), s32[]{:S(2)}) async-start(), calls=%async_computation.3 | async-start | bytes 5160960 | tf_op jit(solution)/shard_map/reduce_scatter | solution.py:139
  41.3 7.9 %copy-start = (bf16[96,1024]{1,0:T(8,128)(2,1)}, bf16[96,1024]{1,0:T(8,128)(2,1)S(1)}, u32[]{:S(2)}) copy-start(bf16[96,1024]{1,0:T(8,128)(2,1)S(1)} %reshape_squeeze.6.x_ref) | copy-start | bytes 589828
  41.4 15.3 %copy-start.1 = (bf16[96,1024]{1,0:T(8,128)(2,1)}, bf16[96,1024]{1,0:T(8,128)(2,1)S(1)}, u32[]{:S(2)}) copy-start(bf16[96,1024]{1,0:T(8,128)(2,1)S(1)} %reshape_squeeze.7.y_ref) | copy-start | bytes 589828
  68.8 79.0 %all-gather.2.cloned.1.call-start = ((), (), s32[]{:S(2)}) async-start(), calls=%async_computation.4 | async-start | bytes 5160960 | tf_op jit(solution)/shard_map/all_gather | solution.py:141
  170.5 23.2 %all-to-all-start.1 = ((bf16[32,2,1536]{2,1,0:T(2,128)(2,1)}), bf16[32,2,1536]{2,1,0:T(2,128)(2,1)S(1)}, u32[]{:S(2)}, u32[]{:S(2)}) async-start(bf16[32,2,1536]{2,1,0:T(2,128)(2,1)} %reshape.68), calls=%async_computation.2 | async-start | bytes 393216 | tf_op jit(solution)/shard_map/all_to_all | solution.py:145
Sparse Core Ops, SparseCore 0:
  68.9 41.7 reduce-scatter.1
  113.7 34.0 all-gather.1

commit v8 on v7

--- a/solution.py
+++ b/solution.py
@@ -45,7 +45,7 @@
 def backward_rows(gathered, w_gate, w_up):
     rows, ff = gathered.shape[1], gathered.shape[2]
     cols = w_gate.shape[0]
-    tile = 512 if ff % 512 == 0 else ff
+    tile = 1024 if ff % 1024 == 0 else ff
 
     def plane(p):
         return pl.BlockSpec((None, rows, tile), lambda k: (p, 0, k))

time: 205 us -> 202 us (0.985)
  Pallas kernels: 37.4 us -> 34.2 us
    pallas_call x1, Pallas kernels: 18.7 us -> 15.6 us  [backward_rows(): pl.pallas_call(_rows_body, grid=(ff // tile,), in_specs=[plane(2), plane(...]
where the time goes in v8:
time: 202 us; the launch traced here: 201 us
  waiting for transfers between devices  75.9 us (38%)
  Pallas kernels  34.2 us (17%)
  matrix products  25 us (12%)
  blocking collectives  20.6 us (10%)
  other arithmetic  17.5 us (9%)
  between operations  14.3 us (7%)
  local copies, waits for them, and re-layouts  8.02 us (4%)
  starting transfers between devices  4.91 us (2%)
    reduce_scatter x1, waiting for transfers between devices, on_device(): lax.psum_scatter(parts, 'dp', scatter_dimension=2, tiled=True)  41.7 us
    all_gather x1, waiting for transfers between devices, on_device(): lax.all_gather(jnp.stack([hidden, d_up, d_gate]), 'dp', axis=2, tiled=True)  34.2 us
    all_to_all x1, blocking collectives, on_device(): recv = lax.all_to_all(send, ALL, 0, 0, tiled=True)  20.6 us
    pallas_call x1, Pallas kernels, backward_grads(): pl.pallas_call(_grads_body, grid=(ff // tile,), in_specs=[plane(2), plane...  18.6 us
    pallas_call x1, Pallas kernels, backward_rows(): pl.pallas_call(_rows_body, grid=(ff // tile,), in_specs=[plane(2), plane(...  15.6 us
    dot_general x1, matrix products, on_device(): lax.dot_general(rows_grad, w_down, (((1,), (1,)), ((), ())), preferred_el...  9.74 us
    dot_general x1, matrix products, on_device(): up_part = jnp.dot(rows_in, w_up, preferred_element_type=jnp.float32)  7.68 us
    dot_general x1, matrix products, on_device(): gate_part = jnp.dot(rows_in, w_gate, preferred_element_type=jnp.float32)  7.61 us
  transfers between devices with their start and end apart: 3, of which 2 were waited for; matrix products, arithmetic and copies ran while one was open for 0% of the time, Pallas kernels for 9%

profile of v8, /device:TPU:0, one launch (start us, length us, event | category | flops | bytes accessed | tf_op | source)
XLA Modules:
  0.0 200.5 jit_solution(17859567235885719998)
XLA Ops:
  7.2 0.0 reduce-scatter.2.cloned.1.call-start
  7.2 0.7 fusion.4
  8.0 0.8 select_reduce_fusion
  8.8 0.7 fusion.5
  9.5 1.0 maximum_bitcast_fusion
  10.5 0.3 copy.15
  10.8 0.3 broadcast_in_dim.2
  11.1 1.1 scatter_fusion
  12.2 0.2 reshape.38
  12.4 0.3 copy.23
  12.8 0.5 all_to_all.16
  13.3 0.5 broadcast.47
  13.8 2.9 %reduce.3 = bf16[32,6144]{1,0:T(8,128)(2,1)S(1)} reduce(bf16[32,1,6144]{2,1,0:T(2,128)(2,1)S(1)} %all_to_all.16, bf16[]{:T(256)} %broadcast.47), dimensions={1}, to_apply=%all_to_all.16.reduce_sub_computation | reduce | bytes 786434 | tf_op jit(solution)/shard_map/all_to_all | solution.py:128
  16.8 0.3 reshape.66
  17.0 20.6 %all_to_all.20 = bf16[32,2,3072]{2,1,0:T(2,128)(2,1)S(1)} all-to-all(bf16[32,2,3072]{2,1,0:T(2,128)(2,1)S(1)} %reshape.66), channel_id=1, replica_groups=mesh['dp'=4,'expert'=8] {'dp','expert'}, dimensions={0} | all-to-all | bytes 786432 | tf_op jit(solution)/shard_map/all_to_all | solution.py:128
  37.7 0.3 reshape.67
  38.0 2.3 %reduce = bf16[32,6144]{1,0:T(8,128)(2,1)S(1)} reduce(bf16[32,1,6144]{2,1,0:T(2,128)(2,1)S(1)} %reshape.67, bf16[]{:T(256)} %constant.19), dimensions={1}, to_apply=%all_to_all.13.reduce_sub_computation | reduce | bytes 786434 | tf_op jit(solution)/shard_map/all_to_all | solution.py:128
  40.3 0.6 reshape.39
  40.9 0.2 fusion.6
  41.1 0.2 reshape_squeeze.6.x_ref
  41.3 0.2 reshape_squeeze.7.y_ref
  41.4 7.7 %fusion.1 = bf16[1,96,7168]{2,1,0:T(8,128)(2,1)S(1)} fusion(bf16[96,1024]{1,0:T(8,128)(2,1)S(1)} %reshape_squeeze.6.x_ref, bf16[1024,7168]{1,0:T(8,128)(2,1)} %wu_ref.1), kind=kOutput, calls=%fused_computation.6 | convolution fusion | flops 1409974272 | bytes 16252928 | tf_op jit(solution)/shard_map/dot_general | solution.py:134
  49.1 7.6 %fusion = bf16[1,96,7168]{2,1,0:T(8,128)(2,1)S(1)} fusion(bf16[96,1024]{1,0:T(8,128)(2,1)S(1)} %reshape_squeeze.6.x_ref, bf16[1024,7168]{1,0:T(8,128)(2,1)} %wg_ref.1), kind=kOutput, calls=%fused_computation.5 | convolution fusion | flops 1409974272 | bytes 16252928 | tf_op jit(solution)/shard_map/dot_general | solution.py:133
  56.8 9.7 %fusion.2 = bf16[1,96,7168]{2,1,0:T(8,128)(2,1)S(1)} fusion(bf16[96,1024]{1,0:T(8,128)(2,1)S(1)} %reshape_squeeze.7.y_ref, bf16[7168,1024]{1,0:T(8,128)(2,1)} %param.11), kind=kOutput, calls=%fused_computation.7 | convolution fusion | flops 1409974272 | bytes 16252928 | tf_op jit(solution)/shard_map/dot_general | solution.py:135
  66.5 2.2 %pad_maximum_fusion = bf16[3,96,7168]{2,1,0:T(8,128)(2,1)} fusion(bf16[1,96,7168]{2,1,0:T(8,128)(2,1)S(1)} %fusion.2, bf16[1,96,7168]{2,1,0:T(8,128)(2,1)S(1)} %fusion.1, bf16[1,96,7168]{2,1,0:T(8,128)(2,1)S(1)} %fusion), kind=kLoop, calls=%fused_computation.8 | loop fusion | flops 4128768 | bytes 8257536 | tf_op jit(solution)/shard_map/stack | solution.py:138
  68.7 0.0 reduce-scatter.2.cloned.1.call-update
  68.8 0.3 all-gather.2.cloned.1.call-start
  69.0 41.7 %reduce-scatter.2.cloned.1.call-done = bf16[3,96,1792]{2,1,0:T(8,128)(2,1)} async-done(((bf16[3,96,7168]{2,1,0:T(8,128)(2,1)}), bf16[3,96,1792]{2,1,0:T(8,128)(2,1)}) %reduce-scatter.2.cloned.1.call-update) | async-done | bytes 1032208 | tf_op jit(solution)/shard_map/reduce_scatter | solution.py:139
  110.7 1.4 convert_element_type.36
  112.1 0.4 multiply_convert_fusion.2
  112.5 1.1 pad_maximum_fusion.1
  113.5 0.0 all-gather.2.cloned.1.call-update
  113.6 34.2 %all-gather.2.cloned.1.call-done.dg_ref.du_ref.h_ref = bf16[3,96,7168]{2,1,0:T(8,128)(2,1)} async-done(((bf16[3,96,1792]{2,1,0:T(8,128)(2,1)}), bf16[3,96,7168]{2,1,0:T(8,128)(2,1)}) %all-gather.2.cloned.1.call-update) | async-done | bytes 4128784 | tf_op jit(solution)/shard_map/all_gather | solution.py:141
  147.8 15.6 %shard_map.93 = f32[1024,96]{1,0:T(8,128)} custom-call(bf16[3,96,7168]{2,1,0:T(8,128)(2,1)} %all-gather.2.cloned.1.call-done.dg_ref.du_ref.h_ref, bf16[3,96,7168]{2,1,0:T(8,128)(2,1)} %all-gather.2.cloned.1.call-done.dg_ref.du_ref.h_ref, bf16[1024,7168]{1,0:T(8,128)(2,1)} %wg_ref.1, bf16[1024,7168]{1,0:T(8,128)(2,1)} %wu_ref.1), custom_call_target="tpu_custom_call" | custom-call | flops 2818572288 | bytes 32505856 | tf_op jit(solution)/shard_map/pallas_call | solution.py:53
  163.4 1.1 convert_bitcast_fusion
  164.5 0.1 copy.18
  164.6 0.1 all_to_all.17
  164.8 1.8 reduce.4
  166.5 0.8 reshape.68
  167.4 4.6 %all-to-all-start.1 = ((bf16[32,2,1536]{2,1,0:T(2,128)(2,1)}), bf16[32,2,1536]{2,1,0:T(2,128)(2,1)S(1)}, u32[]{:S(2)}, u32[]{:S(2)}) async-start(bf16[32,2,1536]{2,1,0:T(2,128)(2,1)} %reshape.68), calls=%async_computation.2 | async-start | bytes 393216 | tf_op jit(solution)/shard_map/all_to_all | solution.py:145
  172.0 18.6 %shard_map.94 = (bf16[1024,7168]{1,0:T(8,128)(2,1)}, bf16[1024,7168]{1,0:T(8,128)(2,1)}, bf16[7168,1024]{1,0:T(8,128)(2,1)}) custom-call(bf16[3,96,7168]{2,1,0:T(8,128)(2,1)} %all-gather.2.cloned.1.call-done.dg_ref.du_ref.h_ref, bf16[3,96,7168]{2,1,0:T(8,128)(2,1)} %all-gather.2.cloned.1.call-done.dg_ref.du_ref.h_ref, ...), custom_call_target="tpu_custom_call" | custom-call | flops 4227858432 | bytes 48562176 | tf_op jit(solution)/shard_map/pallas_call | solution.py:80
  190.6 0.0 all-to-all-done.1
  190.6 0.1 reshape.69
  190.7 1.1 convert_reduce_fusion
  191.8 0.3 reshape.46
  192.1 0.2 copy.20
  192.3 0.1 copy.21
  192.4 1.3 gather_fusion
  (6 shorter events, 0.1 us)
Async XLA Ops:
  7.2 103.5 %reduce-scatter.2.cloned.1.call-start = ((), (), s32[]{:S(2)}) async-start(), calls=%async_computation.3 | async-start | bytes 5160960 | tf_op jit(solution)/shard_map/reduce_scatter | solution.py:139
  41.3 7.9 %copy-start = (bf16[96,1024]{1,0:T(8,128)(2,1)}, bf16[96,1024]{1,0:T(8,128)(2,1)S(1)}, u32[]{:S(2)}) copy-start(bf16[96,1024]{1,0:T(8,128)(2,1)S(1)} %reshape_squeeze.6.x_ref) | copy-start | bytes 589828
  41.4 15.3 %copy-start.1 = (bf16[96,1024]{1,0:T(8,128)(2,1)}, bf16[96,1024]{1,0:T(8,128)(2,1)S(1)}, u32[]{:S(2)}) copy-start(bf16[96,1024]{1,0:T(8,128)(2,1)S(1)} %reshape_squeeze.7.y_ref) | copy-start | bytes 589828
  68.8 79.0 %all-gather.2.cloned.1.call-start = ((), (), s32[]{:S(2)}) async-start(), calls=%async_computation.4 | async-start | bytes 5160960 | tf_op jit(solution)/shard_map/all_gather | solution.py:141
  167.4 23.2 %all-to-all-start.1 = ((bf16[32,2,1536]{2,1,0:T(2,128)(2,1)}), bf16[32,2,1536]{2,1,0:T(2,128)(2,1)S(1)}, u32[]{:S(2)}, u32[]{:S(2)}) async-start(bf16[32,2,1536]{2,1,0:T(2,128)(2,1)} %reshape.68), calls=%async_computation.2 | async-start | bytes 393216 | tf_op jit(solution)/shard_map/all_to_all | solution.py:145
Sparse Core Ops, SparseCore 0:
  68.9 41.7 reduce-scatter.1
  113.7 34.0 all-gather.1

commit v9 on v8

--- a/solution.py
+++ b/solution.py
@@ -120,12 +120,14 @@
 
     both = jnp.stack([inputs, grad_out])
     slots = jnp.zeros((2, EXPERTS * capacity, width), jnp.bfloat16).at[:, slot_ids].set(both)
-    send = slots.reshape(2, EXPERTS, capacity, replicas, columns)
-    send = jnp.transpose(send, (3, 1, 0, 2, 4))
     send = jnp.broadcast_to(
-        send[:, :, None], (replicas, EXPERTS, group, 2, capacity, columns)
-    ).reshape(replicas * members, 2 * capacity * columns)
-    recv = lax.all_to_all(send, ALL, 0, 0, tiled=True)
+        jnp.transpose(slots.reshape(2, EXPERTS, capacity * width), (1, 0, 2))[:, None],
+        (EXPERTS, group, 2, capacity * width),
+    ).reshape(members, 2 * capacity * width)
+    recv = lax.all_to_all(send, "expert", 0, 0, tiled=True)
+    recv = recv.reshape(members * 2 * capacity, replicas, columns)
+    recv = jnp.transpose(recv, (1, 0, 2)).reshape(replicas, members * 2 * capacity * columns)
+    recv = lax.all_to_all(recv, "dp", 0, 0, tiled=True)
     recv = recv.reshape(replicas * members, 2, capacity, columns)
     rows_in = recv[:, 0].reshape(-1, columns)
     rows_grad = recv[:, 1].reshape(-1, columns)

time: 202 us -> 212 us (1.050)
  blocking collectives: 20.6 us -> 29.2 us
    all_to_all x1 -> x2, blocking collectives: 20.6 us -> 29.2 us  [the longest x1 19.2 us: on_device(): recv = lax.all_to_all(send, 'expert', 0, 0, tiled=True)]
    all_to_all x2 -> x4, other arithmetic: 5.26 us -> 6.95 us  [the longest x2 3.68 us: on_device(): recv = lax.all_to_all(recv, 'dp', 0, 0, tiled=True)]
where the time goes in v9:
time: 212 us; the launch traced here: 211 us
  waiting for transfers between devices  76 us (36%)
  Pallas kernels  34.2 us (16%)
  blocking collectives  29.2 us (14%)
  matrix products  25 us (12%)
  other arithmetic  19.2 us (9%)
  between operations  14.3 us (7%)
  local copies, waits for them, and re-layouts  8.29 us (4%)
  starting transfers between devices  4.9 us (2%)
    reduce_scatter x1, waiting for transfers between devices, on_device(): lax.psum_scatter(parts, 'dp', scatter_dimension=2, tiled=True)  41.7 us
    all_gather x1, waiting for transfers between devices, on_device(): lax.all_gather(jnp.stack([hidden, d_up, d_gate]), 'dp', axis=2, tiled=True)  34.3 us
    all_to_all x1, blocking collectives, on_device(): recv = lax.all_to_all(send, 'expert', 0, 0, tiled=True)  19.2 us
    pallas_call x1, Pallas kernels, backward_grads(): pl.pallas_call(_grads_body, grid=(ff // tile,), in_specs=[plane(2), plane...  18.6 us
    pallas_call x1, Pallas kernels, backward_rows(): pl.pallas_call(_rows_body, grid=(ff // tile,), in_specs=[plane(2), plane(...  15.6 us
    all_to_all x1, blocking collectives, on_device(): recv = lax.all_to_all(recv, 'dp', 0, 0, tiled=True)  10 us
    dot_general x1, matrix products, on_device(): lax.dot_general(rows_grad, w_down, (((1,), (1,)), ((), ())), preferred_el...  9.74 us
    dot_general x1, matrix products, on_device(): up_part = jnp.dot(rows_in, w_up, preferred_element_type=jnp.float32)  7.68 us
  transfers between devices with their start and end apart: 3, of which 2 were waited for; matrix products, arithmetic and copies ran while one was open for 0% of the time, Pallas kernels for 9%

profile of v9, /device:TPU:0, one launch (start us, length us, event | category | flops | bytes accessed | tf_op | source)
XLA Modules:
  0.0 211.1 jit_solution(7480576060537975123)
XLA Ops:
  7.2 0.7 fusion.4
  8.0 0.8 select_reduce_fusion
  8.8 0.7 fusion.5
  9.5 1.0 maximum_bitcast_fusion
  10.5 0.3 copy.15
  10.8 0.3 broadcast_in_dim.2
  11.1 1.1 scatter_fusion
  12.2 0.2 copy.16
  12.4 0.2 reshape.46
  12.6 0.5 broadcast.48
  13.1 0.9 reduce.4
  14.1 0.3 reshape.76
  14.4 19.2 %all_to_all.28 = bf16[8,2,12288]{2,1,0:T(2,128)(2,1)S(1)} all-to-all(bf16[8,2,12288]{2,1,0:T(2,128)(2,1)S(1)} %reshape.76), channel_id=1, replica_groups=mesh['dp'=4,'expert'=8] {'expert'}, dimensions={0} | all-to-all | bytes 786432 | tf_op jit(solution)/shard_map/all_to_all | solution.py:127
  33.5 0.4 reshape.77
  33.9 2.4 %reduce = bf16[8,24576]{1,0:T(8,128)(2,1)S(1)} reduce(bf16[8,1,24576]{2,1,0:T(2,128)(2,1)S(1)} %reshape.77, bf16[]{:T(256)} %constant.19), dimensions={1}, to_apply=%all_to_all.19.reduce_sub_computation | reduce | bytes 786434 | tf_op jit(solution)/shard_map/all_to_all | solution.py:127
  36.3 0.3 reshape.47
  36.6 1.1 reduce.5
  37.7 0.4 reshape.78
  38.1 10.0 %all_to_all.29 = bf16[4,2,24576]{2,1,0:T(2,128)(2,1)S(1)} all-to-all(bf16[4,2,24576]{2,1,0:T(2,128)(2,1)S(1)} %reshape.78), channel_id=1, replica_groups=mesh['dp'=4,'expert'=8] {'dp'}, dimensions={0} | all-to-all | bytes 786432 | tf_op jit(solution)/shard_map/all_to_all | solution.py:130
  48.1 0.4 reshape.79
  48.6 2.5 %reduce.1 = bf16[4,49152]{1,0:T(4,128)(2,1)S(1)} reduce(bf16[4,1,49152]{2,1,0:T(2,128)(2,1)S(1)} %reshape.79, bf16[]{:T(256)} %constant.19), dimensions={1}, to_apply=%all_to_all.21.reduce_sub_computation | reduce | bytes 786434 | tf_op jit(solution)/shard_map/all_to_all | solution.py:130
  51.1 0.3 reshape.48
  51.4 0.2 fusion.6
  51.6 0.2 reshape_squeeze.6.x_ref
  51.8 0.2 reshape_squeeze.7.y_ref
  52.0 7.7 %fusion.1 = bf16[1,96,7168]{2,1,0:T(8,128)(2,1)S(1)} fusion(bf16[96,1024]{1,0:T(8,128)(2,1)S(1)} %reshape_squeeze.6.x_ref, bf16[1024,7168]{1,0:T(8,128)(2,1)} %wu_ref.1), kind=kOutput, calls=%fused_computation.6 | convolution fusion | flops 1409974272 | bytes 16252928 | tf_op jit(solution)/shard_map/dot_general | solution.py:136
  59.7 7.6 %fusion = bf16[1,96,7168]{2,1,0:T(8,128)(2,1)S(1)} fusion(bf16[96,1024]{1,0:T(8,128)(2,1)S(1)} %reshape_squeeze.6.x_ref, bf16[1024,7168]{1,0:T(8,128)(2,1)} %wg_ref.1), kind=kOutput, calls=%fused_computation.5 | convolution fusion | flops 1409974272 | bytes 16252928 | tf_op jit(solution)/shard_map/dot_general | solution.py:135
  67.3 9.7 %fusion.2 = bf16[1,96,7168]{2,1,0:T(8,128)(2,1)S(1)} fusion(bf16[96,1024]{1,0:T(8,128)(2,1)S(1)} %reshape_squeeze.7.y_ref, bf16[7168,1024]{1,0:T(8,128)(2,1)} %param.11), kind=kOutput, calls=%fused_computation.7 | convolution fusion | flops 1409974272 | bytes 16252928 | tf_op jit(solution)/shard_map/dot_general | solution.py:137
  77.0 2.2 %pad_maximum_fusion = bf16[3,96,7168]{2,1,0:T(8,128)(2,1)} fusion(bf16[1,96,7168]{2,1,0:T(8,128)(2,1)S(1)} %fusion.2, bf16[1,96,7168]{2,1,0:T(8,128)(2,1)S(1)} %fusion.1, bf16[1,96,7168]{2,1,0:T(8,128)(2,1)S(1)} %fusion), kind=kLoop, calls=%fused_computation.8 | loop fusion | flops 4128768 | bytes 8257536 | tf_op jit(solution)/shard_map/stack | solution.py:140
  79.3 0.3 all-gather.2.cloned.1.call-start
  79.6 41.7 %reduce-scatter.2.cloned.1.call-done = bf16[3,96,1792]{2,1,0:T(8,128)(2,1)} async-done(((bf16[3,96,7168]{2,1,0:T(8,128)(2,1)}), bf16[3,96,1792]{2,1,0:T(8,128)(2,1)}) %reduce-scatter.2.cloned.1.call-update) | async-done | bytes 1032208 | tf_op jit(solution)/shard_map/reduce_scatter | solution.py:141
  121.3 1.4 convert_element_type.36
  122.6 0.4 multiply_convert_fusion.2
  123.0 1.1 pad_maximum_fusion.1
  124.1 34.3 %all-gather.2.cloned.1.call-done.dg_ref.du_ref.h_ref = bf16[3,96,7168]{2,1,0:T(8,128)(2,1)} async-done(((bf16[3,96,1792]{2,1,0:T(8,128)(2,1)}), bf16[3,96,7168]{2,1,0:T(8,128)(2,1)}) %all-gather.2.cloned.1.call-update) | async-done | bytes 4128784 | tf_op jit(solution)/shard_map/all_gather | solution.py:143
  158.4 15.6 %shard_map.93 = f32[1024,96]{1,0:T(8,128)} custom-call(bf16[3,96,7168]{2,1,0:T(8,128)(2,1)} %all-gather.2.cloned.1.call-done.dg_ref.du_ref.h_ref, bf16[3,96,7168]{2,1,0:T(8,128)(2,1)} %all-gather.2.cloned.1.call-done.dg_ref.du_ref.h_ref, bf16[1024,7168]{1,0:T(8,128)(2,1)} %wg_ref.1, bf16[1024,7168]{1,0:T(8,128)(2,1)} %wu_ref.1), custom_call_target="tpu_custom_call" | custom-call | flops 2818572288 | bytes 32505856 | tf_op jit(solution)/shard_map/pallas_call | solution.py:53
  174.0 1.1 convert_bitcast_fusion
  175.0 0.1 copy.19
  175.2 0.1 all_to_all.24
  175.3 1.8 reduce.6
  177.1 0.8 reshape.80
  177.9 4.6 %all-to-all-start.2 = ((bf16[32,2,1536]{2,1,0:T(2,128)(2,1)}), bf16[32,2,1536]{2,1,0:T(2,128)(2,1)S(1)}, u32[]{:S(2)}, u32[]{:S(2)}) async-start(bf16[32,2,1536]{2,1,0:T(2,128)(2,1)} %reshape.80), calls=%async_computation.3 | async-start | bytes 393216 | tf_op jit(solution)/shard_map/all_to_all | solution.py:147
  182.5 18.6 %shard_map.94 = (bf16[1024,7168]{1,0:T(8,128)(2,1)}, bf16[1024,7168]{1,0:T(8,128)(2,1)}, bf16[7168,1024]{1,0:T(8,128)(2,1)}) custom-call(bf16[3,96,7168]{2,1,0:T(8,128)(2,1)} %all-gather.2.cloned.1.call-done.dg_ref.du_ref.h_ref, bf16[3,96,7168]{2,1,0:T(8,128)(2,1)} %all-gather.2.cloned.1.call-done.dg_ref.du_ref.h_ref, ...), custom_call_target="tpu_custom_call" | custom-call | flops 4227858432 | bytes 48562176 | tf_op jit(solution)/shard_map/pallas_call | solution.py:80
  201.1 0.1 reshape.81
  201.3 1.1 convert_reduce_fusion
  202.4 0.3 reshape.55
  202.7 0.2 copy.21
  203.0 1.3 gather_fusion
  (11 shorter events, 0.2 us)
Async XLA Ops:
  7.2 114.1 %reduce-scatter.2.cloned.1.call-start = ((), (), s32[]{:S(2)}) async-start(), calls=%async_computation.4 | async-start | bytes 5160960 | tf_op jit(solution)/shard_map/reduce_scatter | solution.py:141
  51.8 7.9 %copy-start = (bf16[96,1024]{1,0:T(8,128)(2,1)}, bf16[96,1024]{1,0:T(8,128)(2,1)S(1)}, u32[]{:S(2)}) copy-start(bf16[96,1024]{1,0:T(8,128)(2,1)S(1)} %reshape_squeeze.6.x_ref) | copy-start | bytes 589828
  52.0 15.3 %copy-start.1 = (bf16[96,1024]{1,0:T(8,128)(2,1)}, bf16[96,1024]{1,0:T(8,128)(2,1)S(1)}, u32[]{:S(2)}) copy-start(bf16[96,1024]{1,0:T(8,128)(2,1)S(1)} %reshape_squeeze.7.y_ref) | copy-start | bytes 589828
  79.3 79.1 %all-gather.2.cloned.1.call-start = ((), (), s32[]{:S(2)}) async-start(), calls=%async_computation.5 | async-start | bytes 5160960 | tf_op jit(solution)/shard_map/all_gather | solution.py:143
  177.9 23.2 %all-to-all-start.2 = ((bf16[32,2,1536]{2,1,0:T(2,128)(2,1)}), bf16[32,2,1536]{2,1,0:T(2,128)(2,1)S(1)}, u32[]{:S(2)}, u32[]{:S(2)}) async-start(bf16[32,2,1536]{2,1,0:T(2,128)(2,1)} %reshape.80), calls=%async_computation.3 | async-start | bytes 393216 | tf_op jit(solution)/shard_map/all_to_all | solution.py:147
Sparse Core Ops, SparseCore 0:
  79.4 41.8 reduce-scatter.1
  124.2 34.1 all-gather.1

commit v10 on v8

--- a/solution.py
+++ b/solution.py
@@ -71,7 +71,7 @@
 def backward_grads(gathered, rows_in, rows_grad):
     rows, ff = gathered.shape[1], gathered.shape[2]
     cols = rows_in.shape[1]
-    tile = 512 if ff % 512 == 0 else ff
+    tile = 1024 if ff % 1024 == 0 else ff
     bf = jnp.bfloat16
 
     def plane(p):

time: 202 us -> 200 us (0.990)
  no operation moved by 1% of the time
where the time goes in v10:
time: 200 us; the launch traced here: 199 us
  waiting for transfers between devices  75.9 us (38%)
  Pallas kernels  32.8 us (16%)
  matrix products  25 us (12%)
  blocking collectives  20.6 us (10%)
  other arithmetic  17.5 us (9%)
  between operations  14.3 us (7%)
  local copies, waits for them, and re-layouts  8.02 us (4%)
  starting transfers between devices  4.91 us (2%)
    reduce_scatter x1, waiting for transfers between devices, on_device(): lax.psum_scatter(parts, 'dp', scatter_dimension=2, tiled=True)  41.7 us
    all_gather x1, waiting for transfers between devices, on_device(): lax.all_gather(jnp.stack([hidden, d_up, d_gate]), 'dp', axis=2, tiled=True)  34.2 us
    all_to_all x1, blocking collectives, on_device(): recv = lax.all_to_all(send, ALL, 0, 0, tiled=True)  20.6 us
    pallas_call x1, Pallas kernels, backward_grads(): pl.pallas_call(_grads_body, grid=(ff // tile,), in_specs=[plane(2), plane...  17.2 us
    pallas_call x1, Pallas kernels, backward_rows(): pl.pallas_call(_rows_body, grid=(ff // tile,), in_specs=[plane(2), plane(...  15.6 us
    dot_general x1, matrix products, on_device(): lax.dot_general(rows_grad, w_down, (((1,), (1,)), ((), ())), preferred_el...  9.74 us
    dot_general x1, matrix products, on_device(): up_part = jnp.dot(rows_in, w_up, preferred_element_type=jnp.float32)  7.68 us
    dot_general x1, matrix products, on_device(): gate_part = jnp.dot(rows_in, w_gate, preferred_element_type=jnp.float32)  7.61 us
  transfers between devices with their start and end apart: 3, of which 2 were waited for; matrix products, arithmetic and copies ran while one was open for 0% of the time, Pallas kernels for 9%

profile of v10, /device:TPU:0, one launch (start us, length us, event | category | flops | bytes accessed | tf_op | source)
XLA Modules:
  0.0 199.1 jit_solution(6232899136138562802)
XLA Ops:
  7.2 0.0 reduce-scatter.2.cloned.1.call-start
  7.2 0.7 fusion.4
  8.0 0.8 select_reduce_fusion
  8.8 0.7 fusion.5
  9.5 1.0 maximum_bitcast_fusion
  10.5 0.3 copy.15
  10.8 0.3 broadcast_in_dim.2
  11.1 1.1 scatter_fusion
  12.2 0.2 reshape.38
  12.4 0.3 copy.23
  12.8 0.5 all_to_all.16
  13.3 0.5 broadcast.47
  13.8 2.9 %reduce.3 = bf16[32,6144]{1,0:T(8,128)(2,1)S(1)} reduce(bf16[32,1,6144]{2,1,0:T(2,128)(2,1)S(1)} %all_to_all.16, bf16[]{:T(256)} %broadcast.47), dimensions={1}, to_apply=%all_to_all.16.reduce_sub_computation | reduce | bytes 786434 | tf_op jit(solution)/shard_map/all_to_all | solution.py:128
  16.8 0.3 reshape.66
  17.0 20.6 %all_to_all.20 = bf16[32,2,3072]{2,1,0:T(2,128)(2,1)S(1)} all-to-all(bf16[32,2,3072]{2,1,0:T(2,128)(2,1)S(1)} %reshape.66), channel_id=1, replica_groups=mesh['dp'=4,'expert'=8] {'dp','expert'}, dimensions={0} | all-to-all | bytes 786432 | tf_op jit(solution)/shard_map/all_to_all | solution.py:128
  37.7 0.3 reshape.67
  38.0 2.3 %reduce = bf16[32,6144]{1,0:T(8,128)(2,1)S(1)} reduce(bf16[32,1,6144]{2,1,0:T(2,128)(2,1)S(1)} %reshape.67, bf16[]{:T(256)} %constant.19), dimensions={1}, to_apply=%all_to_all.13.reduce_sub_computation | reduce | bytes 786434 | tf_op jit(solution)/shard_map/all_to_all | solution.py:128
  40.3 0.6 reshape.39
  40.9 0.2 fusion.6
  41.1 0.2 reshape_squeeze.6.x_ref
  41.3 0.2 reshape_squeeze.7.y_ref
  41.4 7.7 %fusion.1 = bf16[1,96,7168]{2,1,0:T(8,128)(2,1)S(1)} fusion(bf16[96,1024]{1,0:T(8,128)(2,1)S(1)} %reshape_squeeze.6.x_ref, bf16[1024,7168]{1,0:T(8,128)(2,1)} %wu_ref.1), kind=kOutput, calls=%fused_computation.6 | convolution fusion | flops 1409974272 | bytes 16252928 | tf_op jit(solution)/shard_map/dot_general | solution.py:134
  49.1 7.6 %fusion = bf16[1,96,7168]{2,1,0:T(8,128)(2,1)S(1)} fusion(bf16[96,1024]{1,0:T(8,128)(2,1)S(1)} %reshape_squeeze.6.x_ref, bf16[1024,7168]{1,0:T(8,128)(2,1)} %wg_ref.1), kind=kOutput, calls=%fused_computation.5 | convolution fusion | flops 1409974272 | bytes 16252928 | tf_op jit(solution)/shard_map/dot_general | solution.py:133
  56.8 9.7 %fusion.2 = bf16[1,96,7168]{2,1,0:T(8,128)(2,1)S(1)} fusion(bf16[96,1024]{1,0:T(8,128)(2,1)S(1)} %reshape_squeeze.7.y_ref, bf16[7168,1024]{1,0:T(8,128)(2,1)} %param.11), kind=kOutput, calls=%fused_computation.7 | convolution fusion | flops 1409974272 | bytes 16252928 | tf_op jit(solution)/shard_map/dot_general | solution.py:135
  66.5 2.2 %pad_maximum_fusion = bf16[3,96,7168]{2,1,0:T(8,128)(2,1)} fusion(bf16[1,96,7168]{2,1,0:T(8,128)(2,1)S(1)} %fusion.2, bf16[1,96,7168]{2,1,0:T(8,128)(2,1)S(1)} %fusion.1, bf16[1,96,7168]{2,1,0:T(8,128)(2,1)S(1)} %fusion), kind=kLoop, calls=%fused_computation.8 | loop fusion | flops 4128768 | bytes 8257536 | tf_op jit(solution)/shard_map/stack | solution.py:138
  68.7 0.0 reduce-scatter.2.cloned.1.call-update
  68.8 0.3 all-gather.2.cloned.1.call-start
  69.0 41.7 %reduce-scatter.2.cloned.1.call-done = bf16[3,96,1792]{2,1,0:T(8,128)(2,1)} async-done(((bf16[3,96,7168]{2,1,0:T(8,128)(2,1)}), bf16[3,96,1792]{2,1,0:T(8,128)(2,1)}) %reduce-scatter.2.cloned.1.call-update) | async-done | bytes 1032208 | tf_op jit(solution)/shard_map/reduce_scatter | solution.py:139
  110.7 1.4 convert_element_type.36
  112.1 0.4 multiply_convert_fusion.2
  112.5 1.1 pad_maximum_fusion.1
  113.5 0.0 all-gather.2.cloned.1.call-update
  113.6 34.2 %all-gather.2.cloned.1.call-done.dg_ref.du_ref.h_ref = bf16[3,96,7168]{2,1,0:T(8,128)(2,1)} async-done(((bf16[3,96,1792]{2,1,0:T(8,128)(2,1)}), bf16[3,96,7168]{2,1,0:T(8,128)(2,1)}) %all-gather.2.cloned.1.call-update) | async-done | bytes 4128784 | tf_op jit(solution)/shard_map/all_gather | solution.py:141
  147.8 15.6 %shard_map.93 = f32[1024,96]{1,0:T(8,128)} custom-call(bf16[3,96,7168]{2,1,0:T(8,128)(2,1)} %all-gather.2.cloned.1.call-done.dg_ref.du_ref.h_ref, bf16[3,96,7168]{2,1,0:T(8,128)(2,1)} %all-gather.2.cloned.1.call-done.dg_ref.du_ref.h_ref, bf16[1024,7168]{1,0:T(8,128)(2,1)} %wg_ref.1, bf16[1024,7168]{1,0:T(8,128)(2,1)} %wu_ref.1), custom_call_target="tpu_custom_call" | custom-call | flops 2818572288 | bytes 32505856 | tf_op jit(solution)/shard_map/pallas_call | solution.py:53
  163.4 1.1 convert_bitcast_fusion
  164.5 0.1 copy.18
  164.6 0.1 all_to_all.17
  164.8 1.8 reduce.4
  166.5 0.8 reshape.68
  167.4 4.6 %all-to-all-start.1 = ((bf16[32,2,1536]{2,1,0:T(2,128)(2,1)}), bf16[32,2,1536]{2,1,0:T(2,128)(2,1)S(1)}, u32[]{:S(2)}, u32[]{:S(2)}) async-start(bf16[32,2,1536]{2,1,0:T(2,128)(2,1)} %reshape.68), calls=%async_computation.2 | async-start | bytes 393216 | tf_op jit(solution)/shard_map/all_to_all | solution.py:145
  172.0 17.2 %shard_map.94 = (bf16[1024,7168]{1,0:T(8,128)(2,1)}, bf16[1024,7168]{1,0:T(8,128)(2,1)}, bf16[7168,1024]{1,0:T(8,128)(2,1)}) custom-call(bf16[3,96,7168]{2,1,0:T(8,128)(2,1)} %all-gather.2.cloned.1.call-done.dg_ref.du_ref.h_ref, bf16[3,96,7168]{2,1,0:T(8,128)(2,1)} %all-gather.2.cloned.1.call-done.dg_ref.du_ref.h_ref, ...), custom_call_target="tpu_custom_call" | custom-call | flops 4227858432 | bytes 48562176 | tf_op jit(solution)/shard_map/pallas_call | solution.py:80
  189.2 0.0 all-to-all-done.1
  189.2 0.1 reshape.69
  189.3 1.1 convert_reduce_fusion
  190.5 0.3 reshape.46
  190.7 0.2 copy.20
  190.9 0.1 copy.21
  191.0 1.3 gather_fusion
  (6 shorter events, 0.1 us)
Async XLA Ops:
  7.2 103.5 %reduce-scatter.2.cloned.1.call-start = ((), (), s32[]{:S(2)}) async-start(), calls=%async_computation.3 | async-start | bytes 5160960 | tf_op jit(solution)/shard_map/reduce_scatter | solution.py:139
  41.3 7.9 %copy-start = (bf16[96,1024]{1,0:T(8,128)(2,1)}, bf16[96,1024]{1,0:T(8,128)(2,1)S(1)}, u32[]{:S(2)}) copy-start(bf16[96,1024]{1,0:T(8,128)(2,1)S(1)} %reshape_squeeze.6.x_ref) | copy-start | bytes 589828
  41.4 15.3 %copy-start.1 = (bf16[96,1024]{1,0:T(8,128)(2,1)}, bf16[96,1024]{1,0:T(8,128)(2,1)S(1)}, u32[]{:S(2)}) copy-start(bf16[96,1024]{1,0:T(8,128)(2,1)S(1)} %reshape_squeeze.7.y_ref) | copy-start | bytes 589828
  68.8 79.0 %all-gather.2.cloned.1.call-start = ((), (), s32[]{:S(2)}) async-start(), calls=%async_computation.4 | async-start | bytes 5160960 | tf_op jit(solution)/shard_map/all_gather | solution.py:141
  167.4 21.8 %all-to-all-start.1 = ((bf16[32,2,1536]{2,1,0:T(2,128)(2,1)}), bf16[32,2,1536]{2,1,0:T(2,128)(2,1)S(1)}, u32[]{:S(2)}, u32[]{:S(2)}) async-start(bf16[32,2,1536]{2,1,0:T(2,128)(2,1)} %reshape.68), calls=%async_computation.2 | async-start | bytes 393216 | tf_op jit(solution)/shard_map/all_to_all | solution.py:145
Sparse Core Ops, SparseCore 0:
  68.9 41.7 reduce-scatter.1
  113.7 34.0 all-gather.1

commit v11 on v10

--- a/solution.py
+++ b/solution.py
@@ -22,6 +22,39 @@
     return lax.dot_general(
         left, right, (((0,), (0,)), ((), ())), preferred_element_type=jnp.float32
     )
+
+
+def _fwd_body(x_ref, y_ref, wg_ref, wu_ref, wd_ref, out_ref):
+    x = x_ref[...]
+    nt = (((1,), (1,)), ((), ()))
+    out_ref[0] = jnp.dot(x, wg_ref[...], preferred_element_type=jnp.float32).astype(out_ref.dtype)
+    out_ref[1] = jnp.dot(x, wu_ref[...], preferred_element_type=jnp.float32).astype(out_ref.dtype)
+    out_ref[2] = lax.dot_general(
+        y_ref[...], wd_ref[...], nt, preferred_element_type=jnp.float32
+    ).astype(out_ref.dtype)
+
+
+def forward_parts(rows_in, rows_grad, w_gate, w_up, w_down):
+    rows, cols = rows_in.shape
+    ff = w_gate.shape[1]
+    tile = 1024 if ff % 1024 == 0 else ff
+    return pl.pallas_call(
+        _fwd_body,
+        grid=(ff // tile,),
+        in_specs=[
+            pl.BlockSpec((rows, cols), lambda k: (0, 0)),
+            pl.BlockSpec((rows, cols), lambda k: (0, 0)),
+            pl.BlockSpec((cols, tile), lambda k: (0, k)),
+            pl.BlockSpec((cols, tile), lambda k: (0, k)),
+            pl.BlockSpec((tile, cols), lambda k: (k, 0)),
+        ],
+        out_specs=pl.BlockSpec((3, rows, tile), lambda k: (0, 0, k)),
+        out_shape=jax.ShapeDtypeStruct((3, rows, ff), jnp.bfloat16),
+        compiler_params=pltpu.CompilerParams(dimension_semantics=("parallel",)),
+        cost_estimate=pl.CostEstimate(
+            flops=6 * rows * ff * cols, transcendentals=0,
+            bytes_accessed=2 * (3 * cols * ff + 3 * rows * ff + 2 * rows * cols)),
+    )(rows_in, rows_grad, w_gate, w_up, w_down)
 
 
 def _rows_body(dg_ref, du_ref, wg_ref, wu_ref, drows_ref):
@@ -130,12 +163,7 @@
     rows_in = recv[:, 0].reshape(-1, columns)
     rows_grad = recv[:, 1].reshape(-1, columns)
 
-    gate_part = jnp.dot(rows_in, w_gate, preferred_element_type=jnp.float32)
-    up_part = jnp.dot(rows_in, w_up, preferred_element_type=jnp.float32)
-    dhid_part = lax.dot_general(
-        rows_grad, w_down, (((1,), (1,)), ((), ())), preferred_element_type=jnp.float32
-    )
-    parts = jnp.stack([gate_part, up_part, dhid_part]).astype(jnp.bfloat16)
+    parts = forward_parts(rows_in, rows_grad, w_gate, w_up, w_down)
     reduced = lax.psum_scatter(parts, "dp", scatter_dimension=2, tiled=True).astype(jnp.float32)
     hidden, d_up, d_gate = nonlinear(reduced[0], reduced[1], reduced[2])
     gathered = lax.all_gather(jnp.stack([hidden, d_up, d_gate]), "dp", axis=2, tiled=True)

time: 200 us -> 193 us (0.965)
  matrix products: 25 us -> 0 us
  Pallas kernels: 32.8 us -> 52.6 us
  other arithmetic: 17.5 us -> 15.3 us
    dot_general x3 -> x0, matrix products: 25 us -> none  [the longest x1 9.74 us: on_device(): lax.dot_general(rows_grad, w_down, (((1,), (1,)), ((), ())), preferred_el...]
    pallas_call x0 -> x1, Pallas kernels: none -> 19.8 us  [forward_parts(): pl.pallas_call(_fwd_body, grid=(ff // tile,), in_specs=[pl.BlockSpec((row...]
    another operation x1 -> x0, other arithmetic: 2.23 us -> none  [on_device(): parts = jnp.stack([gate_part, up_part, dhid_part]).astype(jnp.bfloat16)]
where the time goes in v11:
time: 193 us
  waiting for transfers between devices  76 us (39%)
  Pallas kernels  52.6 us (27%)
  blocking collectives  20.6 us (11%)
  other arithmetic  15.3 us (8%)
  between operations  14.2 us (7%)
  local copies, waits for them, and re-layouts  9.34 us (5%)
  starting transfers between devices  4.87 us (3%)
    reduce_scatter x1, waiting for transfers between devices, on_device(): lax.psum_scatter(parts, 'dp', scatter_dimension=2, tiled=True)  41.7 us
    all_gather x1, waiting for transfers between devices, on_device(): lax.all_gather(jnp.stack([hidden, d_up, d_gate]), 'dp', axis=2, tiled=True)  34.2 us
    all_to_all x1, blocking collectives, on_device(): recv = lax.all_to_all(send, ALL, 0, 0, tiled=True)  20.6 us
    pallas_call x1, Pallas kernels, forward_parts(): pl.pallas_call(_fwd_body, grid=(ff // tile,), in_specs=[pl.BlockSpec((row...  19.8 us
    pallas_call x1, Pallas kernels, backward_grads(): pl.pallas_call(_grads_body, grid=(ff // tile,), in_specs=[plane(2), plane...  17.2 us
    pallas_call x1, Pallas kernels, backward_rows(): pl.pallas_call(_rows_body, grid=(ff // tile,), in_specs=[plane(2), plane(...  15.6 us
    all_to_all x2, other arithmetic, on_device(): recv = lax.all_to_all(send, ALL, 0, 0, tiled=True)  5.26 us
    all_to_all x1, starting transfers between devices, on_device(): back = lax.all_to_all(back, ALL, 0, 0, tiled=True)  4.61 us
  transfers between devices with their start and end apart: 3, of which 2 were waited for; matrix products, arithmetic and copies ran while one was open for 0% of the time, Pallas kernels for 9%

profile of v11, /device:TPU:0, one launch (start us, length us, event | category | flops | bytes accessed | tf_op | source)
XLA Modules:
  0.0 192.9 jit_solution(3255205035063327330)
XLA Ops:
  7.2 0.0 reduce-scatter.2.cloned.1.call-start
  7.2 0.7 fusion.1
  8.0 0.8 select_reduce_fusion
  8.8 0.7 fusion.2
  9.5 1.0 maximum_bitcast_fusion
  10.5 0.3 copy.15
  10.8 0.3 broadcast_in_dim.2
  11.1 1.1 scatter_fusion
  12.2 0.2 reshape.38
  12.4 0.3 copy.23
  12.8 0.5 all_to_all.16
  13.3 0.5 broadcast.47
  13.8 2.9 %reduce.3 = bf16[32,6144]{1,0:T(8,128)(2,1)S(1)} reduce(bf16[32,1,6144]{2,1,0:T(2,128)(2,1)S(1)} %all_to_all.16, bf16[]{:T(256)} %broadcast.47), dimensions={1}, to_apply=%all_to_all.16.reduce_sub_computation | reduce | bytes 786434 | tf_op jit(solution)/shard_map/all_to_all | solution.py:161
  16.8 0.3 reshape.66
  17.0 20.6 %all_to_all.20 = bf16[32,2,3072]{2,1,0:T(2,128)(2,1)S(1)} all-to-all(bf16[32,2,3072]{2,1,0:T(2,128)(2,1)S(1)} %reshape.66), channel_id=1, replica_groups=mesh['dp'=4,'expert'=8] {'dp','expert'}, dimensions={0} | all-to-all | bytes 786432 | tf_op jit(solution)/shard_map/all_to_all | solution.py:161
  37.7 0.3 reshape.67
  38.0 2.3 %reduce = bf16[32,6144]{1,0:T(8,128)(2,1)S(1)} reduce(bf16[32,1,6144]{2,1,0:T(2,128)(2,1)S(1)} %reshape.67, bf16[]{:T(256)} %constant.19), dimensions={1}, to_apply=%all_to_all.13.reduce_sub_computation | reduce | bytes 786434 | tf_op jit(solution)/shard_map/all_to_all | solution.py:161
  40.3 0.6 reshape.39
  40.9 0.2 fusion.3
  41.1 0.8 reshape_squeeze.7.y_ref
  41.9 0.8 reshape_squeeze.6.x_ref
  42.8 19.8 %shard_map.93 = bf16[3,96,7168]{2,1,0:T(8,128)(2,1)} custom-call(bf16[96,1024]{1,0:T(8,128)(2,1)} %reshape_squeeze.6.x_ref, bf16[96,1024]{1,0:T(8,128)(2,1)} %reshape_squeeze.7.y_ref, bf16[1024,7168]{1,0:T(8,128)(2,1)} %wg_ref.3, bf16[1024,7168]{1,0:T(8,128)(2,1)} %wu_ref.3, bf16[7168,1024]{1,0:T(8,128)(2,1)} %wd_ref.1), custom_call_target="tpu_custom_call" | custom-call | flops 4227858432 | bytes 48562176 | tf_op jit(solution)/shard_map/pallas_call | solution.py:41
  62.5 0.0 reduce-scatter.2.cloned.1.call-update
  62.6 0.2 all-gather.2.cloned.1.call-start
  62.8 41.7 %reduce-scatter.2.cloned.1.call-done = bf16[3,96,1792]{2,1,0:T(8,128)(2,1)} async-done(((bf16[3,96,7168]{2,1,0:T(8,128)(2,1)}), bf16[3,96,1792]{2,1,0:T(8,128)(2,1)}) %reduce-scatter.2.cloned.1.call-update) | async-done | bytes 1032208 | tf_op jit(solution)/shard_map/reduce_scatter | solution.py:167
  104.5 1.4 convert_element_type.35
  105.9 0.4 multiply_convert_fusion.2
  106.2 1.1 pad_maximum_fusion
  107.3 0.0 all-gather.2.cloned.1.call-update
  107.3 34.2 %all-gather.2.cloned.1.call-done.dg_ref.du_ref.h_ref = bf16[3,96,7168]{2,1,0:T(8,128)(2,1)} async-done(((bf16[3,96,1792]{2,1,0:T(8,128)(2,1)}), bf16[3,96,7168]{2,1,0:T(8,128)(2,1)}) %all-gather.2.cloned.1.call-update) | async-done | bytes 4128784 | tf_op jit(solution)/shard_map/all_gather | solution.py:169
  141.6 15.6 %shard_map.94 = f32[1024,96]{1,0:T(8,128)} custom-call(bf16[3,96,7168]{2,1,0:T(8,128)(2,1)} %all-gather.2.cloned.1.call-done.dg_ref.du_ref.h_ref, bf16[3,96,7168]{2,1,0:T(8,128)(2,1)} %all-gather.2.cloned.1.call-done.dg_ref.du_ref.h_ref, bf16[1024,7168]{1,0:T(8,128)(2,1)} %wg_ref.3, bf16[1024,7168]{1,0:T(8,128)(2,1)} %wu_ref.3), custom_call_target="tpu_custom_call" | custom-call | flops 2818572288 | bytes 32505856 | tf_op jit(solution)/shard_map/pallas_call | solution.py:86
  157.2 1.1 convert_bitcast_fusion
  158.2 0.1 copy.18
  158.4 0.1 all_to_all.17
  158.5 1.8 reduce.4
  160.3 0.8 reshape.68
  161.1 4.6 %all-to-all-start.1 = ((bf16[32,2,1536]{2,1,0:T(2,128)(2,1)}), bf16[32,2,1536]{2,1,0:T(2,128)(2,1)S(1)}, u32[]{:S(2)}, u32[]{:S(2)}) async-start(bf16[32,2,1536]{2,1,0:T(2,128)(2,1)} %reshape.68), calls=%async_computation.2 | async-start | bytes 393216 | tf_op jit(solution)/shard_map/all_to_all | solution.py:173
  165.7 17.2 %shard_map.95 = (bf16[1024,7168]{1,0:T(8,128)(2,1)}, bf16[1024,7168]{1,0:T(8,128)(2,1)}, bf16[7168,1024]{1,0:T(8,128)(2,1)}) custom-call(bf16[3,96,7168]{2,1,0:T(8,128)(2,1)} %all-gather.2.cloned.1.call-done.dg_ref.du_ref.h_ref, bf16[3,96,7168]{2,1,0:T(8,128)(2,1)} %all-gather.2.cloned.1.call-done.dg_ref.du_ref.h_ref, ...), custom_call_target="tpu_custom_call" | custom-call | flops 4227858432 | bytes 48562176 | tf_op jit(solution)/shard_map/pallas_call | solution.py:113
  183.0 0.0 all-to-all-done.1
  183.0 0.1 reshape.69
  183.1 1.1 convert_reduce_fusion
  184.2 0.3 reshape.46
  184.5 0.2 copy.20
  184.7 0.1 copy.21
  184.8 1.3 gather_fusion
  (2 shorter events, 0.0 us)
Async XLA Ops:
  7.2 97.3 %reduce-scatter.2.cloned.1.call-start = ((), (), s32[]{:S(2)}) async-start(), calls=%async_computation.3 | async-start | bytes 5160960 | tf_op jit(solution)/shard_map/reduce_scatter | solution.py:167
  62.6 79.0 %all-gather.2.cloned.1.call-start = ((), (), s32[]{:S(2)}) async-start(), calls=%async_computation.4 | async-start | bytes 5160960 | tf_op jit(solution)/shard_map/all_gather | solution.py:169
  161.1 21.8 %all-to-all-start.1 = ((bf16[32,2,1536]{2,1,0:T(2,128)(2,1)}), bf16[32,2,1536]{2,1,0:T(2,128)(2,1)S(1)}, u32[]{:S(2)}, u32[]{:S(2)}) async-start(bf16[32,2,1536]{2,1,0:T(2,128)(2,1)} %reshape.68), calls=%async_computation.2 | async-start | bytes 393216 | tf_op jit(solution)/shard_map/all_to_all | solution.py:173
Sparse Core Ops, SparseCore 0:
  62.7 41.7 reduce-scatter.1
  107.5 34.0 all-gather.1

commit v12 on v11

--- a/solution.py
+++ b/solution.py
@@ -75,8 +75,8 @@
     gd_ref[...] = lax.dot_general(h_ref[...], y_ref[...], tn, preferred_element_type=jnp.float32).astype(gd_ref.dtype)
 
 
-def backward_rows(gathered, w_gate, w_up):
-    rows, ff = gathered.shape[1], gathered.shape[2]
+def backward_rows(pair, w_gate, w_up):
+    rows, ff = pair.shape[1], pair.shape[2]
     cols = w_gate.shape[0]
     tile = 1024 if ff % 1024 == 0 else ff
 
@@ -87,8 +87,8 @@
         _rows_body,
         grid=(ff // tile,),
         in_specs=[
-            plane(2),
             plane(1),
+            plane(0),
             pl.BlockSpec((cols, tile), lambda k: (0, k)),
             pl.BlockSpec((cols, tile), lambda k: (0, k)),
         ],
@@ -98,11 +98,11 @@
         cost_estimate=pl.CostEstimate(
             flops=4 * rows * ff * cols, transcendentals=0,
             bytes_accessed=2 * (2 * cols * ff + 2 * rows * ff) + 4 * rows * cols),
-    )(gathered, gathered, w_gate, w_up)
-
-
-def backward_grads(gathered, rows_in, rows_grad):
-    rows, ff = gathered.shape[1], gathered.shape[2]
+    )(pair, pair, w_gate, w_up)
+
+
+def backward_grads(pair, hidden, rows_in, rows_grad):
+    rows, ff = pair.shape[1], pair.shape[2]
     cols = rows_in.shape[1]
     tile = 1024 if ff % 1024 == 0 else ff
     bf = jnp.bfloat16
@@ -114,9 +114,9 @@
         _grads_body,
         grid=(ff // tile,),
         in_specs=[
-            plane(2),
             plane(1),
             plane(0),
+            pl.BlockSpec((None, rows, tile), lambda k: (0, 0, k)),
             pl.BlockSpec((rows, cols), lambda k: (0, 0)),
             pl.BlockSpec((rows, cols), lambda k: (0, 0)),
         ],
@@ -134,7 +134,7 @@
         cost_estimate=pl.CostEstimate(
             flops=6 * rows * ff * cols, transcendentals=0,
             bytes_accessed=2 * (3 * cols * ff + 3 * rows * ff + 2 * rows * cols)),
-    )(gathered, gathered, gathered, rows_in, rows_grad)
+    )(pair, pair, hidden, rows_in, rows_grad)
 
 
 def on_device(inputs, grad_out, labels, w_gate, w_up, w_down):
@@ -166,16 +166,17 @@
     parts = forward_parts(rows_in, rows_grad, w_gate, w_up, w_down)
     reduced = lax.psum_scatter(parts, "dp", scatter_dimension=2, tiled=True).astype(jnp.float32)
     hidden, d_up, d_gate = nonlinear(reduced[0], reduced[1], reduced[2])
-    gathered = lax.all_gather(jnp.stack([hidden, d_up, d_gate]), "dp", axis=2, tiled=True)
-
-    d_rows = backward_rows(gathered, w_gate, w_up).T
+    pair = lax.all_gather(jnp.stack([d_up, d_gate]), "dp", axis=2, tiled=True)
+    hidden = lax.all_gather(hidden[None], "dp", axis=2, tiled=True)
+
+    d_rows = backward_rows(pair, w_gate, w_up).T
     back = d_rows.astype(jnp.bfloat16).reshape(replicas * members, capacity * columns)
     back = lax.all_to_all(back, ALL, 0, 0, tiled=True)
     back = back.reshape(replicas, EXPERTS, group, capacity, columns).astype(jnp.float32)
     summed = jnp.sum(back, axis=2)
     summed = jnp.transpose(summed, (1, 2, 0, 3)).reshape(EXPERTS * capacity, width)
     grad_in = summed[slot_ids].astype(jnp.bfloat16)
-    grad_gate, grad_up, grad_down = backward_grads(gathered, rows_in, rows_grad)
+    grad_gate, grad_up, grad_down = backward_grads(pair, hidden, rows_in, rows_grad)
     return (grad_in, grad_gate, grad_up, grad_down)
 
 

time: 193 us -> 186 us (0.964)
  waiting for transfers between devices: 76 us -> 68.1 us
    all_gather x1 -> x2, waiting for transfers between devices: 34.2 us -> 25.7 us  [the longest x1 25.7 us: on_device(): pair = lax.all_gather(jnp.stack([d_up, d_gate]), 'dp', axis=2, tiled=True)]
  transfers between devices with their start and end apart: 3 -> 4, of which waited for: 2 -> 2; matrix products, arithmetic and copies ran while one was open for 0% -> 2% of each run, Pallas kernels for 9% -> 18%
where the time goes in v12:
time: 186 us
  waiting for transfers between devices  68.1 us (37%)
  Pallas kernels  52.8 us (28%)
  blocking collectives  20.6 us (11%)
  other arithmetic  15.8 us (8%)
  between operations  13.9 us (7%)
  local copies, waits for them, and re-layouts  9.34 us (5%)
  starting transfers between devices  4.92 us (3%)
    reduce_scatter x1, waiting for transfers between devices, on_device(): lax.psum_scatter(parts, 'dp', scatter_dimension=2, tiled=True)  41.9 us
    all_gather x1, waiting for transfers between devices, on_device(): pair = lax.all_gather(jnp.stack([d_up, d_gate]), 'dp', axis=2, tiled=True)  25.7 us
    all_to_all x1, blocking collectives, on_device(): recv = lax.all_to_all(send, ALL, 0, 0, tiled=True)  20.6 us
    pallas_call x1, Pallas kernels, forward_parts(): pl.pallas_call(_fwd_body, grid=(ff // tile,), in_specs=[pl.BlockSpec((row...  19.8 us
    pallas_call x1, Pallas kernels, backward_grads(): pl.pallas_call(_grads_body, grid=(ff // tile,), in_specs=[plane(1), plane...  17.2 us
    pallas_call x1, Pallas kernels, backward_rows(): pl.pallas_call(_rows_body, grid=(ff // tile,), in_specs=[plane(1), plane(...  15.8 us
    all_to_all x2, other arithmetic, on_device(): recv = lax.all_to_all(send, ALL, 0, 0, tiled=True)  5.26 us
    all_to_all x1, starting transfers between devices, on_device(): back = lax.all_to_all(back, ALL, 0, 0, tiled=True)  4.61 us
  transfers between devices with their start and end apart: 4, of which 2 were waited for; matrix products, arithmetic and copies ran while one was open for 2% of the time, Pallas kernels for 18%

profile of v12, /device:TPU:0, one launch (start us, length us, event | category | flops | bytes accessed | tf_op | source)
XLA Modules:
  0.0 185.6 jit_solution(1494389496189519084)
XLA Ops:
  7.2 0.0 reduce-scatter.2.cloned.1.call-start
  7.2 0.7 fusion.1
  8.0 0.8 select_reduce_fusion
  8.8 0.7 fusion.2
  9.5 1.0 maximum_bitcast_fusion
  10.5 0.3 copy.15
  10.8 0.3 broadcast_in_dim.2
  11.1 1.1 scatter_fusion
  12.2 0.2 reshape.38
  12.4 0.3 copy.23
  12.8 0.5 all_to_all.16
  13.3 0.5 broadcast.47
  13.8 2.9 %reduce.3 = bf16[32,6144]{1,0:T(8,128)(2,1)S(1)} reduce(bf16[32,1,6144]{2,1,0:T(2,128)(2,1)S(1)} %all_to_all.16, bf16[]{:T(256)} %broadcast.47), dimensions={1}, to_apply=%all_to_all.16.reduce_sub_computation | reduce | bytes 786434 | tf_op jit(solution)/shard_map/all_to_all | solution.py:161
  16.8 0.3 reshape.66
  17.0 20.6 %all_to_all.20 = bf16[32,2,3072]{2,1,0:T(2,128)(2,1)S(1)} all-to-all(bf16[32,2,3072]{2,1,0:T(2,128)(2,1)S(1)} %reshape.66), channel_id=1, replica_groups=mesh['dp'=4,'expert'=8] {'dp','expert'}, dimensions={0} | all-to-all | bytes 786432 | tf_op jit(solution)/shard_map/all_to_all | solution.py:161
  37.7 0.3 reshape.67
  38.0 2.3 %reduce = bf16[32,6144]{1,0:T(8,128)(2,1)S(1)} reduce(bf16[32,1,6144]{2,1,0:T(2,128)(2,1)S(1)} %reshape.67, bf16[]{:T(256)} %constant.19), dimensions={1}, to_apply=%all_to_all.13.reduce_sub_computation | reduce | bytes 786434 | tf_op jit(solution)/shard_map/all_to_all | solution.py:161
  40.3 0.6 reshape.39
  40.9 0.2 fusion.3
  41.1 0.8 reshape_squeeze.6.x_ref
  41.9 0.8 reshape_squeeze.7.y_ref
  42.8 19.8 %shard_map.93 = bf16[3,96,7168]{2,1,0:T(8,128)(2,1)} custom-call(bf16[96,1024]{1,0:T(8,128)(2,1)} %reshape_squeeze.6.x_ref, bf16[96,1024]{1,0:T(8,128)(2,1)} %reshape_squeeze.7.y_ref, bf16[1024,7168]{1,0:T(8,128)(2,1)} %wg_ref.3, bf16[1024,7168]{1,0:T(8,128)(2,1)} %wu_ref.3, bf16[7168,1024]{1,0:T(8,128)(2,1)} %wd_ref.1), custom_call_target="tpu_custom_call" | custom-call | flops 4227858432 | bytes 48562176 | tf_op jit(solution)/shard_map/pallas_call | solution.py:41
  62.5 0.0 reduce-scatter.2.cloned.1.call-update
  62.5 0.0 all-gather.3.cloned.1.call-start
  62.6 41.9 %reduce-scatter.2.cloned.1.call-done = bf16[3,96,1792]{2,1,0:T(8,128)(2,1)} async-done(((bf16[3,96,7168]{2,1,0:T(8,128)(2,1)}), bf16[3,96,1792]{2,1,0:T(8,128)(2,1)}) %reduce-scatter.2.cloned.1.call-update) | async-done | bytes 1032208 | tf_op jit(solution)/shard_map/reduce_scatter | solution.py:167
  104.5 1.4 convert_element_type.35
  105.9 1.1 multiply_convert_fusion
  107.0 0.9 pad_maximum_fusion
  107.9 0.0 all-gather.3.cloned.1.call-update
  107.9 0.2 all-gather.5.cloned.1.call-start
  108.1 0.5 all-gather.5.cloned.1.call-update
  108.6 25.7 %all-gather.3.cloned.1.call-done.dg_ref.du_ref = bf16[2,96,7168]{2,1,0:T(8,128)(2,1)} async-done(((bf16[2,96,1792]{2,1,0:T(8,128)(2,1)}), bf16[2,96,7168]{2,1,0:T(8,128)(2,1)}) %all-gather.3.cloned.1.call-update) | async-done | bytes 2752528 | tf_op jit(solution)/shard_map/all_gather | solution.py:169
  134.3 15.8 %shard_map.94 = f32[1024,96]{1,0:T(8,128)} custom-call(bf16[2,96,7168]{2,1,0:T(8,128)(2,1)} %all-gather.3.cloned.1.call-done.dg_ref.du_ref, bf16[2,96,7168]{2,1,0:T(8,128)(2,1)} %all-gather.3.cloned.1.call-done.dg_ref.du_ref, bf16[1024,7168]{1,0:T(8,128)(2,1)} %wg_ref.3, bf16[1024,7168]{1,0:T(8,128)(2,1)} %wu_ref.3), custom_call_target="tpu_custom_call" | custom-call | flops 2818572288 | bytes 32505856 | tf_op jit(solution)/shard_map/pallas_call | solution.py:86
  150.1 1.1 convert_bitcast_fusion
  151.2 0.1 copy.18
  151.3 0.1 all_to_all.17
  151.5 1.8 reduce.4
  153.3 0.8 reshape.68
  154.1 4.6 %all-to-all-start.1 = ((bf16[32,2,1536]{2,1,0:T(2,128)(2,1)}), bf16[32,2,1536]{2,1,0:T(2,128)(2,1)S(1)}, u32[]{:S(2)}, u32[]{:S(2)}) async-start(bf16[32,2,1536]{2,1,0:T(2,128)(2,1)} %reshape.68), calls=%async_computation.2 | async-start | bytes 393216 | tf_op jit(solution)/shard_map/all_to_all | solution.py:174
  158.7 0.0 all-gather.5.cloned.1.call-done.h_ref
  158.7 17.2 %shard_map.95 = (bf16[1024,7168]{1,0:T(8,128)(2,1)}, bf16[1024,7168]{1,0:T(8,128)(2,1)}, bf16[7168,1024]{1,0:T(8,128)(2,1)}) custom-call(bf16[2,96,7168]{2,1,0:T(8,128)(2,1)} %all-gather.3.cloned.1.call-done.dg_ref.du_ref, bf16[2,96,7168]{2,1,0:T(8,128)(2,1)} %all-gather.3.cloned.1.call-done.dg_ref.du_ref, ...), custom_call_target="tpu_custom_call" | custom-call | flops 4227858432 | bytes 48562176 | tf_op jit(solution)/shard_map/pallas_call | solution.py:113
  176.0 0.0 all-to-all-done.1
  176.0 0.1 reshape.69
  176.1 1.1 convert_reduce_fusion
  177.2 0.3 reshape.46
  177.5 0.2 copy.20
  177.7 0.1 copy.21
  177.8 1.3 gather_fusion
  (2 shorter events, 0.0 us)
Async XLA Ops:
  7.2 97.3 %reduce-scatter.2.cloned.1.call-start = ((), (), s32[]{:S(2)}) async-start(), calls=%async_computation.3 | async-start | bytes 5160960 | tf_op jit(solution)/shard_map/reduce_scatter | solution.py:167
  62.5 71.8 %all-gather.3.cloned.1.call-start = ((), (), s32[]{:S(2)}) async-start(), calls=%async_computation.4 | async-start | bytes 3440640 | tf_op jit(solution)/shard_map/all_gather | solution.py:169
  107.9 50.8 %all-gather.5.cloned.1.call-start = ((), (), s32[]{:S(2)}) async-start(), calls=%async_computation.5 | async-start | bytes 1720320 | tf_op jit(solution)/shard_map/all_gather | solution.py:170
  154.1 21.9 %all-to-all-start.1 = ((bf16[32,2,1536]{2,1,0:T(2,128)(2,1)}), bf16[32,2,1536]{2,1,0:T(2,128)(2,1)S(1)}, u32[]{:S(2)}, u32[]{:S(2)}) async-start(bf16[32,2,1536]{2,1,0:T(2,128)(2,1)} %reshape.68), calls=%async_computation.2 | async-start | bytes 393216 | tf_op jit(solution)/shard_map/all_to_all | solution.py:174
Sparse Core Ops, SparseCore 0:
  62.7 41.7 reduce-scatter.1
  108.0 26.2 all-gather.2
  136.6 18.5 all-gather.4

commit v13 on v12

--- a/solution.py
+++ b/solution.py
@@ -57,14 +57,18 @@
     )(rows_in, rows_grad, w_gate, w_up, w_down)
 
 
-def _rows_body(dg_ref, du_ref, wg_ref, wu_ref, drows_ref):
+def _rows_body(dg_ref, du_ref, wg_ref, wu_ref, out_ref, acc_ref):
     @pl.when(pl.program_id(0) == 0)
     def _():
-        drows_ref[...] = jnp.zeros_like(drows_ref)
+        acc_ref[...] = jnp.zeros_like(acc_ref)
     nt = (((1,), (1,)), ((), ()))
-    drows_ref[...] += lax.dot_general(
-        wg_ref[...], dg_ref[...], nt, preferred_element_type=jnp.float32
-    ) + lax.dot_general(wu_ref[...], du_ref[...], nt, preferred_element_type=jnp.float32)
+    acc_ref[...] += lax.dot_general(
+        dg_ref[...], wg_ref[...], nt, preferred_element_type=jnp.float32
+    ) + lax.dot_general(du_ref[...], wu_ref[...], nt, preferred_element_type=jnp.float32)
+
+    @pl.when(pl.program_id(0) == pl.num_programs(0) - 1)
+    def _():
+        out_ref[...] = acc_ref[...].astype(out_ref.dtype)
 
 
 def _grads_body(dg_ref, du_ref, h_ref, x_ref, y_ref, gg_ref, gu_ref, gd_ref):
@@ -92,8 +96,9 @@
             pl.BlockSpec((cols, tile), lambda k: (0, k)),
             pl.BlockSpec((cols, tile), lambda k: (0, k)),
         ],
-        out_specs=pl.BlockSpec((cols, rows), lambda k: (0, 0)),
-        out_shape=jax.ShapeDtypeStruct((cols, rows), jnp.float32),
+        out_specs=pl.BlockSpec((rows, cols), lambda k: (0, 0)),
+        out_shape=jax.ShapeDtypeStruct((rows, cols), jnp.bfloat16),
+        scratch_shapes=[pltpu.VMEM((rows, cols), jnp.float32)],
         compiler_params=pltpu.CompilerParams(dimension_semantics=("arbitrary",)),
         cost_estimate=pl.CostEstimate(
             flops=4 * rows * ff * cols, transcendentals=0,
@@ -169,7 +174,7 @@
     pair = lax.all_gather(jnp.stack([d_up, d_gate]), "dp", axis=2, tiled=True)
     hidden = lax.all_gather(hidden[None], "dp", axis=2, tiled=True)
 
-    d_rows = backward_rows(pair, w_gate, w_up).T
+    d_rows = backward_rows(pair, w_gate, w_up)
     back = d_rows.astype(jnp.bfloat16).reshape(replicas * members, capacity * columns)
     back = lax.all_to_all(back, ALL, 0, 0, tiled=True)
     back = back.reshape(replicas, EXPERTS, group, capacity, columns).astype(jnp.float32)

time: 186 us -> 187 us (level)
  transfers between devices with their start and end apart: 4 -> 4, of which waited for: 2 -> 2; matrix products, arithmetic and copies ran while one was open for 2% -> 1% of each run, Pallas kernels for 18% -> 18%
where the time goes in v13:
time: 187 us; the launch traced here: 186 us
  waiting for transfers between devices  68.1 us (36%)
  Pallas kernels  53.3 us (29%)
  blocking collectives  20.6 us (11%)
  other arithmetic  14.8 us (8%)
  between operations  13.9 us (7%)
  local copies, waits for them, and re-layouts  10.5 us (6%)
  starting transfers between devices  4.9 us (3%)
    reduce_scatter x1, waiting for transfers between devices, on_device(): lax.psum_scatter(parts, 'dp', scatter_dimension=2, tiled=True)  41.9 us
    all_gather x1, waiting for transfers between devices, on_device(): pair = lax.all_gather(jnp.stack([d_up, d_gate]), 'dp', axis=2, tiled=True)  25.7 us
    all_to_all x1, blocking collectives, on_device(): recv = lax.all_to_all(send, ALL, 0, 0, tiled=True)  20.6 us
    pallas_call x1, Pallas kernels, forward_parts(): pl.pallas_call(_fwd_body, grid=(ff // tile,), in_specs=[pl.BlockSpec((row...  19.8 us
    pallas_call x1, Pallas kernels, backward_grads(): pl.pallas_call(_grads_body, grid=(ff // tile,), in_specs=[plane(1), plane...  17.2 us
    pallas_call x1, Pallas kernels, backward_rows(): pl.pallas_call(_rows_body, grid=(ff // tile,), in_specs=[plane(1), plane(...  16.4 us
    all_to_all x2, other arithmetic, on_device(): recv = lax.all_to_all(send, ALL, 0, 0, tiled=True)  5.26 us
    all_to_all x1, starting transfers between devices, on_device(): back = lax.all_to_all(back, ALL, 0, 0, tiled=True)  4.6 us
  transfers between devices with their start and end apart: 4, of which 2 were waited for; matrix products, arithmetic and copies ran while one was open for 1% of the time, Pallas kernels for 18%

profile of v13, /device:TPU:0, one launch (start us, length us, event | category | flops | bytes accessed | tf_op | source)
XLA Modules:
  0.0 186.3 jit_solution(7684826608648884191)
XLA Ops:
  7.2 0.0 reduce-scatter.2.cloned.1.call-start
  7.2 0.7 fusion.1
  8.0 0.8 select_reduce_fusion
  8.8 0.7 fusion.2
  9.5 1.0 maximum_bitcast_fusion
  10.5 0.3 copy.20
  10.8 0.3 broadcast_in_dim.2
  11.1 1.1 scatter_fusion
  12.2 0.2 reshape.38
  12.4 0.3 copy.27
  12.8 0.5 all_to_all.16
  13.3 0.5 broadcast.47
  13.8 2.9 %reduce.3 = bf16[32,6144]{1,0:T(8,128)(2,1)S(1)} reduce(bf16[32,1,6144]{2,1,0:T(2,128)(2,1)S(1)} %all_to_all.16, bf16[]{:T(256)} %broadcast.47), dimensions={1}, to_apply=%all_to_all.16.reduce_sub_computation | reduce | bytes 786434 | tf_op jit(solution)/shard_map/all_to_all | solution.py:166
  16.8 0.3 reshape.66
  17.0 20.6 %all_to_all.20 = bf16[32,2,3072]{2,1,0:T(2,128)(2,1)S(1)} all-to-all(bf16[32,2,3072]{2,1,0:T(2,128)(2,1)S(1)} %reshape.66), channel_id=1, replica_groups=mesh['dp'=4,'expert'=8] {'dp','expert'}, dimensions={0} | all-to-all | bytes 786432 | tf_op jit(solution)/shard_map/all_to_all | solution.py:166
  37.7 0.3 reshape.67
  38.0 2.3 %reduce = bf16[32,6144]{1,0:T(8,128)(2,1)S(1)} reduce(bf16[32,1,6144]{2,1,0:T(2,128)(2,1)S(1)} %reshape.67, bf16[]{:T(256)} %constant.19), dimensions={1}, to_apply=%all_to_all.13.reduce_sub_computation | reduce | bytes 786434 | tf_op jit(solution)/shard_map/all_to_all | solution.py:166
  40.3 0.6 reshape.39
  40.9 0.2 fusion.3
  41.1 0.8 reshape_squeeze.6.x_ref
  41.9 0.8 reshape_squeeze.7.y_ref
  42.8 19.8 %shard_map.93 = bf16[3,96,7168]{2,1,0:T(8,128)(2,1)} custom-call(bf16[96,1024]{1,0:T(8,128)(2,1)} %reshape_squeeze.6.x_ref, bf16[96,1024]{1,0:T(8,128)(2,1)} %reshape_squeeze.7.y_ref, bf16[1024,7168]{1,0:T(8,128)(2,1)} %wg_ref.3, bf16[1024,7168]{1,0:T(8,128)(2,1)} %wu_ref.3, bf16[7168,1024]{1,0:T(8,128)(2,1)} %wd_ref.1), custom_call_target="tpu_custom_call" | custom-call | flops 4227858432 | bytes 48562176 | tf_op jit(solution)/shard_map/pallas_call | solution.py:41
  62.5 0.0 reduce-scatter.2.cloned.1.call-update
  62.5 0.0 all-gather.3.cloned.1.call-start
  62.6 41.9 %reduce-scatter.2.cloned.1.call-done = bf16[3,96,1792]{2,1,0:T(8,128)(2,1)} async-done(((bf16[3,96,7168]{2,1,0:T(8,128)(2,1)}), bf16[3,96,1792]{2,1,0:T(8,128)(2,1)}) %reduce-scatter.2.cloned.1.call-update) | async-done | bytes 1032208 | tf_op jit(solution)/shard_map/reduce_scatter | solution.py:172
  104.5 1.4 convert_element_type.29
  105.9 1.1 multiply_convert_fusion
  107.0 0.9 pad_maximum_fusion
  107.9 0.0 all-gather.3.cloned.1.call-update
  107.9 0.2 all-gather.5.cloned.1.call-start
  108.1 0.5 all-gather.5.cloned.1.call-update
  108.6 25.7 %all-gather.3.cloned.1.call-done.dg_ref.du_ref = bf16[2,96,7168]{2,1,0:T(8,128)(2,1)} async-done(((bf16[2,96,1792]{2,1,0:T(8,128)(2,1)}), bf16[2,96,7168]{2,1,0:T(8,128)(2,1)}) %all-gather.3.cloned.1.call-update) | async-done | bytes 2752528 | tf_op jit(solution)/shard_map/all_gather | solution.py:174
  134.3 16.4 %shard_map.94 = bf16[96,1024]{1,0:T(8,128)(2,1)} custom-call(bf16[2,96,7168]{2,1,0:T(8,128)(2,1)} %all-gather.3.cloned.1.call-done.dg_ref.du_ref, bf16[2,96,7168]{2,1,0:T(8,128)(2,1)} %all-gather.3.cloned.1.call-done.dg_ref.du_ref, bf16[1024,7168]{1,0:T(8,128)(2,1)} %wg_ref.3, bf16[1024,7168]{1,0:T(8,128)(2,1)} %wu_ref.3), custom_call_target="tpu_custom_call" | custom-call | flops 2818572288 | bytes 32505856 | tf_op jit(solution)/shard_map/pallas_call | solution.py:90
  150.7 1.5 all_to_all.17
  152.2 1.8 reduce.4
  154.0 0.8 reshape.68
  154.8 4.6 %all-to-all-start.1 = ((bf16[32,2,1536]{2,1,0:T(2,128)(2,1)}), bf16[32,2,1536]{2,1,0:T(2,128)(2,1)S(1)}, u32[]{:S(2)}, u32[]{:S(2)}) async-start(bf16[32,2,1536]{2,1,0:T(2,128)(2,1)} %reshape.68), calls=%async_computation.2 | async-start | bytes 393216 | tf_op jit(solution)/shard_map/all_to_all | solution.py:179
  159.4 0.0 all-gather.5.cloned.1.call-done.h_ref
  159.4 17.2 %shard_map.95 = (bf16[1024,7168]{1,0:T(8,128)(2,1)}, bf16[1024,7168]{1,0:T(8,128)(2,1)}, bf16[7168,1024]{1,0:T(8,128)(2,1)}) custom-call(bf16[2,96,7168]{2,1,0:T(8,128)(2,1)} %all-gather.3.cloned.1.call-done.dg_ref.du_ref, bf16[2,96,7168]{2,1,0:T(8,128)(2,1)} %all-gather.3.cloned.1.call-done.dg_ref.du_ref, ...), custom_call_target="tpu_custom_call" | custom-call | flops 4227858432 | bytes 48562176 | tf_op jit(solution)/shard_map/pallas_call | solution.py:118
  176.6 0.0 all-to-all-done.1
  176.6 0.1 reshape.69
  176.8 1.1 convert_reduce_fusion
  177.9 0.3 reshape.46
  178.2 0.2 copy.24
  178.4 0.1 copy.25
  178.5 1.3 gather_fusion
  (2 shorter events, 0.0 us)
Async XLA Ops:
  7.2 97.3 %reduce-scatter.2.cloned.1.call-start = ((), (), s32[]{:S(2)}) async-start(), calls=%async_computation.3 | async-start | bytes 5160960 | tf_op jit(solution)/shard_map/reduce_scatter | solution.py:172
  62.5 71.8 %all-gather.3.cloned.1.call-start = ((), (), s32[]{:S(2)}) async-start(), calls=%async_computation.4 | async-start | bytes 3440640 | tf_op jit(solution)/shard_map/all_gather | solution.py:174
  107.9 51.5 %all-gather.5.cloned.1.call-start = ((), (), s32[]{:S(2)}) async-start(), calls=%async_computation.5 | async-start | bytes 1720320 | tf_op jit(solution)/shard_map/all_gather | solution.py:175
  154.8 21.9 %all-to-all-start.1 = ((bf16[32,2,1536]{2,1,0:T(2,128)(2,1)}), bf16[32,2,1536]{2,1,0:T(2,128)(2,1)S(1)}, u32[]{:S(2)}, u32[]{:S(2)}) async-start(bf16[32,2,1536]{2,1,0:T(2,128)(2,1)} %reshape.68), calls=%async_computation.2 | async-start | bytes 393216 | tf_op jit(solution)/shard_map/all_to_all | solution.py:179
Sparse Core Ops, SparseCore 0:
  62.7 41.7 reduce-scatter.1
  108.0 26.2 all-gather.2
  136.6 18.5 all-gather.4

commit v14 on v12

--- a/solution.py
+++ b/solution.py
@@ -22,6 +22,28 @@
     return lax.dot_general(
         left, right, (((0,), (0,)), ((), ())), preferred_element_type=jnp.float32
     )
+
+
+def _nonlinear_body(r_ref, pair_ref, h_ref):
+    gate = r_ref[0].astype(jnp.float32)
+    up = r_ref[1].astype(jnp.float32)
+    dhid = r_ref[2].astype(jnp.float32)
+    sig = 1.0 / (1.0 + jnp.exp(-gate))
+    act = gate * sig
+    h_ref[0] = (act * up).astype(h_ref.dtype)
+    pair_ref[0] = (dhid * act).astype(pair_ref.dtype)
+    pair_ref[1] = (dhid * up * sig * (1.0 + gate * (1.0 - sig))).astype(pair_ref.dtype)
+
+
+def nonlinear_stacks(reduced):
+    _, rows, n = reduced.shape
+    return pl.pallas_call(
+        _nonlinear_body,
+        out_shape=[
+            jax.ShapeDtypeStruct((2, rows, n), jnp.bfloat16),
+            jax.ShapeDtypeStruct((1, rows, n), jnp.bfloat16),
+        ],
+    )(reduced)
 
 
 def _fwd_body(x_ref, y_ref, wg_ref, wu_ref, wd_ref, out_ref):
@@ -164,10 +186,10 @@
     rows_grad = recv[:, 1].reshape(-1, columns)
 
     parts = forward_parts(rows_in, rows_grad, w_gate, w_up, w_down)
-    reduced = lax.psum_scatter(parts, "dp", scatter_dimension=2, tiled=True).astype(jnp.float32)
-    hidden, d_up, d_gate = nonlinear(reduced[0], reduced[1], reduced[2])
-    pair = lax.all_gather(jnp.stack([d_up, d_gate]), "dp", axis=2, tiled=True)
-    hidden = lax.all_gather(hidden[None], "dp", axis=2, tiled=True)
+    reduced = lax.psum_scatter(parts, "dp", scatter_dimension=2, tiled=True)
+    pair, hidden = nonlinear_stacks(reduced)
+    pair = lax.all_gather(pair, "dp", axis=2, tiled=True)
+    hidden = lax.all_gather(hidden, "dp", axis=2, tiled=True)
 
     d_rows = backward_rows(pair, w_gate, w_up).T
     back = d_rows.astype(jnp.bfloat16).reshape(replicas * members, capacity * columns)

time: 186 us -> 185 us (level)
  other arithmetic: 15.8 us -> 12.5 us
  Pallas kernels: 52.8 us -> 55.3 us
    pallas_call x0 -> x1, Pallas kernels: none -> 2.54 us  [nonlinear_stacks(): pl.pallas_call(_nonlinear_body, out_shape=[jax.ShapeDtypeStruct((2, rows,...]
    convert_element_type x2 -> x0, other arithmetic: 2.46 us -> none  [the longest x1 1.37 us: on_device(): lax.psum_scatter(parts, 'dp', scatter_dimension=2, tiled=True)]
where the time goes in v14:
time: 185 us
  waiting for transfers between devices  68.1 us (37%)
  Pallas kernels  55.3 us (30%)
  blocking collectives  20.6 us (11%)
  between operations  13.9 us (8%)
  other arithmetic  12.5 us (7%)
  local copies, waits for them, and re-layouts  9.34 us (5%)
  starting transfers between devices  4.92 us (3%)
    reduce_scatter x1, waiting for transfers between devices, on_device(): reduced = lax.psum_scatter(parts, 'dp', scatter_dimension=2, tiled=True)  41.9 us
    all_gather x1, waiting for transfers between devices, on_device(): pair = lax.all_gather(pair, 'dp', axis=2, tiled=True)  25.7 us
    all_to_all x1, blocking collectives, on_device(): recv = lax.all_to_all(send, ALL, 0, 0, tiled=True)  20.6 us
    pallas_call x1, Pallas kernels, forward_parts(): pl.pallas_call(_fwd_body, grid=(ff // tile,), in_specs=[pl.BlockSpec((row...  19.8 us
    pallas_call x1, Pallas kernels, backward_grads(): pl.pallas_call(_grads_body, grid=(ff // tile,), in_specs=[plane(1), plane...  17.2 us
    pallas_call x1, Pallas kernels, backward_rows(): pl.pallas_call(_rows_body, grid=(ff // tile,), in_specs=[plane(1), plane(...  15.8 us
    all_to_all x2, other arithmetic, on_device(): recv = lax.all_to_all(send, ALL, 0, 0, tiled=True)  5.26 us
    all_to_all x1, starting transfers between devices, on_device(): back = lax.all_to_all(back, ALL, 0, 0, tiled=True)  4.62 us
  transfers between devices with their start and end apart: 4, of which 2 were waited for; matrix products, arithmetic and copies ran while one was open for 2% of the time, Pallas kernels for 18%

profile of v14, /device:TPU:0, one launch (start us, length us, event | category | flops | bytes accessed | tf_op | source)
XLA Modules:
  0.0 184.8 jit_solution(14553711195816348932)
XLA Ops:
  7.2 0.0 reduce-scatter.2.cloned.1.call-start
  7.2 0.7 fusion
  8.0 0.8 select_reduce_fusion
  8.8 0.7 fusion.1
  9.5 1.0 maximum_bitcast_fusion
  10.5 0.3 copy.15
  10.8 0.3 broadcast_in_dim.2
  11.1 1.1 scatter_fusion
  12.2 0.2 reshape.38
  12.4 0.3 copy.23
  12.8 0.5 all_to_all.16
  13.3 0.5 broadcast.29
  13.8 2.9 %reduce.3 = bf16[32,6144]{1,0:T(8,128)(2,1)S(1)} reduce(bf16[32,1,6144]{2,1,0:T(2,128)(2,1)S(1)} %all_to_all.16, bf16[]{:T(256)} %broadcast.29), dimensions={1}, to_apply=%all_to_all.16.reduce_sub_computation | reduce | bytes 786434 | tf_op jit(solution)/shard_map/all_to_all | solution.py:183
  16.8 0.3 reshape.66
  17.0 20.6 %all_to_all.20 = bf16[32,2,3072]{2,1,0:T(2,128)(2,1)S(1)} all-to-all(bf16[32,2,3072]{2,1,0:T(2,128)(2,1)S(1)} %reshape.66), channel_id=1, replica_groups=mesh['dp'=4,'expert'=8] {'dp','expert'}, dimensions={0} | all-to-all | bytes 786432 | tf_op jit(solution)/shard_map/all_to_all | solution.py:183
  37.7 0.3 reshape.67
  38.0 2.3 %reduce = bf16[32,6144]{1,0:T(8,128)(2,1)S(1)} reduce(bf16[32,1,6144]{2,1,0:T(2,128)(2,1)S(1)} %reshape.67, bf16[]{:T(256)} %constant.17), dimensions={1}, to_apply=%all_to_all.13.reduce_sub_computation | reduce | bytes 786434 | tf_op jit(solution)/shard_map/all_to_all | solution.py:183
  40.3 0.6 reshape.39
  40.9 0.2 fusion.2
  41.1 0.8 reshape_squeeze.6.x_ref
  41.9 0.8 reshape_squeeze.7.y_ref
  42.8 19.8 %shard_map.93 = bf16[3,96,7168]{2,1,0:T(8,128)(2,1)} custom-call(bf16[96,1024]{1,0:T(8,128)(2,1)} %reshape_squeeze.6.x_ref, bf16[96,1024]{1,0:T(8,128)(2,1)} %reshape_squeeze.7.y_ref, bf16[1024,7168]{1,0:T(8,128)(2,1)} %wg_ref.3, bf16[1024,7168]{1,0:T(8,128)(2,1)} %wu_ref.3, bf16[7168,1024]{1,0:T(8,128)(2,1)} %wd_ref.1), custom_call_target="tpu_custom_call" | custom-call | flops 4227858432 | bytes 48562176 | tf_op jit(solution)/shard_map/pallas_call | solution.py:63
  62.5 0.0 reduce-scatter.2.cloned.1.call-update
  62.5 0.0 all-gather.3.cloned.1.call-start
  62.6 41.9 %reduce-scatter.2.cloned.1.call-done.r_ref = bf16[3,96,1792]{2,1,0:T(8,128)(2,1)} async-done(((bf16[3,96,7168]{2,1,0:T(8,128)(2,1)}), bf16[3,96,1792]{2,1,0:T(8,128)(2,1)}) %reduce-scatter.2.cloned.1.call-update) | async-done | bytes 1032208 | tf_op jit(solution)/shard_map/reduce_scatter | solution.py:189
  104.5 2.5 %shard_map.94 = (bf16[2,96,1792]{2,1,0:T(8,128)(2,1)}, bf16[1,96,1792]{2,1,0:T(8,128)(2,1)}) custom-call(bf16[3,96,1792]{2,1,0:T(8,128)(2,1)} %reduce-scatter.2.cloned.1.call-done.r_ref), custom_call_target="tpu_custom_call" | custom-call | tf_op jit(solution)/shard_map/pallas_call | solution.py:40
  107.0 0.0 all-gather.3.cloned.1.call-update
  107.0 0.2 all-gather.5.cloned.1.call-start
  107.3 0.5 all-gather.5.cloned.1.call-update
  107.8 25.7 %all-gather.3.cloned.1.call-done.dg_ref.du_ref = bf16[2,96,7168]{2,1,0:T(8,128)(2,1)} async-done(((bf16[2,96,1792]{2,1,0:T(8,128)(2,1)}), bf16[2,96,7168]{2,1,0:T(8,128)(2,1)}) %all-gather.3.cloned.1.call-update) | async-done | bytes 2752528 | tf_op jit(solution)/shard_map/all_gather | solution.py:191
  133.5 15.8 %shard_map.95 = f32[1024,96]{1,0:T(8,128)} custom-call(bf16[2,96,7168]{2,1,0:T(8,128)(2,1)} %all-gather.3.cloned.1.call-done.dg_ref.du_ref, bf16[2,96,7168]{2,1,0:T(8,128)(2,1)} %all-gather.3.cloned.1.call-done.dg_ref.du_ref, bf16[1024,7168]{1,0:T(8,128)(2,1)} %wg_ref.3, bf16[1024,7168]{1,0:T(8,128)(2,1)} %wu_ref.3), custom_call_target="tpu_custom_call" | custom-call | flops 2818572288 | bytes 32505856 | tf_op jit(solution)/shard_map/pallas_call | solution.py:108
  149.3 1.1 convert_bitcast_fusion
  150.3 0.1 copy.18
  150.5 0.1 all_to_all.17
  150.6 1.8 reduce.4
  152.4 0.8 reshape.68
  153.2 4.6 %all-to-all-start.1 = ((bf16[32,2,1536]{2,1,0:T(2,128)(2,1)}), bf16[32,2,1536]{2,1,0:T(2,128)(2,1)S(1)}, u32[]{:S(2)}, u32[]{:S(2)}) async-start(bf16[32,2,1536]{2,1,0:T(2,128)(2,1)} %reshape.68), calls=%async_computation.2 | async-start | bytes 393216 | tf_op jit(solution)/shard_map/all_to_all | solution.py:196
  157.9 0.0 all-gather.5.cloned.1.call-done.h_ref
  157.9 17.2 %shard_map.96 = (bf16[1024,7168]{1,0:T(8,128)(2,1)}, bf16[1024,7168]{1,0:T(8,128)(2,1)}, bf16[7168,1024]{1,0:T(8,128)(2,1)}) custom-call(bf16[2,96,7168]{2,1,0:T(8,128)(2,1)} %all-gather.3.cloned.1.call-done.dg_ref.du_ref, bf16[2,96,7168]{2,1,0:T(8,128)(2,1)} %all-gather.3.cloned.1.call-done.dg_ref.du_ref, ...), custom_call_target="tpu_custom_call" | custom-call | flops 4227858432 | bytes 48562176 | tf_op jit(solution)/shard_map/pallas_call | solution.py:135
  175.1 0.0 all-to-all-done.1
  175.1 0.1 reshape.69
  175.3 1.1 convert_reduce_fusion
  176.4 0.3 reshape.46
  176.7 0.2 copy.20
  176.9 0.1 copy.21
  176.9 1.3 gather_fusion
  (2 shorter events, 0.0 us)
Async XLA Ops:
  7.2 97.3 %reduce-scatter.2.cloned.1.call-start = ((), (), s32[]{:S(2)}) async-start(), calls=%async_computation.3 | async-start | bytes 5160960 | tf_op jit(solution)/shard_map/reduce_scatter | solution.py:189
  62.5 71.0 %all-gather.3.cloned.1.call-start = ((), (), s32[]{:S(2)}) async-start(), calls=%async_computation.4 | async-start | bytes 3440640 | tf_op jit(solution)/shard_map/all_gather | solution.py:191
  107.0 50.8 %all-gather.5.cloned.1.call-start = ((), (), s32[]{:S(2)}) async-start(), calls=%async_computation.5 | async-start | bytes 1720320 | tf_op jit(solution)/shard_map/all_gather | solution.py:192
  153.2 21.9 %all-to-all-start.1 = ((bf16[32,2,1536]{2,1,0:T(2,128)(2,1)}), bf16[32,2,1536]{2,1,0:T(2,128)(2,1)S(1)}, u32[]{:S(2)}, u32[]{:S(2)}) async-start(bf16[32,2,1536]{2,1,0:T(2,128)(2,1)} %reshape.68), calls=%async_computation.2 | async-start | bytes 393216 | tf_op jit(solution)/shard_map/all_to_all | solution.py:196
Sparse Core Ops, SparseCore 0:
  62.7 41.7 reduce-scatter.1
  107.2 26.2 all-gather.2
  135.7 18.5 all-gather.4

commit v15 on v14

--- a/solution.py
+++ b/solution.py
@@ -179,7 +179,7 @@
     send = jnp.transpose(send, (3, 1, 0, 2, 4))
     send = jnp.broadcast_to(
         send[:, :, None], (replicas, EXPERTS, group, 2, capacity, columns)
-    ).reshape(replicas * members, 2 * capacity * columns)
+    ).reshape(replicas * members, 2, capacity * columns)
     recv = lax.all_to_all(send, ALL, 0, 0, tiled=True)
     recv = recv.reshape(replicas * members, 2, capacity, columns)
     rows_in = recv[:, 0].reshape(-1, columns)

time: 185 us -> 180 us (0.973)
  other arithmetic: 12.5 us -> 7.21 us
    all_to_all x2 -> x0, other arithmetic: 5.26 us -> none  [on_device(): recv = lax.all_to_all(send, ALL, 0, 0, tiled=True)]
where the time goes in v15:
time: 180 us
  waiting for transfers between devices  68.3 us (38%)
  Pallas kernels  55.3 us (31%)
  blocking collectives  20.6 us (11%)
  between operations  13.9 us (8%)
  local copies, waits for them, and re-layouts  9.23 us (5%)
  other arithmetic  7.21 us (4%)
  starting transfers between devices  4.92 us (3%)
    reduce_scatter x1, waiting for transfers between devices, on_device(): reduced = lax.psum_scatter(parts, 'dp', scatter_dimension=2, tiled=True)  41.9 us
    all_gather x1, waiting for transfers between devices, on_device(): pair = lax.all_gather(pair, 'dp', axis=2, tiled=True)  25.7 us
    all_to_all x1, blocking collectives, on_device(): recv = lax.all_to_all(send, ALL, 0, 0, tiled=True)  20.6 us
    pallas_call x1, Pallas kernels, forward_parts(): pl.pallas_call(_fwd_body, grid=(ff // tile,), in_specs=[pl.BlockSpec((row...  19.8 us
    pallas_call x1, Pallas kernels, backward_grads(): pl.pallas_call(_grads_body, grid=(ff // tile,), in_specs=[plane(1), plane...  17.2 us
    pallas_call x1, Pallas kernels, backward_rows(): pl.pallas_call(_rows_body, grid=(ff // tile,), in_specs=[plane(1), plane(...  15.8 us
    all_to_all x1, starting transfers between devices, on_device(): back = lax.all_to_all(back, ALL, 0, 0, tiled=True)  4.8 us
  transfers between devices with their start and end apart: 4, of which 2 were waited for; matrix products, arithmetic and copies ran while one was open for 2% of the time, Pallas kernels for 18%

profile of v15, /device:TPU:0, one launch (start us, length us, event | category | flops | bytes accessed | tf_op | source)
XLA Modules:
  0.0 179.5 jit_solution(15953951639092918318)
XLA Ops:
  7.2 0.0 reduce-scatter.2.cloned.1.call-start
  7.2 0.7 fusion
  8.0 0.8 select_reduce_fusion
  8.8 0.7 fusion.1
  9.5 1.0 maximum_bitcast_fusion
  10.5 0.3 copy.15
  10.8 0.3 broadcast_in_dim.2
  11.1 1.1 scatter_fusion
  12.2 0.2 reshape.34
  12.4 0.3 copy.24
  12.8 0.5 reshape_broadcast_in_dim.3
  13.3 0.4 copy.17
  13.7 20.6 %all_to_all.15 = bf16[32,2,3072]{2,1,0:T(2,128)(2,1)S(1)} all-to-all(bf16[32,2,3072]{2,1,0:T(2,128)(2,1)S(1)} %copy.17), channel_id=1, replica_groups=mesh['dp'=4,'expert'=8] {'dp','expert'}, dimensions={0} | all-to-all | bytes 786432 | tf_op jit(solution)/shard_map/all_to_all | solution.py:183
  34.4 0.1 copy.18
  34.4 0.6 reshape.35
  35.0 0.2 fusion.2
  35.2 0.8 reshape_squeeze.6.x_ref
  36.0 0.8 reshape_squeeze.7.y_ref
  36.9 19.8 %shard_map.93 = bf16[3,96,7168]{2,1,0:T(8,128)(2,1)} custom-call(bf16[96,1024]{1,0:T(8,128)(2,1)} %reshape_squeeze.6.x_ref, bf16[96,1024]{1,0:T(8,128)(2,1)} %reshape_squeeze.7.y_ref, bf16[1024,7168]{1,0:T(8,128)(2,1)} %wg_ref.3, bf16[1024,7168]{1,0:T(8,128)(2,1)} %wu_ref.3, bf16[7168,1024]{1,0:T(8,128)(2,1)} %wd_ref.1), custom_call_target="tpu_custom_call" | custom-call | flops 4227858432 | bytes 48562176 | tf_op jit(solution)/shard_map/pallas_call | solution.py:63
  56.6 0.0 reduce-scatter.2.cloned.1.call-update
  56.6 0.0 all-gather.3.cloned.1.call-start
  56.7 41.9 %reduce-scatter.2.cloned.1.call-done.r_ref = bf16[3,96,1792]{2,1,0:T(8,128)(2,1)} async-done(((bf16[3,96,7168]{2,1,0:T(8,128)(2,1)}), bf16[3,96,1792]{2,1,0:T(8,128)(2,1)}) %reduce-scatter.2.cloned.1.call-update) | async-done | bytes 1032208 | tf_op jit(solution)/shard_map/reduce_scatter | solution.py:189
  98.6 2.5 %shard_map.94 = (bf16[2,96,1792]{2,1,0:T(8,128)(2,1)}, bf16[1,96,1792]{2,1,0:T(8,128)(2,1)}) custom-call(bf16[3,96,1792]{2,1,0:T(8,128)(2,1)} %reduce-scatter.2.cloned.1.call-done.r_ref), custom_call_target="tpu_custom_call" | custom-call | tf_op jit(solution)/shard_map/pallas_call | solution.py:40
  101.1 0.0 all-gather.3.cloned.1.call-update
  101.1 0.0 all-gather.5.cloned.1.call-start
  101.2 0.7 all-gather.5.cloned.1.call-update
  101.9 25.7 %all-gather.3.cloned.1.call-done.dg_ref.du_ref = bf16[2,96,7168]{2,1,0:T(8,128)(2,1)} async-done(((bf16[2,96,1792]{2,1,0:T(8,128)(2,1)}), bf16[2,96,7168]{2,1,0:T(8,128)(2,1)}) %all-gather.3.cloned.1.call-update) | async-done | bytes 2752528 | tf_op jit(solution)/shard_map/all_gather | solution.py:191
  127.6 15.8 %shard_map.95 = f32[1024,96]{1,0:T(8,128)} custom-call(bf16[2,96,7168]{2,1,0:T(8,128)(2,1)} %all-gather.3.cloned.1.call-done.dg_ref.du_ref, bf16[2,96,7168]{2,1,0:T(8,128)(2,1)} %all-gather.3.cloned.1.call-done.dg_ref.du_ref, bf16[1024,7168]{1,0:T(8,128)(2,1)} %wg_ref.3, bf16[1024,7168]{1,0:T(8,128)(2,1)} %wu_ref.3), custom_call_target="tpu_custom_call" | custom-call | flops 2818572288 | bytes 32505856 | tf_op jit(solution)/shard_map/pallas_call | solution.py:108
  143.4 1.1 convert_bitcast_fusion
  144.4 0.1 copy.19
  144.6 0.1 all_to_all.12
  144.7 0.5 broadcast.28
  145.3 1.8 reduce.2
  147.0 0.8 reshape.61
  147.8 4.8 %all-to-all-start.1 = ((bf16[32,2,1536]{2,1,0:T(2,128)(2,1)}), bf16[32,2,1536]{2,1,0:T(2,128)(2,1)S(1)}, u32[]{:S(2)}, u32[]{:S(2)}) async-start(bf16[32,2,1536]{2,1,0:T(2,128)(2,1)} %reshape.61), calls=%async_computation.2 | async-start | bytes 393216 | tf_op jit(solution)/shard_map/all_to_all | solution.py:196
  152.7 0.0 all-gather.5.cloned.1.call-done.h_ref
  152.7 17.2 %shard_map.96 = (bf16[1024,7168]{1,0:T(8,128)(2,1)}, bf16[1024,7168]{1,0:T(8,128)(2,1)}, bf16[7168,1024]{1,0:T(8,128)(2,1)}) custom-call(bf16[2,96,7168]{2,1,0:T(8,128)(2,1)} %all-gather.3.cloned.1.call-done.dg_ref.du_ref, bf16[2,96,7168]{2,1,0:T(8,128)(2,1)} %all-gather.3.cloned.1.call-done.dg_ref.du_ref, ...), custom_call_target="tpu_custom_call" | custom-call | flops 4227858432 | bytes 48562176 | tf_op jit(solution)/shard_map/pallas_call | solution.py:135
  169.9 0.0 all-to-all-done.1
  169.9 0.1 reshape.62
  170.1 1.1 convert_reduce_fusion
  171.2 0.3 reshape.42
  171.5 0.2 copy.21
  171.7 0.1 copy.22
  171.7 1.3 gather_fusion
  (2 shorter events, 0.0 us)
Async XLA Ops:
  7.2 91.4 %reduce-scatter.2.cloned.1.call-start = ((), (), s32[]{:S(2)}) async-start(), calls=%async_computation.3 | async-start | bytes 5160960 | tf_op jit(solution)/shard_map/reduce_scatter | solution.py:189
  56.6 70.9 %all-gather.3.cloned.1.call-start = ((), (), s32[]{:S(2)}) async-start(), calls=%async_computation.4 | async-start | bytes 3440640 | tf_op jit(solution)/shard_map/all_gather | solution.py:191
  101.1 51.5 %all-gather.5.cloned.1.call-start = ((), (), s32[]{:S(2)}) async-start(), calls=%async_computation.5 | async-start | bytes 1720320 | tf_op jit(solution)/shard_map/all_gather | solution.py:192
  147.8 22.1 %all-to-all-start.1 = ((bf16[32,2,1536]{2,1,0:T(2,128)(2,1)}), bf16[32,2,1536]{2,1,0:T(2,128)(2,1)S(1)}, u32[]{:S(2)}, u32[]{:S(2)}) async-start(bf16[32,2,1536]{2,1,0:T(2,128)(2,1)} %reshape.61), calls=%async_computation.2 | async-start | bytes 393216 | tf_op jit(solution)/shard_map/all_to_all | solution.py:196
Sparse Core Ops, SparseCore 0:
  56.8 41.7 reduce-scatter.1
  101.3 26.2 all-gather.2
  129.8 18.5 all-gather.4
